TPU v7x, 256 devices: a whole 4x4x8 slice. The times are simulated.
256 devices in a mesh: req: 16 (over x, y), cuts: 16 (over z, core).
Axes of the slice: x: 4, y: 4, z: 8, core: 2. Of those that a mesh axis runs over, the one named last changes fastest.
Arguments:
- queries: bfloat16 [16, 2048, 1024], P('req', 'cuts')
- new_keys: bfloat16 [16, 2048, 1024], P('req', 'cuts'), may hold values from -6 to 6
- new_values: bfloat16 [16, 2048, 1024], P('req', 'cuts'), may hold values from -12 to 12
- cache_keys: bfloat16 [16, 4096, 1024], P('req', 'cuts')
- cache_values: bfloat16 [16, 4096, 1024], P('req', 'cuts'), may hold values from -12 to 12
- cache_lengths: int32 [16], P('req'), may hold values from 2 to 4096, as said below
- relative_bias: float32 [16, 32], replicated, may hold values from -4 to 4
- residual: bfloat16 [16, 2048, 1024], P('req', 'cuts')
- out_weight: bfloat16 [1024, 1024], replicated, may hold values from -0.1875 to 0.1875
- norm_gain: bfloat16 [1024], replicated, may hold values from 0.5 to 1.5
- router_weight: bfloat16 [1024, 16], replicated, may hold values from -0.1875 to 0.1875
- routes: int32 [16, 2048, 2], P('req', 'cuts'), may hold values from 0 to 15, all different within a row; in each aligned block of 128 rows (0 to 127, 128 to 255, ..., all dimensions but the last counted through in order) at most 20 rows name the same one
- gate_weight: bfloat16 [16, 1024, 2816], P('req', None, 'cuts'), may hold values from -0.1875 to 0.1875
- up_weight: bfloat16 [16, 1024, 2816], P('req', None, 'cuts'), may hold values from -0.1875 to 0.1875
- down_weight: bfloat16 [16, 1024, 2816], P('req', None, 'cuts'), may hold values from -0.109375 to 0.109375
Outputs:
- layer_out: bfloat16 [16, 2048, 1024], P('req', 'cuts')
Inputs may be any that keep to these rules, and one draw needn't show every extreme that they name: `cache_lengths`: each cached length lies under 256 or above 3840; some request's cache is full. `routes`: among the 128 tokens of one device no expert is named by more than 20 tokens, a bound that some block reaches.
All inputs are finite; a program needn't handle non-finite values.
Results may differ from a plain program's by a relative error of at most 0.03.
Values may be sent and summed in bfloat16 or wider, within the bound.
No kernel may reach another device: no remote copies, remote signals or barrier semaphores. Data moves between devices by JAX's collectives and lax.ppermute only.
A program may use at most 128 MiB of HBM per device.

v0:
```python
from functools import partial

import jax
import jax.numpy as jnp
import numpy as np
from jax import lax
from jax.sharding import PartitionSpec as P

MAXDIST = 128


def shortened(value):
    return jax.tree.map(lambda a: a.astype(jnp.bfloat16) if a.dtype == jnp.float32 else a, value)


def bucket_number(distance, bucket_count, reach_limit):
    exact_count = bucket_count // 2
    if distance < exact_count:
        return distance
    level_value = exact_count + int(
        np.floor(exact_count * np.log(distance / exact_count) / np.log(reach_limit / exact_count))
    )
    return min(bucket_count - 1, level_value)


def bucket_edges(bucket_count, reach_limit):
    edge_list = []
    for target in range(1, bucket_count):
        probe_value = 0
        while bucket_number(probe_value, bucket_count, reach_limit) < target:
            probe_value += 1
        edge_list.append(probe_value)
    return edge_list


def bucket_index(distance, edge_list):
    bucket_level = jnp.zeros(distance.shape, jnp.int32)
    for edge_value in edge_list:
        bucket_level = bucket_level + (distance >= edge_value).astype(jnp.int32)
    return bucket_level


def block_masks(block_index, length, cache_rows, q_rows, query_total, bucket_count):
    cache_slots = block_index * cache_rows + jnp.arange(cache_rows, dtype=jnp.int32)
    new_slots = block_index * q_rows + jnp.arange(q_rows, dtype=jnp.int32)
    key_pos = jnp.concatenate([cache_slots, length + new_slots])
    key_live = jnp.concatenate([cache_slots < length, new_slots >= 0])
    query_pos = length + jnp.arange(query_total, dtype=jnp.int32)
    visible = key_live[None, :] & (key_pos[None, :] <= query_pos[:, None])
    distance = jnp.maximum(query_pos[:, None] - key_pos[None, :], 0)
    return (visible, bucket_index(distance, bucket_edges(bucket_count, MAXDIST)))


def head_partial(visible, bucket, operands):
    query_rows, key_rows, value_rows, bias_table = operands
    scores = (
        lax.dot_general(
            query_rows, key_rows, (((1,), (1,)), ((), ())), preferred_element_type=jnp.float32
        )
        / 8.0
    )
    masked = jnp.where(visible, scores + jnp.take(bias_table, bucket), -1e30)
    block_peak = jnp.max(masked, axis=1)
    weights = jnp.where(visible, jnp.exp(masked - block_peak[:, None]), 0.0)
    block_total = jnp.sum(weights, axis=1)
    numerator = jnp.dot(
        weights.astype(jnp.bfloat16), value_rows, preferred_element_type=jnp.float32
    )
    block_out = (numerator / jnp.maximum(block_total, 1.0)[:, None]).astype(jnp.bfloat16)
    return (block_out, block_peak, block_total)


def block_partials(query_rows, key_rows, value_rows, tables, visible, bucket):
    head_count = tables.shape[0]
    head_dim = query_rows.shape[1] // head_count
    head_queries = query_rows.reshape(query_rows.shape[0], head_count, head_dim).transpose(1, 0, 2)
    head_keys = key_rows.reshape(key_rows.shape[0], head_count, head_dim).transpose(1, 0, 2)
    head_values = value_rows.reshape(value_rows.shape[0], head_count, head_dim).transpose(1, 0, 2)
    return lax.map(
        partial(head_partial, visible, bucket), (head_queries, head_keys, head_values, tables)
    )


def merge_blocks(block_out, block_peak, block_total):
    best_peak = jnp.max(block_peak, axis=0)
    factor = jnp.exp(block_peak - best_peak[None]) * block_total
    weighted = jnp.sum(factor[..., None] * block_out.astype(jnp.float32), axis=0)
    return (weighted / jnp.sum(factor, axis=0)[..., None]).astype(jnp.bfloat16)


def expert_part(row_block, gate_piece, up_piece, down_piece):
    gate_act = jnp.einsum(
        "necd,edf->necf", row_block, gate_piece, preferred_element_type=jnp.float32
    )
    up_act = jnp.einsum("necd,edf->necf", row_block, up_piece, preferred_element_type=jnp.float32)
    act_rows = (jax.nn.gelu(gate_act) * up_act).astype(jnp.bfloat16)
    return jnp.einsum("necf,edf->necd", act_rows, down_piece, preferred_element_type=jnp.float32)


def per_device(
    queries,
    new_keys,
    new_values,
    cache_keys,
    cache_values,
    cache_lengths,
    relative_bias,
    residual,
    out_weight,
    norm_gain,
    router_weight,
    routes,
    gate_weight,
    up_weight,
    down_weight,
):
    cut_count = lax.axis_size("cuts")
    cut_index = lax.axis_index("cuts")
    q_rows = queries.shape[1]
    cache_rows = cache_keys.shape[1]
    model_width = queries.shape[2]
    head_count = relative_bias.shape[0]
    head_dim = model_width // head_count
    bucket_count = relative_bias.shape[1]
    length = cache_lengths[0]
    query_total = q_rows * cut_count
    local_keys = jnp.concatenate([cache_keys[0], new_keys[0]], axis=0)
    local_values = jnp.concatenate([cache_values[0], new_values[0]], axis=0)
    every_query = lax.all_gather(queries[0], "cuts", axis=0, tiled=True)
    visible, bucket = block_masks(cut_index, length, cache_rows, q_rows, query_total, bucket_count)
    block_out, block_peak, block_total = block_partials(
        every_query, local_keys, local_values, relative_bias, visible, bucket
    )
    block_out = block_out.transpose(1, 0, 2).reshape(cut_count, q_rows, model_width)
    block_peak = block_peak.T.reshape(cut_count, q_rows, head_count)
    block_total = block_total.T.reshape(cut_count, q_rows, head_count)
    block_out = lax.all_to_all(
        shortened(block_out), "cuts", split_axis=0, concat_axis=0, tiled=True
    ).astype(block_out.dtype)
    block_peak, block_total = (
        lax.all_to_all(
            shortened(block_peak), "cuts", split_axis=0, concat_axis=0, tiled=True
        ).astype(block_peak.dtype),
        lax.all_to_all(
            shortened(block_total), "cuts", split_axis=0, concat_axis=0, tiled=True
        ).astype(block_total.dtype),
    )
    block_out = block_out.reshape(cut_count, q_rows, head_count, head_dim)
    attended = merge_blocks(block_out, block_peak, block_total).reshape(q_rows, model_width)
    hidden = residual[0].astype(jnp.float32) + jnp.dot(
        attended, out_weight, preferred_element_type=jnp.float32
    )
    inv_rms = lax.rsqrt(jnp.mean(hidden * hidden, axis=1, keepdims=True) + 1e-06)
    normed = (hidden * inv_rms * norm_gain.astype(jnp.float32)).astype(jnp.bfloat16)
    experts = router_weight.shape[1]
    capacity = (10 * q_rows + 4 * experts - 1) // (4 * experts)
    logits = jnp.dot(normed, router_weight, preferred_element_type=jnp.float32)
    chosen = routes[0]
    onehot = (chosen[:, :, None] == jnp.arange(experts, dtype=jnp.int32)[None, None, :]).astype(
        jnp.float32
    )
    gate_values = jax.nn.sigmoid(jnp.sum(onehot * logits[:, None, :], axis=2))
    named_count = jnp.sum(onehot, axis=1)
    earlier_mask = (jnp.arange(q_rows)[:, None] > jnp.arange(q_rows)[None, :]).astype(jnp.bfloat16)
    earlier = jnp.dot(
        earlier_mask, named_count.astype(jnp.bfloat16), preferred_element_type=jnp.float32
    )
    slot_number = jnp.sum(onehot * earlier[:, None, :], axis=2)
    slot_hot = (
        slot_number[:, :, None] == jnp.arange(capacity, dtype=jnp.float32)[None, None, :]
    ).astype(jnp.float32)
    dispatch = jnp.einsum("tke,tkc->ect", onehot, slot_hot)
    buffers = jnp.einsum(
        "ect,td->ecd", dispatch.astype(jnp.bfloat16), normed, preferred_element_type=jnp.float32
    ).astype(jnp.bfloat16)
    arrived = lax.all_to_all(buffers, "req", split_axis=0, concat_axis=0, tiled=True)
    local_experts = gate_weight.shape[0]
    gathered = lax.all_gather(arrived, "cuts", axis=0, tiled=True)
    row_count = lax.axis_size("cuts") * arrived.shape[0]
    row_block = gathered.reshape(row_count, local_experts, capacity, model_width)
    expert_out = lax.psum_scatter(
        expert_part(row_block, gate_weight, up_weight, down_weight)
        .reshape(row_count, local_experts * capacity, model_width)
        .astype(jnp.bfloat16),
        "cuts",
        scatter_dimension=0,
        tiled=True,
    )
    returned = lax.all_to_all(expert_out, "req", split_axis=0, concat_axis=0, tiled=True)
    combine = jnp.einsum(
        "tke,tkc,tk->ect", onehot, slot_hot, gate_values, precision=lax.Precision.HIGHEST
    )
    gathered_back = jnp.einsum(
        "ect,ecd->td", combine, returned.astype(jnp.float32), precision=lax.Precision.HIGHEST
    )
    layer_out = hidden + gathered_back
    return layer_out.astype(jnp.bfloat16)[None]


def solution(mesh):
    return jax.shard_map(
        per_device,
        mesh=mesh,
        in_specs=(
            P("req", "cuts", None),
            P("req", "cuts", None),
            P("req", "cuts", None),
            P("req", "cuts", None),
            P("req", "cuts", None),
            P("req"),
            P(),
            P("req", "cuts", None),
            P(),
            P(),
            P(),
            P("req", "cuts", None),
            P("req", None, "cuts"),
            P("req", None, "cuts"),
            P("req", None, "cuts"),
        ),
        out_specs=P("req", "cuts", None),
        check_vma=False,
    )
```

profile of v0, /device:TPU:8, one launch (start us, length us, event | category | flops | bytes accessed | tf_op | source)
XLA Modules:
  0.0 968.7 jit_solution(8223163654308807281)
XLA Ops:
  17.1 10.8 %convert_add_fusion = s32[2048,384]{0,1:T(8,128)} fusion(s32[384]{0:T(512)S(1)} %pad_add_fusion, s32[2048]{0:T(1024)S(1)} %iota_add_fusion), kind=kLoop, calls=%fused_computation.63 | loop fusion | flops 73924608 | bytes 3155456 | tf_op jit(solution)/shard_map/add | solution.py:39
  27.9 33.1 %all-gather.6.cloned.1.call-done = bf16[1,2048,1024]{1,2,0:T(8,128)(2,1)} async-done(((bf16[1,128,1024]{1,2,0:T(8,128)(2,1)}), bf16[1,2048,1024]{1,2,0:T(8,128)(2,1)}) %all-gather.6.cloned.1.call-update) | async-done | bytes 4194320 | tf_op jit(solution)/shard_map/all_gather | solution.py:129
  61.0 562.9 %while.15 = (s32[]{:T(128)}, bf16[16,2048,64]{1,2,0:T(8,128)(2,1)}, bf16[16,2048]{1,0:T(8,128)(2,1)S(1)}, bf16[16,2048]{1,0:T(8,128)(2,1)S(1)}, bf16[16,2048,64]...) while((s32[]{:T(128)}, bf16[16,2048,64]{1,2,0:T(8,128)(2,1)}, ...), condition=%wide.region_3.4_spmd.clone, body=%wide.region_0.3_spmd.clone.sunk | while | flops 270792704 | bytes 13345049 | solution.py:79
  63.1 29.3 %fusion.139 = (f32[2048]{0:T(1024)S(1)}, f32[2048,384]{0,1:T(8,128)S(1)}) fusion(f32[]{:T(128)} %bitcast.298, f32[]{:T(128)} %bitcast.299, f32[]{:T(128)} %bitcast.300, f32[]{:T(128)} %bitcast.301, f32[]{:T(128)} %bitcast.302, f32[]{:T(128)} %bitcast.303, f32[]{:T(128)} %bitcast.304, f32[]{:T(128)} %bitcast.305, f32[]{:T(128)} %bitcast.306, ...), kind=kOutput, calls=%fused_computation.158.clone.1 | convolution fusion | flops 162002944 | bytes 6638464 | tf_op jit(solution)/shard_map/while/body/eval_jaxpr/dot_general | solution.py:57
  98.3 29.3 %fusion.139 = (f32[2048]{0:T(1024)S(1)}, f32[2048,384]{0,1:T(8,128)S(1)}) fusion(f32[]{:T(128)} %bitcast.298, f32[]{:T(128)} %bitcast.299, f32[]{:T(128)} %bitcast.300, f32[]{:T(128)} %bitcast.301, f32[]{:T(128)} %bitcast.302, f32[]{:T(128)} %bitcast.303, f32[]{:T(128)} %bitcast.304, f32[]{:T(128)} %bitcast.305, f32[]{:T(128)} %bitcast.306, ...), kind=kOutput, calls=%fused_computation.158.clone.1 | convolution fusion | flops 162002944 | bytes 6638464 | tf_op jit(solution)/shard_map/while/body/eval_jaxpr/dot_general | solution.py:57
  128.6 2.6 fusion.141
  133.4 29.3 %fusion.139 = (f32[2048]{0:T(1024)S(1)}, f32[2048,384]{0,1:T(8,128)S(1)}) fusion(f32[]{:T(128)} %bitcast.298, f32[]{:T(128)} %bitcast.299, f32[]{:T(128)} %bitcast.300, f32[]{:T(128)} %bitcast.301, f32[]{:T(128)} %bitcast.302, f32[]{:T(128)} %bitcast.303, f32[]{:T(128)} %bitcast.304, f32[]{:T(128)} %bitcast.305, f32[]{:T(128)} %bitcast.306, ...), kind=kOutput, calls=%fused_computation.158.clone.1 | convolution fusion | flops 162002944 | bytes 6638464 | tf_op jit(solution)/shard_map/while/body/eval_jaxpr/dot_general | solution.py:57
  163.7 2.5 fusion.141
  168.6 29.3 %fusion.139 = (f32[2048]{0:T(1024)S(1)}, f32[2048,384]{0,1:T(8,128)S(1)}) fusion(f32[]{:T(128)} %bitcast.298, f32[]{:T(128)} %bitcast.299, f32[]{:T(128)} %bitcast.300, f32[]{:T(128)} %bitcast.301, f32[]{:T(128)} %bitcast.302, f32[]{:T(128)} %bitcast.303, f32[]{:T(128)} %bitcast.304, f32[]{:T(128)} %bitcast.305, f32[]{:T(128)} %bitcast.306, ...), kind=kOutput, calls=%fused_computation.158.clone.1 | convolution fusion | flops 162002944 | bytes 6638464 | tf_op jit(solution)/shard_map/while/body/eval_jaxpr/dot_general | solution.py:57
  198.9 2.5 fusion.141
  203.8 29.3 %fusion.139 = (f32[2048]{0:T(1024)S(1)}, f32[2048,384]{0,1:T(8,128)S(1)}) fusion(f32[]{:T(128)} %bitcast.298, f32[]{:T(128)} %bitcast.299, f32[]{:T(128)} %bitcast.300, f32[]{:T(128)} %bitcast.301, f32[]{:T(128)} %bitcast.302, f32[]{:T(128)} %bitcast.303, f32[]{:T(128)} %bitcast.304, f32[]{:T(128)} %bitcast.305, f32[]{:T(128)} %bitcast.306, ...), kind=kOutput, calls=%fused_computation.158.clone.1 | convolution fusion | flops 162002944 | bytes 6638464 | tf_op jit(solution)/shard_map/while/body/eval_jaxpr/dot_general | solution.py:57
  239.0 29.3 %fusion.139 = (f32[2048]{0:T(1024)S(1)}, f32[2048,384]{0,1:T(8,128)S(1)}) fusion(f32[]{:T(128)} %bitcast.298, f32[]{:T(128)} %bitcast.299, f32[]{:T(128)} %bitcast.300, f32[]{:T(128)} %bitcast.301, f32[]{:T(128)} %bitcast.302, f32[]{:T(128)} %bitcast.303, f32[]{:T(128)} %bitcast.304, f32[]{:T(128)} %bitcast.305, f32[]{:T(128)} %bitcast.306, ...), kind=kOutput, calls=%fused_computation.158.clone.1 | convolution fusion | flops 162002944 | bytes 6638464 | tf_op jit(solution)/shard_map/while/body/eval_jaxpr/dot_general | solution.py:57
  269.3 2.6 fusion.141
  274.2 29.3 %fusion.139 = (f32[2048]{0:T(1024)S(1)}, f32[2048,384]{0,1:T(8,128)S(1)}) fusion(f32[]{:T(128)} %bitcast.298, f32[]{:T(128)} %bitcast.299, f32[]{:T(128)} %bitcast.300, f32[]{:T(128)} %bitcast.301, f32[]{:T(128)} %bitcast.302, f32[]{:T(128)} %bitcast.303, f32[]{:T(128)} %bitcast.304, f32[]{:T(128)} %bitcast.305, f32[]{:T(128)} %bitcast.306, ...), kind=kOutput, calls=%fused_computation.158.clone.1 | convolution fusion | flops 162002944 | bytes 6638464 | tf_op jit(solution)/shard_map/while/body/eval_jaxpr/dot_general | solution.py:57
  304.5 2.5 fusion.141
  309.4 29.3 %fusion.139 = (f32[2048]{0:T(1024)S(1)}, f32[2048,384]{0,1:T(8,128)S(1)}) fusion(f32[]{:T(128)} %bitcast.298, f32[]{:T(128)} %bitcast.299, f32[]{:T(128)} %bitcast.300, f32[]{:T(128)} %bitcast.301, f32[]{:T(128)} %bitcast.302, f32[]{:T(128)} %bitcast.303, f32[]{:T(128)} %bitcast.304, f32[]{:T(128)} %bitcast.305, f32[]{:T(128)} %bitcast.306, ...), kind=kOutput, calls=%fused_computation.158.clone.1 | convolution fusion | flops 162002944 | bytes 6638464 | tf_op jit(solution)/shard_map/while/body/eval_jaxpr/dot_general | solution.py:57
  344.5 29.3 %fusion.139 = (f32[2048]{0:T(1024)S(1)}, f32[2048,384]{0,1:T(8,128)S(1)}) fusion(f32[]{:T(128)} %bitcast.298, f32[]{:T(128)} %bitcast.299, f32[]{:T(128)} %bitcast.300, f32[]{:T(128)} %bitcast.301, f32[]{:T(128)} %bitcast.302, f32[]{:T(128)} %bitcast.303, f32[]{:T(128)} %bitcast.304, f32[]{:T(128)} %bitcast.305, f32[]{:T(128)} %bitcast.306, ...), kind=kOutput, calls=%fused_computation.158.clone.1 | convolution fusion | flops 162002944 | bytes 6638464 | tf_op jit(solution)/shard_map/while/body/eval_jaxpr/dot_general | solution.py:57
  374.8 2.5 fusion.141
  379.7 29.3 %fusion.139 = (f32[2048]{0:T(1024)S(1)}, f32[2048,384]{0,1:T(8,128)S(1)}) fusion(f32[]{:T(128)} %bitcast.298, f32[]{:T(128)} %bitcast.299, f32[]{:T(128)} %bitcast.300, f32[]{:T(128)} %bitcast.301, f32[]{:T(128)} %bitcast.302, f32[]{:T(128)} %bitcast.303, f32[]{:T(128)} %bitcast.304, f32[]{:T(128)} %bitcast.305, f32[]{:T(128)} %bitcast.306, ...), kind=kOutput, calls=%fused_computation.158.clone.1 | convolution fusion | flops 162002944 | bytes 6638464 | tf_op jit(solution)/shard_map/while/body/eval_jaxpr/dot_general | solution.py:57
  410.0 2.5 fusion.141
  414.9 29.3 %fusion.139 = (f32[2048]{0:T(1024)S(1)}, f32[2048,384]{0,1:T(8,128)S(1)}) fusion(f32[]{:T(128)} %bitcast.298, f32[]{:T(128)} %bitcast.299, f32[]{:T(128)} %bitcast.300, f32[]{:T(128)} %bitcast.301, f32[]{:T(128)} %bitcast.302, f32[]{:T(128)} %bitcast.303, f32[]{:T(128)} %bitcast.304, f32[]{:T(128)} %bitcast.305, f32[]{:T(128)} %bitcast.306, ...), kind=kOutput, calls=%fused_computation.158.clone.1 | convolution fusion | flops 162002944 | bytes 6638464 | tf_op jit(solution)/shard_map/while/body/eval_jaxpr/dot_general | solution.py:57
  445.2 2.5 fusion.141
  450.1 29.3 %fusion.139 = (f32[2048]{0:T(1024)S(1)}, f32[2048,384]{0,1:T(8,128)S(1)}) fusion(f32[]{:T(128)} %bitcast.298, f32[]{:T(128)} %bitcast.299, f32[]{:T(128)} %bitcast.300, f32[]{:T(128)} %bitcast.301, f32[]{:T(128)} %bitcast.302, f32[]{:T(128)} %bitcast.303, f32[]{:T(128)} %bitcast.304, f32[]{:T(128)} %bitcast.305, f32[]{:T(128)} %bitcast.306, ...), kind=kOutput, calls=%fused_computation.158.clone.1 | convolution fusion | flops 162002944 | bytes 6638464 | tf_op jit(solution)/shard_map/while/body/eval_jaxpr/dot_general | solution.py:57
  480.4 2.6 fusion.141
  485.3 29.3 %fusion.139 = (f32[2048]{0:T(1024)S(1)}, f32[2048,384]{0,1:T(8,128)S(1)}) fusion(f32[]{:T(128)} %bitcast.298, f32[]{:T(128)} %bitcast.299, f32[]{:T(128)} %bitcast.300, f32[]{:T(128)} %bitcast.301, f32[]{:T(128)} %bitcast.302, f32[]{:T(128)} %bitcast.303, f32[]{:T(128)} %bitcast.304, f32[]{:T(128)} %bitcast.305, f32[]{:T(128)} %bitcast.306, ...), kind=kOutput, calls=%fused_computation.158.clone.1 | convolution fusion | flops 162002944 | bytes 6638464 | tf_op jit(solution)/shard_map/while/body/eval_jaxpr/dot_general | solution.py:57
  520.5 29.3 %fusion.139 = (f32[2048]{0:T(1024)S(1)}, f32[2048,384]{0,1:T(8,128)S(1)}) fusion(f32[]{:T(128)} %bitcast.298, f32[]{:T(128)} %bitcast.299, f32[]{:T(128)} %bitcast.300, f32[]{:T(128)} %bitcast.301, f32[]{:T(128)} %bitcast.302, f32[]{:T(128)} %bitcast.303, f32[]{:T(128)} %bitcast.304, f32[]{:T(128)} %bitcast.305, f32[]{:T(128)} %bitcast.306, ...), kind=kOutput, calls=%fused_computation.158.clone.1 | convolution fusion | flops 162002944 | bytes 6638464 | tf_op jit(solution)/shard_map/while/body/eval_jaxpr/dot_general | solution.py:57
  550.7 2.5 fusion.141
  555.6 29.3 %fusion.139 = (f32[2048]{0:T(1024)S(1)}, f32[2048,384]{0,1:T(8,128)S(1)}) fusion(f32[]{:T(128)} %bitcast.298, f32[]{:T(128)} %bitcast.299, f32[]{:T(128)} %bitcast.300, f32[]{:T(128)} %bitcast.301, f32[]{:T(128)} %bitcast.302, f32[]{:T(128)} %bitcast.303, f32[]{:T(128)} %bitcast.304, f32[]{:T(128)} %bitcast.305, f32[]{:T(128)} %bitcast.306, ...), kind=kOutput, calls=%fused_computation.158.clone.1 | convolution fusion | flops 162002944 | bytes 6638464 | tf_op jit(solution)/shard_map/while/body/eval_jaxpr/dot_general | solution.py:57
  585.9 2.5 fusion.141
  590.8 29.3 %fusion.139 = (f32[2048]{0:T(1024)S(1)}, f32[2048,384]{0,1:T(8,128)S(1)}) fusion(f32[]{:T(128)} %bitcast.298, f32[]{:T(128)} %bitcast.299, f32[]{:T(128)} %bitcast.300, f32[]{:T(128)} %bitcast.301, f32[]{:T(128)} %bitcast.302, f32[]{:T(128)} %bitcast.303, f32[]{:T(128)} %bitcast.304, f32[]{:T(128)} %bitcast.305, f32[]{:T(128)} %bitcast.306, ...), kind=kOutput, calls=%fused_computation.158.clone.1 | convolution fusion | flops 162002944 | bytes 6638464 | tf_op jit(solution)/shard_map/while/body/eval_jaxpr/dot_general | solution.py:57
  621.1 2.6 fusion.141
  624.6 4.4 all-to-all-start.1
  629.6 7.2 all-to-all-done.1
  636.8 3.5 all-to-all-start
  640.3 3.6 copy.129
  643.9 3.0 copy.112
  648.0 6.2 all-to-all-start.2
  655.1 93.4 %all-to-all-done.2 = bf16[16,128,1024]{1,2,0:T(8,128)(2,1)} async-done(((bf16[16,128,1024]{1,2,0:T(8,128)(2,1)}), bf16[16,128,1024]{1,2,0:T(8,128)(2,1)}, u32[]{:S(2)}, u32[]{:S(2)}) %all-to-all-start.2) | async-done | bytes 4194336 | tf_op jit(solution)/shard_map/all_to_all | solution.py:137
  748.6 3.1 fusion.43
  754.5 19.5 %all_to_all.25 = bf16[16,20,1024]{2,1,0:T(8,128)(2,1)S(1)} all-to-all(bf16[16,20,1024]{2,1,0:T(8,128)(2,1)S(1)} %convolution_convert_fusion.1), channel_id=1, replica_groups=mesh['req'=16,'cuts'=16] {'req'}, dimensions={0} | all-to-all | bytes 1310720 | tf_op jit(solution)/shard_map/all_to_all | solution.py:176
  775.3 63.0 %all-gather.4.cloned.1.call-done = bf16[256,20,1024]{2,0,1:T(8,128)(2,1)} async-done(((bf16[16,20,1024]{2,0,1:T(8,128)(2,1)}), bf16[256,20,1024]{2,0,1:T(8,128)(2,1)}) %all-gather.4.cloned.1.call-update) | async-done | bytes 10485776 | tf_op jit(solution)/shard_map/all_gather | solution.py:178
  838.3 9.4 fusion.95
  847.7 18.0 %convolution_convert_fusion = bf16[256,20,1024]{2,0,1:T(8,128)(2,1)} fusion(f32[256,20,176]{0,2,1:T(8,128)} %fusion.95, bf16[256,20,1024]{2,0,1:T(8,128)(2,1)} %all-gather.4.cloned.1.call-done, bf16[1,1024,176]{1,2,0:T(8,128)(2,1)S(1)} %copy-done.7, bf16[1,1024,176]{1,2,0:T(8,128)(2,1)} %param.30), kind=kOutput, calls=%fused_computation.52 | convolution fusion | flops 3705241600 | bytes 25296896 | tf_op jit(solution)/shard_map/necf,edf->necd/dot_general | solution.py:97
  865.7 73.2 %reduce-scatter.2.cloned.1.call-done = bf16[16,20,1024]{2,0,1:T(8,128)(2,1)} async-done(((bf16[256,20,1024]{2,0,1:T(8,128)(2,1)}), bf16[16,20,1024]{2,0,1:T(8,128)(2,1)}) %reduce-scatter.2.cloned.1.call-update) | async-done | bytes 655376 | tf_op jit(solution)/shard_map/reduce_scatter | solution.py:181
  941.3 7.3 all-to-all-start.4
  948.6 3.3 convolution_bitcast_fusion
  951.9 7.1 all-to-all-done.4
  959.0 3.2 fusion.88
  (174 shorter events, 82.3 us)
Async XLA Ops:
  6.5 745.2 %copy-start = (bf16[1024,1024]{1,0:T(8,128)(2,1)S(1)}, bf16[1024,1024]{1,0:T(8,128)(2,1)}, u32[]{:S(2)}) copy-start(bf16[1024,1024]{1,0:T(8,128)(2,1)} %param.25) | copy-start | bytes 6291460
  6.5 54.4 %all-gather.6.cloned.1.call-start = ((), (), s32[]{:S(2)}) async-start(), calls=%async_computation.8 | async-start | bytes 4456448 | tf_op jit(solution)/shard_map/all_gather | solution.py:129
  624.6 12.2 %all-to-all-start.1 = ((bf16[16,128,16]{1,2,0:T(8,128)(2,1)}), bf16[16,128,16]{1,2,0:T(8,128)(2,1)S(1)}, u32[]{:S(2)}, u32[]{:S(2)}) async-start(bf16[16,128,16]{1,2,0:T(8,128)(2,1)} %copy_bitcast_fusion), calls=%async_computation.1 | async-start | bytes 131072 | tf_op jit(solution)/shard_map/all_to_all | solution.py:144
  636.8 11.3 %all-to-all-start = ((bf16[16,128,16]{1,2,0:T(8,128)(2,1)}), bf16[16,128,16]{1,2,0:T(8,128)(2,1)S(1)}, u32[]{:S(2)}, u32[]{:S(2)}) async-start(bf16[16,128,16]{1,2,0:T(8,128)(2,1)} %copy_bitcast_fusion.1), calls=%async_computation | async-start | bytes 131072 | tf_op jit(solution)/shard_map/all_to_all | solution.py:141
  646.9 7.6 copy-start.5
  646.9 7.6 copy-start.6
  648.0 100.5 %all-to-all-start.2 = ((bf16[16,128,1024]{1,2,0:T(8,128)(2,1)}), bf16[16,128,1024]{1,2,0:T(8,128)(2,1)}, u32[]{:S(2)}, u32[]{:S(2)}) async-start(bf16[16,128,1024]{1,2,0:T(8,128)(2,1)} %copy.112), calls=%async_computation.2 | async-start | bytes 8388608 | tf_op jit(solution)/shard_map/all_to_all | solution.py:137
  654.2 97.5 %copy-start.2 = (bf16[1,128,1024]{2,1,0:T(8,128)(2,1)S(1)}, bf16[1,128,1024]{2,1,0:T(8,128)(2,1)}, u32[]{:S(2)}) copy-start(bf16[1,128,1024]{2,1,0:T(8,128)(2,1)} %param.24) | copy-start | bytes 786436
  654.2 184.0 %all-gather.4.cloned.1.call-start = ((), (), s32[]{:S(2)}) async-start(), calls=%async_computation.6 | async-start | bytes 11141120 | tf_op jit(solution)/shard_map/all_gather | solution.py:178
  751.6 0.8 copy-start.4
  753.2 22.0 %copy-start.3 = (f32[128,2]{1,0:T(8,128)}, f32[128,2]{1,0:T(8,128)S(1)}, u32[]{:S(2)}) copy-start(f32[128,2]{1,0:T(8,128)S(1)} %get-tuple-element.164) | copy-start | bytes 3076
  754.5 83.8 %copy-start.1 = (bf16[1,1024,176]{1,2,0:T(8,128)(2,1)S(1)}, bf16[1,1024,176]{1,2,0:T(8,128)(2,1)}, u32[]{:S(2)}) copy-start(bf16[1,1024,176]{1,2,0:T(8,128)(2,1)} %param.29) | copy-start | bytes 1081348
  775.2 72.5 %copy-start.7 = (bf16[1,1024,176]{1,2,0:T(8,128)(2,1)S(1)}, bf16[1,1024,176]{1,2,0:T(8,128)(2,1)}, u32[]{:S(2)}) copy-start(bf16[1,1024,176]{1,2,0:T(8,128)(2,1)} %param.31) | copy-start | bytes 1081348
  775.2 163.7 %reduce-scatter.2.cloned.1.call-start = ((), (), s32[]{:S(2)}) async-start(), calls=%async_computation.7 | async-start | bytes 11141120 | tf_op jit(solution)/shard_map/reduce_scatter | solution.py:181
  941.3 17.7 %all-to-all-start.4 = ((bf16[16,20,1024]{2,1,0:T(8,128)(2,1)}), bf16[16,20,1024]{2,1,0:T(8,128)(2,1)S(1)}, u32[]{:S(2)}, u32[]{:S(2)}) async-start(bf16[16,20,1024]{2,1,0:T(8,128)(2,1)} %copy.120), calls=%async_computation.5 | async-start | bytes 1572864 | tf_op jit(solution)/shard_map/all_to_all | solution.py:189
Sparse Core Ops, SparseCore 0:
  9.1 51.8 all-gather.5
  775.3 62.9 all-gather.3
  865.9 73.0 reduce-scatter.1
where the time goes:
time: 976 us; the launch traced here: 969 us
  matrix products  545 us (56%)
  waiting for transfers between devices  278 us (28%)
  local copies, waits for them, and re-layouts  56 us (6%)
  other arithmetic  33 us (3%)
  starting transfers between devices  21.6 us (2%)
  blocking collectives  19.5 us (2%)
  between operations  14 us (1%)
    dot_general x16, matrix products, head_partial(): lax.dot_general(query_rows, key_rows, (((1,), (1,)), ((), ())), preferred...  469 us
    all_to_all x1, waiting for transfers between devices, per_device(): lax.all_to_all(shortened(block_out), 'cuts', split_axis=0, concat_axis=0,...  93.4 us
    reduce_scatter x1, waiting for transfers between devices, per_device(): lax.psum_scatter(expert_part(row_block, gate_weight, up_weight, down_weig...  73.2 us
    all_gather x1, waiting for transfers between devices, per_device(): gathered = lax.all_gather(arrived, 'cuts', axis=0, tiled=True)  63 us
    dot_general x16, matrix products, head_partial(): jnp.dot(weights.astype(jnp.bfloat16), value_rows, preferred_element_type=...  40.8 us
    all_gather x1, waiting for transfers between devices, per_device(): every_query = lax.all_gather(queries[0], 'cuts', axis=0, tiled=True)  33.1 us
    gather x32, local copies, waits for them, and re-layouts, head_partial(): masked = jnp.where(visible, scores + jnp.take(bias_table, bucket), -1e+30)  22.6 us
  transfers between devices with their start and end apart: 7, of which 7 were waited for; matrix products, arithmetic and copies ran while one was open for 3% of the time, Pallas kernels for 0%

commit v1 on v0

--- a/solution.py
+++ b/solution.py
@@ -5,6 +5,8 @@
 import numpy as np
 from jax import lax
 from jax.sharding import PartitionSpec as P
+from jax.experimental import pallas as pl
+from jax.experimental.pallas import tpu as pltpu
 
 MAXDIST = 128
 
@@ -40,45 +42,105 @@
     return bucket_level
 
 
-def block_masks(block_index, length, cache_rows, q_rows, query_total, bucket_count):
-    cache_slots = block_index * cache_rows + jnp.arange(cache_rows, dtype=jnp.int32)
-    new_slots = block_index * q_rows + jnp.arange(q_rows, dtype=jnp.int32)
-    key_pos = jnp.concatenate([cache_slots, length + new_slots])
-    key_live = jnp.concatenate([cache_slots < length, new_slots >= 0])
-    query_pos = length + jnp.arange(query_total, dtype=jnp.int32)
-    visible = key_live[None, :] & (key_pos[None, :] <= query_pos[:, None])
-    distance = jnp.maximum(query_pos[:, None] - key_pos[None, :], 0)
-    return (visible, bucket_index(distance, bucket_edges(bucket_count, MAXDIST)))
-
-
-def head_partial(visible, bucket, operands):
-    query_rows, key_rows, value_rows, bias_table = operands
-    scores = (
-        lax.dot_general(
-            query_rows, key_rows, (((1,), (1,)), ((), ())), preferred_element_type=jnp.float32
+def attention_kernel(scalars, q_ref, k_ref, v_ref, tc_ref, tn_ref, o_ref, peak_ref, total_ref):
+    length = scalars[0]
+    cut = scalars[1]
+    block = pl.program_id(0)
+    q_rows = q_ref.shape[0]
+    head_count, key_span, head_dim = k_ref.shape
+    cache_rows = tc_ref.shape[2] - q_rows
+    new_rows = key_span - cache_rows
+    row = lax.broadcasted_iota(jnp.int32, (q_rows, key_span), 0)
+    col = lax.broadcasted_iota(jnp.int32, (q_rows, key_span), 1)
+    cache_live = cut * cache_rows + col < length
+    new_live = cut * new_rows + (col - cache_rows) <= block * q_rows + row
+    is_cache = col < cache_rows
+    visible = (is_cache & cache_live) | (jnp.logical_not(is_cache) & new_live)
+    cache_width = tc_ref.shape[2]
+    new_width = tn_ref.shape[2]
+    for h in range(head_count):
+        query = q_ref[:, h * head_dim:(h + 1) * head_dim]
+        scores = lax.dot_general(
+            query, k_ref[h], (((1,), (1,)), ((), ())), preferred_element_type=jnp.float32
+        ) / 8.0
+        cache_table = jnp.broadcast_to(tc_ref[0, h:h + 1, :], (q_rows, cache_width))
+        cache_bias = pltpu.roll(cache_table, cache_width - q_rows, 1, stride=1, stride_axis=0)
+        new_table = jnp.broadcast_to(tn_ref[0, h:h + 1, :], (q_rows, new_width))
+        new_bias = pltpu.roll(new_table, new_width - q_rows, 1, stride=1, stride_axis=0)
+        bias = jnp.concatenate([cache_bias[:, :cache_rows], new_bias[:, :new_rows]], axis=1)
+        masked = jnp.where(visible, scores + bias, -1e30)
+        peak = jnp.max(masked, axis=1, keepdims=True)
+        weights = jnp.where(visible, jnp.exp(masked - peak), 0.0)
+        total = jnp.sum(weights, axis=1, keepdims=True)
+        numerator = jnp.dot(
+            weights.astype(jnp.bfloat16), v_ref[h], preferred_element_type=jnp.float32
         )
-        / 8.0
-    )
-    masked = jnp.where(visible, scores + jnp.take(bias_table, bucket), -1e30)
-    block_peak = jnp.max(masked, axis=1)
-    weights = jnp.where(visible, jnp.exp(masked - block_peak[:, None]), 0.0)
-    block_total = jnp.sum(weights, axis=1)
-    numerator = jnp.dot(
-        weights.astype(jnp.bfloat16), value_rows, preferred_element_type=jnp.float32
-    )
-    block_out = (numerator / jnp.maximum(block_total, 1.0)[:, None]).astype(jnp.bfloat16)
-    return (block_out, block_peak, block_total)
-
-
-def block_partials(query_rows, key_rows, value_rows, tables, visible, bucket):
+        o_ref[:, h * head_dim:(h + 1) * head_dim] = (
+            numerator / jnp.maximum(total, 1.0)
+        ).astype(o_ref.dtype)
+        peak_ref[:, h:h + 1] = peak
+        total_ref[:, h:h + 1] = total
+
+
+def bias_tables(tables, length, cut, q_rows, cache_rows, new_rows, query_blocks):
+    edges = bucket_edges(tables.shape[1], MAXDIST)
+    blocks = jnp.arange(query_blocks, dtype=jnp.int32)[:, None]
+    cache_lanes = jnp.arange(cache_rows + q_rows, dtype=jnp.int32)[None, :]
+    new_lanes = jnp.arange(new_rows + q_rows, dtype=jnp.int32)[None, :]
+    cache_distance = length + blocks * q_rows - cut * cache_rows + q_rows - cache_lanes
+    new_distance = (blocks * q_rows - cut * new_rows) + q_rows - new_lanes
+    cache_bucket = bucket_index(jnp.maximum(cache_distance, 0), edges)
+    new_bucket = bucket_index(jnp.maximum(new_distance, 0), edges)
+    cache_table = jnp.take(tables, cache_bucket, axis=1).transpose(1, 0, 2)
+    new_table = jnp.take(tables, new_bucket, axis=1).transpose(1, 0, 2)
+    return cache_table, new_table
+
+
+def block_partials(query_rows, key_rows, value_rows, tables, length, cut, cache_rows, q_rows):
     head_count = tables.shape[0]
-    head_dim = query_rows.shape[1] // head_count
-    head_queries = query_rows.reshape(query_rows.shape[0], head_count, head_dim).transpose(1, 0, 2)
-    head_keys = key_rows.reshape(key_rows.shape[0], head_count, head_dim).transpose(1, 0, 2)
-    head_values = value_rows.reshape(value_rows.shape[0], head_count, head_dim).transpose(1, 0, 2)
-    return lax.map(
-        partial(head_partial, visible, bucket), (head_queries, head_keys, head_values, tables)
-    )
+    model_width = query_rows.shape[1]
+    head_dim = model_width // head_count
+    key_span = key_rows.shape[0]
+    new_rows = key_span - cache_rows
+    query_total = query_rows.shape[0]
+    query_blocks = query_total // q_rows
+    head_keys = key_rows.reshape(key_span, head_count, head_dim).transpose(1, 0, 2)
+    head_values = value_rows.reshape(key_span, head_count, head_dim).transpose(1, 0, 2)
+    cache_table, new_table = bias_tables(
+        tables, length, cut, q_rows, cache_rows, new_rows, query_blocks
+    )
+    scalars = jnp.stack([length, cut]).astype(jnp.int32)
+    grid_spec = pltpu.PrefetchScalarGridSpec(
+        num_scalar_prefetch=1,
+        grid=(query_blocks,),
+        in_specs=[
+            pl.BlockSpec((q_rows, model_width), lambda b, s: (b, 0)),
+            pl.BlockSpec((head_count, key_span, head_dim), lambda b, s: (0, 0, 0)),
+            pl.BlockSpec((head_count, key_span, head_dim), lambda b, s: (0, 0, 0)),
+            pl.BlockSpec((1, head_count, cache_table.shape[2]), lambda b, s: (b, 0, 0)),
+            pl.BlockSpec((1, head_count, new_table.shape[2]), lambda b, s: (b, 0, 0)),
+        ],
+        out_specs=[
+            pl.BlockSpec((q_rows, model_width), lambda b, s: (b, 0)),
+            pl.BlockSpec((q_rows, head_count), lambda b, s: (b, 0)),
+            pl.BlockSpec((q_rows, head_count), lambda b, s: (b, 0)),
+        ],
+    )
+    pairs = query_total * key_span * head_count
+    return pl.pallas_call(
+        attention_kernel,
+        grid_spec=grid_spec,
+        out_shape=[
+            jax.ShapeDtypeStruct((query_total, model_width), jnp.bfloat16),
+            jax.ShapeDtypeStruct((query_total, head_count), jnp.float32),
+            jax.ShapeDtypeStruct((query_total, head_count), jnp.float32),
+        ],
+        cost_estimate=pl.CostEstimate(
+            flops=4 * pairs * head_dim,
+            transcendentals=pairs,
+            bytes_accessed=4 * query_total * model_width + 4 * key_span * model_width,
+        ),
+    )(scalars, query_rows, head_keys, head_values, cache_table, new_table)
 
 
 def merge_blocks(block_out, block_peak, block_total):
@@ -127,13 +189,12 @@
     local_keys = jnp.concatenate([cache_keys[0], new_keys[0]], axis=0)
     local_values = jnp.concatenate([cache_values[0], new_values[0]], axis=0)
     every_query = lax.all_gather(queries[0], "cuts", axis=0, tiled=True)
-    visible, bucket = block_masks(cut_index, length, cache_rows, q_rows, query_total, bucket_count)
     block_out, block_peak, block_total = block_partials(
-        every_query, local_keys, local_values, relative_bias, visible, bucket
-    )
-    block_out = block_out.transpose(1, 0, 2).reshape(cut_count, q_rows, model_width)
-    block_peak = block_peak.T.reshape(cut_count, q_rows, head_count)
-    block_total = block_total.T.reshape(cut_count, q_rows, head_count)
+        every_query, local_keys, local_values, relative_bias, length, cut_index, cache_rows, q_rows
+    )
+    block_out = block_out.reshape(cut_count, q_rows, model_width)
+    block_peak = block_peak.reshape(cut_count, q_rows, head_count)
+    block_total = block_total.reshape(cut_count, q_rows, head_count)
     block_out = lax.all_to_all(
         shortened(block_out), "cuts", split_axis=0, concat_axis=0, tiled=True
     ).astype(block_out.dtype)

time: 976 us -> 501 us (0.51)
  matrix products: 545 us -> 36.1 us
  Pallas kernels: 0 us -> 77.9 us
  waiting for transfers between devices: 278 us -> 244 us
  other arithmetic: 33 us -> 14.2 us
  local copies, waits for them, and re-layouts: 56 us -> 67.1 us
    dot_general x32 -> x0, matrix products: 509 us -> none  [the longest x16 469 us: head_partial(): lax.dot_general(query_rows, key_rows, (((1,), (1,)), ((), ())), preferred...]
    pallas_call x0 -> x1, Pallas kernels: none -> 77.9 us  [block_partials(): pl.pallas_call(attention_kernel, grid_spec=grid_spec, out_shape=[jax.Shap...]
    all_gather x1, waiting for transfers between devices: 33.1 us -> 0.01 us  [per_device(): every_query = lax.all_gather(queries[0], 'cuts', axis=0, tiled=True)]
    gather x32 -> x4, local copies, waits for them, and re-layouts: 22.6 us -> 41.9 us  [the longest x2 23.5 us: bias_tables(): cache_table = jnp.take(tables, cache_bucket, axis=1).transpose(1, 0, 2)]
    reduce_sum x16 -> x0, other arithmetic: 15.7 us -> none  [head_partial(): block_total = jnp.sum(weights, axis=1)]
    dynamic_slice x16 -> x0, local copies, waits for them, and re-layouts: 11.1 us -> none  [block_partials(): lax.map(partial(head_partial, visible, bucket), (head_queries, head_keys,...]
    add x4 -> x2, other arithmetic: 10.8 us -> 0.01 us  [the longest x1 0.01 us: bias_tables(): length + blocks * q_rows - cut * cache_rows + q_rows - cache_lanes]
  transfers between devices with their start and end apart: 7 -> 7, of which waited for: 7 -> 6; matrix products, arithmetic and copies ran while one was open for 3% -> 15% of each run, Pallas kernels for 0% -> 0%
where the time goes in v1:
time: 501 us; the launch traced here: 499 us
  waiting for transfers between devices  244 us (49%)
  Pallas kernels  77.9 us (16%)
  local copies, waits for them, and re-layouts  67.1 us (13%)
  matrix products  36.1 us (7%)
  starting transfers between devices  25.5 us (5%)
  blocking collectives  19.5 us (4%)
  other arithmetic  14.2 us (3%)
  between operations  14.1 us (3%)
    all_to_all x1, waiting for transfers between devices, per_device(): lax.all_to_all(shortened(block_out), 'cuts', split_axis=0, concat_axis=0,...  93.4 us
    pallas_call x1, Pallas kernels, block_partials(): pl.pallas_call(attention_kernel, grid_spec=grid_spec, out_shape=[jax.Shap...  77.9 us
    reduce_scatter x1, waiting for transfers between devices, per_device(): lax.psum_scatter(expert_part(row_block, gate_weight, up_weight, down_weig...  73.2 us
    all_gather x1, waiting for transfers between devices, per_device(): gathered = lax.all_gather(arrived, 'cuts', axis=0, tiled=True)  63 us
    gather x2, local copies, waits for them, and re-layouts, bias_tables(): cache_table = jnp.take(tables, cache_bucket, axis=1).transpose(1, 0, 2)  23.5 us
    all_to_all x1, blocking collectives, per_device(): lax.all_to_all(buffers, 'req', split_axis=0, concat_axis=0, tiled=True)  19.5 us
    gather x2, local copies, waits for them, and re-layouts, bias_tables(): new_table = jnp.take(tables, new_bucket, axis=1).transpose(1, 0, 2)  18.4 us
    dot_general x1, matrix products, expert_part(): jnp.einsum('necf,edf->necd', act_rows, down_piece, preferred_element_type...  17.9 us
  transfers between devices with their start and end apart: 7, of which 6 were waited for; matrix products, arithmetic and copies ran while one was open for 15% of the time, Pallas kernels for 0%

profile of v1, /device:TPU:8, one launch (start us, length us, event | category | flops | bytes accessed | tf_op | source)
XLA Modules:
  0.0 498.7 jit_solution(11241887956498601426)
XLA Ops:
  6.5 0.7 all-gather.6.cloned.1.call-update
  7.9 1.1 copy.123
  9.0 1.0 copy.125
  10.1 2.0 copy.122
  12.1 1.5 copy.124
  13.6 1.1 copy.127
  14.8 1.0 copy.129
  15.8 2.0 copy.126
  17.8 2.4 copy.128
  20.3 0.5 copy-done.11
  21.0 21.1 %gather_fusion = f32[6144,16]{1,0:T(8,128)} fusion(f32[16,32]{0,1:T(8,128)S(1)} %copy.130, s32[6144]{0:T(1024)S(1)} %broadcast_clamp_fusion), kind=kCustom, calls=%fused_computation | custom fusion | bytes 811008 | tf_op jit(solution)/shard_map/jit(_take)/gather | solution.py:94
  42.1 2.4 copy.132
  44.5 0.5 copy-done.9
  45.2 0.6 broadcast_clamp_fusion.1
  45.8 15.5 %gather_fusion.1 = f32[4096,16]{1,0:T(8,128)} fusion(f32[16,32]{0,1:T(8,128)S(1)} %copy.130, s32[4096]{0:T(1024)} %broadcast_clamp_fusion.1), kind=kCustom, calls=%fused_computation.1 | custom fusion | bytes 540672 | tf_op jit(solution)/shard_map/jit(_take)/gather | solution.py:95
  61.3 2.9 copy.135
  64.2 0.7 pad_add_fusion.scalars
  64.8 4.2 maximum_bitcast_fusion
  69.3 0.7 select_bitcast_fusion.1.tn_ref
  70.1 0.8 select_bitcast_fusion.tc_ref
  70.9 77.9 %shard_map.145 = (bf16[2048,1024]{1,0:T(8,128)(2,1)}, f32[2048,16]{1,0:T(8,128)}, f32[2048,16]{1,0:T(8,128)}) custom-call(s32[2]{0:T(128)} %pad_add_fusion.scalars, bf16[2048,1024]{1,0:T(8,128)(2,1)} %bitcast.110, bf16[16,384,64]{2,1,0:T(8,128)(2,1)} %get-tuple-element.17.k_ref, bf16[16,384,64]{2,1,0:T(8,128)(2,1)} %get-tuple-element.18.v_ref, ...), custom_call_target="tpu_custom_call" | custom-call | flops 3221225472 | bytes 9961472 | tf_op jit(solution)/shard_map/pallas_call | solution.py:130
  148.8 1.3 convert_element_type.1062
  150.1 0.8 copy.137
  150.9 8.5 %all-to-all-start.1 = ((bf16[16,128,16]{1,2,0:T(8,128)(2,1)}), bf16[16,128,16]{1,2,0:T(8,128)(2,1)S(1)}, u32[]{:S(2)}, u32[]{:S(2)}) async-start(bf16[16,128,16]{1,2,0:T(8,128)(2,1)} %copy.137), calls=%async_computation.1 | async-start | bytes 131072 | tf_op jit(solution)/shard_map/all_to_all | solution.py:205
  159.4 1.3 convert_element_type.1059
  160.7 0.8 copy.136
  161.5 5.7 %all-to-all-done.1 = bf16[16,128,16]{1,2,0:T(8,128)(2,1)S(1)} async-done(((bf16[16,128,16]{1,2,0:T(8,128)(2,1)}), bf16[16,128,16]{1,2,0:T(8,128)(2,1)S(1)}, u32[]{:S(2)}, u32[]{:S(2)}) %all-to-all-start.1) | async-done | bytes 65568 | tf_op jit(solution)/shard_map/all_to_all | solution.py:205
  167.2 3.5 all-to-all-start
  170.7 6.4 %copy.138 = bf16[16,128,1024]{1,2,0:T(8,128)(2,1)} copy(bf16[16,128,1024]{2,1,0:T(8,128)(2,1)} %bitcast.99) | data formatting | bytes 8388608 | tf_op jit(solution)/shard_map/reshape | solution.py:195
  177.1 1.4 all-to-all-done
  178.5 6.0 %all-to-all-start.2 = ((bf16[16,128,1024]{1,2,0:T(8,128)(2,1)}), bf16[16,128,1024]{1,2,0:T(8,128)(2,1)}, u32[]{:S(2)}, u32[]{:S(2)}) async-start(bf16[16,128,1024]{1,2,0:T(8,128)(2,1)} %copy.138), calls=%async_computation.2 | async-start | bytes 8388608 | tf_op jit(solution)/shard_map/all_to_all | solution.py:198
  185.4 93.4 %all-to-all-done.2 = bf16[16,128,1024]{1,2,0:T(8,128)(2,1)} async-done(((bf16[16,128,1024]{1,2,0:T(8,128)(2,1)}), bf16[16,128,1024]{1,2,0:T(8,128)(2,1)}, u32[]{:S(2)}, u32[]{:S(2)}) %all-to-all-start.2) | async-done | bytes 4194336 | tf_op jit(solution)/shard_map/all_to_all | solution.py:198
  278.8 3.1 fusion
  281.9 0.6 multiply_reduce_fusion
  282.8 0.5 select_reduce_fusion
  283.3 0.8 fusion.11
  284.1 0.5 convolution_convert_fusion.1
  284.6 19.5 %all_to_all.25 = bf16[16,20,1024]{2,1,0:T(8,128)(2,1)S(1)} all-to-all(bf16[16,20,1024]{2,1,0:T(8,128)(2,1)S(1)} %convolution_convert_fusion.1), channel_id=1, replica_groups=mesh['req'=16,'cuts'=16] {'req'}, dimensions={0} | all-to-all | bytes 1310720 | tf_op jit(solution)/shard_map/all_to_all | solution.py:237
  304.1 1.2 copy.147
  305.4 63.0 %all-gather.4.cloned.1.call-done = bf16[256,20,1024]{2,0,1:T(8,128)(2,1)} async-done(((bf16[16,20,1024]{2,0,1:T(8,128)(2,1)}), bf16[256,20,1024]{2,0,1:T(8,128)(2,1)}) %all-gather.4.cloned.1.call-update) | async-done | bytes 10485776 | tf_op jit(solution)/shard_map/all_gather | solution.py:239
  368.4 9.4 %fusion.21 = f32[256,20,176]{0,2,1:T(8,128)} fusion(bf16[256,20,1024]{2,0,1:T(8,128)(2,1)} %all-gather.4.cloned.1.call-done, bf16[1,1024,176]{1,2,0:T(8,128)(2,1)S(1)} %copy-done.3), kind=kOutput, calls=%fused_computation.36 | convolution fusion | flops 1845493760 | bytes 14450688 | tf_op jit(solution)/shard_map/necd,edf->necf/dot_general | solution.py:154
  377.8 17.9 %convolution_convert_fusion = bf16[256,20,1024]{2,0,1:T(8,128)(2,1)} fusion(f32[256,20,176]{0,2,1:T(8,128)} %fusion.21, bf16[256,20,1024]{2,0,1:T(8,128)(2,1)} %all-gather.4.cloned.1.call-done, bf16[1,1024,176]{1,2,0:T(8,128)(2,1)S(1)} %copy-done.14, bf16[1,1024,176]{1,2,0:T(8,128)(2,1)S(1)} %copy-done.15), kind=kOutput, calls=%fused_computation.4 | convolution fusion | flops 3705241600 | bytes 25296896 | tf_op jit(solution)/shard_map/necf,edf->necd/dot_general | solution.py:159
  395.7 73.2 %reduce-scatter.2.cloned.1.call-done = bf16[16,20,1024]{2,0,1:T(8,128)(2,1)} async-done(((bf16[256,20,1024]{2,0,1:T(8,128)(2,1)}), bf16[16,20,1024]{2,0,1:T(8,128)(2,1)}) %reduce-scatter.2.cloned.1.call-update) | async-done | bytes 655376 | tf_op jit(solution)/shard_map/reduce_scatter | solution.py:242
  468.9 2.4 copy.148
  471.3 7.3 %all-to-all-start.4 = ((bf16[16,20,1024]{2,1,0:T(8,128)(2,1)}), bf16[16,20,1024]{2,1,0:T(8,128)(2,1)S(1)}, u32[]{:S(2)}, u32[]{:S(2)}) async-start(bf16[16,20,1024]{2,1,0:T(8,128)(2,1)} %copy.148), calls=%async_computation.5 | async-start | bytes 1572864 | tf_op jit(solution)/shard_map/all_to_all | solution.py:250
  478.6 3.4 convolution_bitcast_fusion
  482.0 6.9 %all-to-all-done.4 = bf16[16,20,1024]{2,1,0:T(8,128)(2,1)S(1)} async-done(((bf16[16,20,1024]{2,1,0:T(8,128)(2,1)}), bf16[16,20,1024]{2,1,0:T(8,128)(2,1)S(1)}, u32[]{:S(2)}, u32[]{:S(2)}) %all-to-all-start.4) | async-done | bytes 655392 | tf_op jit(solution)/shard_map/all_to_all | solution.py:250
  489.0 3.2 fusion.14
  (57 shorter events, 2.0 us)
Async XLA Ops:
  6.5 275.4 %copy-start = (bf16[1024,1024]{1,0:T(8,128)(2,1)S(1)}, bf16[1024,1024]{1,0:T(8,128)(2,1)}, u32[]{:S(2)}) copy-start(bf16[1024,1024]{1,0:T(8,128)(2,1)} %param.23) | copy-start | bytes 6291460
  6.5 64.3 %all-gather.6.cloned.1.call-start = ((), (), s32[]{:S(2)}) async-start(), calls=%async_computation.8 | async-start | bytes 4456448 | tf_op jit(solution)/shard_map/all_gather | solution.py:191
  9.0 11.2 %copy-start.7 = (f32[16,32]{1,0:T(8,128)S(1)}, f32[16,32]{1,0:T(8,128)}, u32[]{:S(2)}) copy-start(f32[16,32]{1,0:T(8,128)} %param.21) | copy-start | bytes 6148
  20.3 0.5 copy-start.11
  44.5 0.5 copy-start.9
  64.2 4.8 copy-start.10
  64.2 5.0 copy-start.12
  64.2 5.2 %copy-start.2 = (f32[16,256,16]{1,2,0:T(8,128)S(1)}, f32[16,256,16]{1,2,0:T(8,128)}, u32[]{:S(2)}) copy-start(f32[16,256,16]{1,2,0:T(8,128)} %copy.135) | copy-start | bytes 786436
  150.9 16.3 %all-to-all-start.1 = ((bf16[16,128,16]{1,2,0:T(8,128)(2,1)}), bf16[16,128,16]{1,2,0:T(8,128)(2,1)S(1)}, u32[]{:S(2)}, u32[]{:S(2)}) async-start(bf16[16,128,16]{1,2,0:T(8,128)(2,1)} %copy.137), calls=%async_computation.1 | async-start | bytes 131072 | tf_op jit(solution)/shard_map/all_to_all | solution.py:205
  167.2 11.3 %all-to-all-start = ((bf16[16,128,16]{1,2,0:T(8,128)(2,1)}), bf16[16,128,16]{1,2,0:T(8,128)(2,1)S(1)}, u32[]{:S(2)}, u32[]{:S(2)}) async-start(bf16[16,128,16]{1,2,0:T(8,128)(2,1)} %copy.136), calls=%async_computation | async-start | bytes 131072 | tf_op jit(solution)/shard_map/all_to_all | solution.py:202
  177.1 7.6 %copy-start.8 = (bf16[1024]{0:T(1024)(128)(2,1)S(1)}, bf16[1024]{0:T(1024)(128)(2,1)}, u32[]{:S(2)}) copy-start(bf16[1024]{0:T(1024)(128)(2,1)} %param.24) | copy-start | bytes 6148
  177.1 7.6 %copy-start.13 = (s32[1,128,2]{1,2,0:T(2,128)S(1)}, s32[1,128,2]{1,2,0:T(2,128)}, u32[]{:S(2)}) copy-start(s32[1,128,2]{1,2,0:T(2,128)} %param.26) | copy-start | bytes 3076
  178.5 100.3 %all-to-all-start.2 = ((bf16[16,128,1024]{1,2,0:T(8,128)(2,1)}), bf16[16,128,1024]{1,2,0:T(8,128)(2,1)}, u32[]{:S(2)}, u32[]{:S(2)}) async-start(bf16[16,128,1024]{1,2,0:T(8,128)(2,1)} %copy.138), calls=%async_computation.2 | async-start | bytes 8388608 | tf_op jit(solution)/shard_map/all_to_all | solution.py:198
  184.5 97.5 %copy-start.4 = (bf16[1,128,1024]{2,1,0:T(8,128)(2,1)S(1)}, bf16[1,128,1024]{2,1,0:T(8,128)(2,1)}, u32[]{:S(2)}) copy-start(bf16[1,128,1024]{2,1,0:T(8,128)(2,1)} %param.22) | copy-start | bytes 786436
  184.5 183.9 %all-gather.4.cloned.1.call-start = ((), (), s32[]{:S(2)}) async-start(), calls=%async_computation.6 | async-start | bytes 11141120 | tf_op jit(solution)/shard_map/all_gather | solution.py:239
  278.8 3.7 copy-start.6
  283.3 22.0 %copy-start.5 = (f32[128,2]{1,0:T(8,128)}, f32[128,2]{1,0:T(8,128)S(1)}, u32[]{:S(2)}) copy-start(f32[128,2]{1,0:T(8,128)S(1)} %get-tuple-element.12) | copy-start | bytes 3076
  283.3 85.1 %copy-start.3 = (bf16[1,1024,176]{1,2,0:T(8,128)(2,1)S(1)}, bf16[1,1024,176]{1,2,0:T(8,128)(2,1)}, u32[]{:S(2)}) copy-start(bf16[1,1024,176]{1,2,0:T(8,128)(2,1)} %param.27) | copy-start | bytes 1081348
  305.3 72.5 %copy-start.14 = (bf16[1,1024,176]{1,2,0:T(8,128)(2,1)S(1)}, bf16[1,1024,176]{1,2,0:T(8,128)(2,1)}, u32[]{:S(2)}) copy-start(bf16[1,1024,176]{1,2,0:T(8,128)(2,1)} %param.29) | copy-start | bytes 1081348
  305.3 72.4 %copy-start.15 = (bf16[1,1024,176]{1,2,0:T(8,128)(2,1)S(1)}, bf16[1,1024,176]{1,2,0:T(8,128)(2,1)}, u32[]{:S(2)}) copy-start(bf16[1,1024,176]{1,2,0:T(8,128)(2,1)} %param.28) | copy-start | bytes 1081348
  305.3 163.5 %reduce-scatter.2.cloned.1.call-start = ((), (), s32[]{:S(2)}) async-start(), calls=%async_computation.7 | async-start | bytes 11141120 | tf_op jit(solution)/shard_map/reduce_scatter | solution.py:242
  471.3 17.7 %all-to-all-start.4 = ((bf16[16,20,1024]{2,1,0:T(8,128)(2,1)}), bf16[16,20,1024]{2,1,0:T(8,128)(2,1)S(1)}, u32[]{:S(2)}, u32[]{:S(2)}) async-start(bf16[16,20,1024]{2,1,0:T(8,128)(2,1)} %copy.148), calls=%async_computation.5 | async-start | bytes 1572864 | tf_op jit(solution)/shard_map/all_to_all | solution.py:250
  478.6 13.6 %copy-start.1 = (bf16[1024,1024]{1,0:T(8,128)(2,1)S(1)}, bf16[1024,1024]{1,0:T(8,128)(2,1)}, u32[]{:S(2)}) copy-start(bf16[1024,1024]{1,0:T(8,128)(2,1)} %param.23) | copy-start | bytes 6291460
Sparse Core Ops, SparseCore 0:
  9.2 44.7 all-gather.5
  305.4 62.9 all-gather.3
  395.8 73.0 reduce-scatter.1

commit v2 on v1

--- a/solution.py
+++ b/solution.py
@@ -91,8 +91,11 @@
     new_distance = (blocks * q_rows - cut * new_rows) + q_rows - new_lanes
     cache_bucket = bucket_index(jnp.maximum(cache_distance, 0), edges)
     new_bucket = bucket_index(jnp.maximum(new_distance, 0), edges)
-    cache_table = jnp.take(tables, cache_bucket, axis=1).transpose(1, 0, 2)
-    new_table = jnp.take(tables, new_bucket, axis=1).transpose(1, 0, 2)
+    choices = jnp.arange(tables.shape[1], dtype=jnp.int32)
+    cache_hot = (cache_bucket[..., None] == choices).astype(jnp.float32)
+    new_hot = (new_bucket[..., None] == choices).astype(jnp.float32)
+    cache_table = jnp.einsum("bmk,hk->bhm", cache_hot, tables, precision=lax.Precision.HIGHEST)
+    new_table = jnp.einsum("bmk,hk->bhm", new_hot, tables, precision=lax.Precision.HIGHEST)
     return cache_table, new_table
 
 
@@ -148,15 +151,6 @@
     factor = jnp.exp(block_peak - best_peak[None]) * block_total
     weighted = jnp.sum(factor[..., None] * block_out.astype(jnp.float32), axis=0)
     return (weighted / jnp.sum(factor, axis=0)[..., None]).astype(jnp.bfloat16)
-
-
-def expert_part(row_block, gate_piece, up_piece, down_piece):
-    gate_act = jnp.einsum(
-        "necd,edf->necf", row_block, gate_piece, preferred_element_type=jnp.float32
-    )
-    up_act = jnp.einsum("necd,edf->necf", row_block, up_piece, preferred_element_type=jnp.float32)
-    act_rows = (jax.nn.gelu(gate_act) * up_act).astype(jnp.bfloat16)
-    return jnp.einsum("necf,edf->necd", act_rows, down_piece, preferred_element_type=jnp.float32)
 
 
 def per_device(
@@ -235,18 +229,16 @@
         "ect,td->ecd", dispatch.astype(jnp.bfloat16), normed, preferred_element_type=jnp.float32
     ).astype(jnp.bfloat16)
     arrived = lax.all_to_all(buffers, "req", split_axis=0, concat_axis=0, tiled=True)
-    local_experts = gate_weight.shape[0]
-    gathered = lax.all_gather(arrived, "cuts", axis=0, tiled=True)
-    row_count = lax.axis_size("cuts") * arrived.shape[0]
-    row_block = gathered.reshape(row_count, local_experts, capacity, model_width)
-    expert_out = lax.psum_scatter(
-        expert_part(row_block, gate_weight, up_weight, down_weight)
-        .reshape(row_count, local_experts * capacity, model_width)
-        .astype(jnp.bfloat16),
-        "cuts",
-        scatter_dimension=0,
-        tiled=True,
-    )
+    full_gate = lax.all_gather(gate_weight[0], "cuts", axis=1, tiled=True)
+    full_up = lax.all_gather(up_weight[0], "cuts", axis=1, tiled=True)
+    full_down = lax.all_gather(down_weight[0], "cuts", axis=1, tiled=True)
+    flat_rows = arrived.reshape(-1, model_width)
+    gate_act = jnp.dot(flat_rows, full_gate, preferred_element_type=jnp.float32)
+    up_act = jnp.dot(flat_rows, full_up, preferred_element_type=jnp.float32)
+    act_rows = (jax.nn.gelu(gate_act) * up_act).astype(jnp.bfloat16)
+    expert_out = lax.dot_general(
+        act_rows, full_down, (((1,), (1,)), ((), ())), preferred_element_type=jnp.float32
+    ).astype(jnp.bfloat16).reshape(arrived.shape)
     returned = lax.all_to_all(expert_out, "req", split_axis=0, concat_axis=0, tiled=True)
     combine = jnp.einsum(
         "tke,tkc,tk->ect", onehot, slot_hot, gate_values, precision=lax.Precision.HIGHEST

time: 501 us -> 351 us (0.70)
  waiting for transfers between devices: 244 us -> 155 us
  local copies, waits for them, and re-layouts: 67.1 us -> 23.6 us
  matrix products: 36.1 us -> 28.5 us
  starting transfers between devices: 25.5 us -> 19.3 us
    reduce_scatter x1 -> x0, waiting for transfers between devices: 73.2 us -> none  [per_device(): lax.psum_scatter(expert_part(row_block, gate_weight, up_weight, down_weig...]
    all_gather x1 -> x3, waiting for transfers between devices: 63 us -> 0.01 us  [the longest x1 0.01 us: per_device(): full_gate = lax.all_gather(gate_weight[0], 'cuts', axis=1, tiled=True)]
    gather x4 -> x0, local copies, waits for them, and re-layouts: 41.9 us -> none  [the longest x2 23.5 us: bias_tables(): cache_table = jnp.take(tables, cache_bucket, axis=1).transpose(1, 0, 2)]
    all_gather x1, waiting for transfers between devices: 0.01 us -> 24.9 us  [per_device(): every_query = lax.all_gather(queries[0], 'cuts', axis=0, tiled=True)]
    all_to_all x1, waiting for transfers between devices: 93.4 us -> 112 us  [per_device(): lax.all_to_all(shortened(block_out), 'cuts', split_axis=0, concat_axis=0,...]
    dot_general x2 -> x4, matrix products: 27.3 us -> 19.8 us  [the longest x1 10.2 us: per_device(): lax.dot_general(act_rows, full_down, (((1,), (1,)), ((), ())), preferred_...]
  transfers between devices with their start and end apart: 7 -> 8, of which waited for: 6 -> 5; matrix products, arithmetic and copies ran while one was open for 15% -> 14% of each run, Pallas kernels for 0% -> 22%
where the time goes in v2:
time: 351 us; the launch traced here: 350 us
  waiting for transfers between devices  155 us (44%)
  Pallas kernels  77.9 us (22%)
  matrix products  28.5 us (8%)
  local copies, waits for them, and re-layouts  23.6 us (7%)
  blocking collectives  19.9 us (6%)
  starting transfers between devices  19.3 us (5%)
  between operations  14 us (4%)
  other arithmetic  11.7 us (3%)
    all_to_all x1, waiting for transfers between devices, per_device(): lax.all_to_all(shortened(block_out), 'cuts', split_axis=0, concat_axis=0,...  112 us
    pallas_call x1, Pallas kernels, block_partials(): pl.pallas_call(attention_kernel, grid_spec=grid_spec, out_shape=[jax.Shap...  77.9 us
    all_gather x1, waiting for transfers between devices, per_device(): every_query = lax.all_gather(queries[0], 'cuts', axis=0, tiled=True)  24.9 us
    all_to_all x1, blocking collectives, per_device(): lax.all_to_all(buffers, 'req', split_axis=0, concat_axis=0, tiled=True)  19.9 us
    dot_general x1, matrix products, per_device(): lax.dot_general(act_rows, full_down, (((1,), (1,)), ((), ())), preferred_...  10.2 us
    all_to_all x1, waiting for transfers between devices, per_device(): lax.all_to_all(expert_out, 'req', split_axis=0, concat_axis=0, tiled=True)  8.75 us
    dot_general x1, matrix products, per_device(): gate_act = jnp.dot(flat_rows, full_gate, preferred_element_type=jnp.float32)  7.5 us
  transfers between devices with their start and end apart: 8, of which 5 were waited for; matrix products, arithmetic and copies ran while one was open for 14% of the time, Pallas kernels for 22%

profile of v2, /device:TPU:8, one launch (start us, length us, event | category | flops | bytes accessed | tf_op | source)
XLA Modules:
  0.0 350.2 jit_solution(13958334641587086634)
XLA Ops:
  6.5 0.7 all-gather.9.cloned.1.call-update
  7.3 0.7 all-gather.11.cloned.1.call-update
  8.1 0.7 all-gather.15.cloned.1.call-update
  9.4 1.1 copy.68
  10.5 1.0 copy.70
  11.5 2.1 copy.67
  13.6 1.5 copy.69
  15.1 1.1 copy.72
  16.3 1.0 copy.74
  17.3 2.1 copy.71
  19.4 2.4 copy.73
  21.8 0.6 pad_add_fusion.scalars
  22.4 4.2 %maximum_bitcast_fusion = (bf16[16,384,64]{2,1,0:T(8,128)(2,1)}, bf16[16,384,64]{2,1,0:T(8,128)(2,1)}) fusion(bf16[128,16,64]{2,0,1:T(8,128)(2,1)} %copy.70, bf16[256,16,64]{2,0,1:T(8,128)(2,1)S(1)} %copy.69, bf16[128,16,64]{2,0,1:T(8,128)(2,1)} %copy.74, bf16[256,16,64]{2,0,1:T(8,128)(2,1)} %copy.73), kind=kLoop, calls=%fused_computation.18 | loop fusion | flops 3145728 | bytes 3145728 | tf_op jit(solution)/shard_map/transpose | solution.py:110
  26.6 0.1 convert_add_fusion.1
  26.8 0.2 convert_add_fusion
  26.9 1.0 convolution_bitcast_fusion.3.tn_ref
  27.9 1.1 convolution_bitcast_fusion.2.tc_ref
  29.1 24.9 %all-gather.9.cloned.1.call-done = bf16[1,2048,1024]{2,1,0:T(8,128)(2,1)} async-done(((bf16[1,128,1024]{2,1,0:T(8,128)(2,1)}), bf16[1,2048,1024]{2,1,0:T(8,128)(2,1)}) %all-gather.9.cloned.1.call-update) | async-done | bytes 4194320 | tf_op jit(solution)/shard_map/all_gather | solution.py:185
  54.0 77.9 %shard_map.145 = (bf16[2048,1024]{1,0:T(8,128)(2,1)}, f32[2048,16]{1,0:T(8,128)}, f32[2048,16]{1,0:T(8,128)}) custom-call(s32[2]{0:T(128)} %pad_add_fusion.scalars, bf16[2048,1024]{1,0:T(8,128)(2,1)} %bitcast.87, bf16[16,384,64]{2,1,0:T(8,128)(2,1)} %get-tuple-element.17.k_ref, bf16[16,384,64]{2,1,0:T(8,128)(2,1)} %get-tuple-element.18.v_ref, ...), custom_call_target="tpu_custom_call" | custom-call | flops 3221225472 | bytes 9961472 | tf_op jit(solution)/shard_map/pallas_call | solution.py:133
  131.8 1.3 convert_element_type.568
  133.1 0.8 copy.76
  133.9 4.4 %all-to-all-start.1 = ((bf16[16,128,16]{1,2,0:T(8,128)(2,1)}), bf16[16,128,16]{1,2,0:T(8,128)(2,1)S(1)}, u32[]{:S(2)}, u32[]{:S(2)}) async-start(bf16[16,128,16]{1,2,0:T(8,128)(2,1)} %copy.76), calls=%async_computation.1 | async-start | bytes 131072 | tf_op jit(solution)/shard_map/all_to_all | solution.py:199
  138.4 0.5 all-gather.13.cloned.1.call-update
  139.0 1.3 convert_element_type.565
  140.2 0.8 copy.75
  141.1 5.3 %all-to-all-done.1 = bf16[16,128,16]{1,2,0:T(8,128)(2,1)S(1)} async-done(((bf16[16,128,16]{1,2,0:T(8,128)(2,1)}), bf16[16,128,16]{1,2,0:T(8,128)(2,1)S(1)}, u32[]{:S(2)}, u32[]{:S(2)}) %all-to-all-start.1) | async-done | bytes 65568 | tf_op jit(solution)/shard_map/all_to_all | solution.py:199
  146.3 3.5 all-to-all-start
  149.8 6.4 %copy.77 = bf16[16,128,1024]{1,2,0:T(8,128)(2,1)} copy(bf16[16,128,1024]{2,1,0:T(8,128)(2,1)} %bitcast.79) | data formatting | bytes 8388608 | tf_op jit(solution)/shard_map/reshape | solution.py:189
  156.3 1.3 all-to-all-done
  157.6 6.0 %all-to-all-start.2 = ((bf16[16,128,1024]{1,2,0:T(8,128)(2,1)}), bf16[16,128,1024]{1,2,0:T(8,128)(2,1)}, u32[]{:S(2)}, u32[]{:S(2)}) async-start(bf16[16,128,1024]{1,2,0:T(8,128)(2,1)} %copy.77), calls=%async_computation.2 | async-start | bytes 8388608 | tf_op jit(solution)/shard_map/all_to_all | solution.py:192
  163.8 0.3 convert_reduce_fusion
  164.0 0.1 fusion.44
  164.3 112.4 %all-to-all-done.2 = bf16[16,128,1024]{1,2,0:T(8,128)(2,1)} async-done(((bf16[16,128,1024]{1,2,0:T(8,128)(2,1)}), bf16[16,128,1024]{1,2,0:T(8,128)(2,1)}, u32[]{:S(2)}, u32[]{:S(2)}) %all-to-all-start.2) | async-done | bytes 4194336 | tf_op jit(solution)/shard_map/all_to_all | solution.py:192
  276.7 3.1 fusion
  279.9 0.5 multiply_reduce_fusion
  280.4 0.3 fusion.111
  280.7 0.5 select_reduce_fusion
  281.2 0.8 fusion.25
  282.0 0.5 convolution_convert_fusion
  282.5 19.9 %all_to_all.25 = bf16[16,20,1024]{2,1,0:T(8,128)(2,1)S(1)} all-to-all(bf16[16,20,1024]{2,1,0:T(8,128)(2,1)S(1)} %convolution_convert_fusion), channel_id=1, replica_groups=mesh['req'=16,'cuts'=16] {'req'}, dimensions={0} | all-to-all | bytes 1310720 | tf_op jit(solution)/shard_map/all_to_all | solution.py:231
  302.4 1.0 reshape.293
  303.4 7.5 %fusion.19 = f32[320,2816]{1,0:T(8,128)} fusion(bf16[320,1024]{1,0:T(8,128)(2,1)} %reshape.293, bf16[1,1024,2816]{1,2,0:T(8,128)(2,1)} %all-gather.11.cloned.1.call-done), kind=kOutput, calls=%fused_computation.17 | convolution fusion | flops 1852702720 | bytes 10027008 | tf_op jit(solution)/shard_map/dot_general | solution.py:236
  310.9 10.2 %fusion.22 = bf16[320,1024]{1,0:T(8,128)(2,1)} fusion(bf16[1,1024,2816]{1,2,0:T(8,128)(2,1)} %all-gather.15.cloned.1.call-done, f32[320,2816]{1,0:T(8,128)} %fusion.19, bf16[320,1024]{1,0:T(8,128)(2,1)S(1)} %copy-done.1, bf16[1,1024,2816]{1,2,0:T(8,128)(2,1)} %all-gather.13.cloned.1.call-done), kind=kOutput, calls=%fused_computation.22 | convolution fusion | flops 3693117440 | bytes 16449536 | tf_op jit(solution)/shard_map/dot_general | solution.py:239
  321.1 2.1 reshape.294
  323.1 5.2 %all-to-all-start.4 = ((bf16[16,20,1024]{2,1,0:T(8,128)(2,1)}), bf16[16,20,1024]{2,1,0:T(8,128)(2,1)S(1)}, u32[]{:S(2)}, u32[]{:S(2)}) async-start(bf16[16,20,1024]{2,1,0:T(8,128)(2,1)} %reshape.294), calls=%async_computation.4 | async-start | bytes 1572864 | tf_op jit(solution)/shard_map/all_to_all | solution.py:242
  328.4 3.3 convolution_bitcast_fusion
  331.7 8.8 %all-to-all-done.4 = bf16[16,20,1024]{2,1,0:T(8,128)(2,1)S(1)} async-done(((bf16[16,20,1024]{2,1,0:T(8,128)(2,1)}), bf16[16,20,1024]{2,1,0:T(8,128)(2,1)S(1)}, u32[]{:S(2)}, u32[]{:S(2)}) %all-to-all-start.4) | async-done | bytes 655392 | tf_op jit(solution)/shard_map/all_to_all | solution.py:242
  340.4 3.2 fusion.28
  (33 shorter events, 0.4 us)
Async XLA Ops:
  6.5 273.3 %copy-start = (bf16[1024,1024]{1,0:T(8,128)(2,1)S(1)}, bf16[1024,1024]{1,0:T(8,128)(2,1)}, u32[]{:S(2)}) copy-start(bf16[1024,1024]{1,0:T(8,128)(2,1)} %param.23) | copy-start | bytes 6291460
  6.5 47.4 %all-gather.9.cloned.1.call-start = ((), (), s32[]{:S(2)}) async-start(), calls=%async_computation.5 | async-start | bytes 4456448 | tf_op jit(solution)/shard_map/all_gather | solution.py:185
  7.3 296.2 %all-gather.11.cloned.1.call-start = ((), (), s32[]{:S(2)}) async-start(), calls=%async_computation.6 | async-start | bytes 6127616 | tf_op jit(solution)/shard_map/all_gather | solution.py:232
  8.0 302.9 %all-gather.15.cloned.1.call-start = ((), (), s32[]{:S(2)}) async-start(), calls=%async_computation.8 | async-start | bytes 6127616 | tf_op jit(solution)/shard_map/all_gather | solution.py:234
  19.4 7.5 %copy-start.5 = (f32[16,32]{1,0:T(8,128)S(1)}, f32[16,32]{1,0:T(8,128)}, u32[]{:S(2)}) copy-start(f32[16,32]{1,0:T(8,128)} %param.21) | copy-start | bytes 6148
  133.9 12.4 %all-to-all-start.1 = ((bf16[16,128,16]{1,2,0:T(8,128)(2,1)}), bf16[16,128,16]{1,2,0:T(8,128)(2,1)S(1)}, u32[]{:S(2)}, u32[]{:S(2)}) async-start(bf16[16,128,16]{1,2,0:T(8,128)(2,1)} %copy.76), calls=%async_computation.1 | async-start | bytes 131072 | tf_op jit(solution)/shard_map/all_to_all | solution.py:199
  138.4 172.5 %all-gather.13.cloned.1.call-start = ((), (), s32[]{:S(2)}) async-start(), calls=%async_computation.7 | async-start | bytes 6127616 | tf_op jit(solution)/shard_map/all_gather | solution.py:233
  146.3 11.3 %all-to-all-start = ((bf16[16,128,16]{1,2,0:T(8,128)(2,1)}), bf16[16,128,16]{1,2,0:T(8,128)(2,1)S(1)}, u32[]{:S(2)}, u32[]{:S(2)}) async-start(bf16[16,128,16]{1,2,0:T(8,128)(2,1)} %copy.75), calls=%async_computation | async-start | bytes 131072 | tf_op jit(solution)/shard_map/all_to_all | solution.py:196
  156.3 7.4 %copy-start.6 = (bf16[1024]{0:T(1024)(128)(2,1)S(1)}, bf16[1024]{0:T(1024)(128)(2,1)}, u32[]{:S(2)}) copy-start(bf16[1024]{0:T(1024)(128)(2,1)} %param.24) | copy-start | bytes 6148
  156.3 7.4 %copy-start.7 = (s32[1,128,2]{1,2,0:T(2,128)S(1)}, s32[1,128,2]{1,2,0:T(2,128)}, u32[]{:S(2)}) copy-start(s32[1,128,2]{1,2,0:T(2,128)} %param.26) | copy-start | bytes 3076
  157.6 119.1 %all-to-all-start.2 = ((bf16[16,128,1024]{1,2,0:T(8,128)(2,1)}), bf16[16,128,1024]{1,2,0:T(8,128)(2,1)}, u32[]{:S(2)}, u32[]{:S(2)}) async-start(bf16[16,128,1024]{1,2,0:T(8,128)(2,1)} %copy.77), calls=%async_computation.2 | async-start | bytes 8388608 | tf_op jit(solution)/shard_map/all_to_all | solution.py:192
  163.6 116.2 %copy-start.2 = (bf16[1,128,1024]{2,1,0:T(8,128)(2,1)S(1)}, bf16[1,128,1024]{2,1,0:T(8,128)(2,1)}, u32[]{:S(2)}) copy-start(bf16[1,128,1024]{2,1,0:T(8,128)(2,1)} %param.22) | copy-start | bytes 786436
  276.7 3.7 %copy-start.4 = (bf16[1024,16]{0,1:T(8,128)(2,1)S(1)}, bf16[1024,16]{0,1:T(8,128)(2,1)}, u32[]{:S(2)}) copy-start(bf16[1024,16]{0,1:T(8,128)(2,1)} %param.25) | copy-start | bytes 98308
  281.2 0.8 copy-start.3
  303.4 7.5 %copy-start.1 = (bf16[320,1024]{1,0:T(8,128)(2,1)S(1)}, bf16[320,1024]{1,0:T(8,128)(2,1)}, u32[]{:S(2)}) copy-start(bf16[320,1024]{1,0:T(8,128)(2,1)} %reshape.293) | copy-start | bytes 1966084
  323.1 17.3 %all-to-all-start.4 = ((bf16[16,20,1024]{2,1,0:T(8,128)(2,1)}), bf16[16,20,1024]{2,1,0:T(8,128)(2,1)S(1)}, u32[]{:S(2)}, u32[]{:S(2)}) async-start(bf16[16,20,1024]{2,1,0:T(8,128)(2,1)} %reshape.294), calls=%async_computation.4 | async-start | bytes 1572864 | tf_op jit(solution)/shard_map/all_to_all | solution.py:242
Sparse Core Ops, SparseCore 0:
  9.2 44.7 all-gather.8
  55.8 43.2 all-gather.10
  100.9 43.3 all-gather.14
  146.0 107.4 all-gather.12

commit v3 on v2

v3 whole, which is shorter than its diff:
```python
from functools import partial

import jax
import jax.numpy as jnp
import numpy as np
from jax import lax
from jax.sharding import PartitionSpec as P
from jax.experimental import pallas as pl
from jax.experimental.pallas import tpu as pltpu

MAXDIST = 128


def shortened(value):
    return jax.tree.map(lambda a: a.astype(jnp.bfloat16) if a.dtype == jnp.float32 else a, value)


def bucket_number(distance, bucket_count, reach_limit):
    exact_count = bucket_count // 2
    if distance < exact_count:
        return distance
    level_value = exact_count + int(
        np.floor(exact_count * np.log(distance / exact_count) / np.log(reach_limit / exact_count))
    )
    return min(bucket_count - 1, level_value)


def bucket_edges(bucket_count, reach_limit):
    edge_list = []
    for target in range(1, bucket_count):
        probe_value = 0
        while bucket_number(probe_value, bucket_count, reach_limit) < target:
            probe_value += 1
        edge_list.append(probe_value)
    return edge_list


def bucket_index(distance, edge_list):
    bucket_level = jnp.zeros(distance.shape, jnp.int32)
    for edge_value in edge_list:
        bucket_level = bucket_level + (distance >= edge_value).astype(jnp.int32)
    return bucket_level


def attention_kernel(scalars, q_ref, k_ref, v_ref, tc_ref, tn_ref, o_ref):
    length = scalars[0]
    block = pl.program_id(0)
    q_rows = q_ref.shape[0]
    key_blocks, key_span, head_dim = k_ref.shape
    cache_rows = tc_ref.shape[2] - q_rows
    new_rows = key_span - cache_rows
    row = lax.broadcasted_iota(jnp.int32, (q_rows, key_span), 0)
    col = lax.broadcasted_iota(jnp.int32, (q_rows, key_span), 1)
    is_cache = col < cache_rows
    cache_width = tc_ref.shape[2]
    new_width = tn_ref.shape[2]
    query = q_ref[...]

    def one_block(g, carry):
        best, weighted, factor_sum = carry
        cache_live = g * cache_rows + col < length
        new_live = g * new_rows + (col - cache_rows) <= block * q_rows + row
        visible = (is_cache & cache_live) | (jnp.logical_not(is_cache) & new_live)
        scores = lax.dot_general(
            query, k_ref[g], (((1,), (1,)), ((), ())), preferred_element_type=jnp.float32
        ) / 8.0
        cache_table = jnp.broadcast_to(tc_ref[0, pl.ds(g, 1), :], (q_rows, cache_width))
        cache_bias = pltpu.roll(cache_table, cache_width - q_rows, 1, stride=1, stride_axis=0)
        new_table = jnp.broadcast_to(tn_ref[0, pl.ds(g, 1), :], (q_rows, new_width))
        new_bias = pltpu.roll(new_table, new_width - q_rows, 1, stride=1, stride_axis=0)
        bias = jnp.concatenate([cache_bias[:, :cache_rows], new_bias[:, :new_rows]], axis=1)
        masked = jnp.where(visible, scores + bias, -1e30)
        peak = jnp.max(masked, axis=1, keepdims=True)
        weights = jnp.where(visible, jnp.exp(masked - peak), 0.0)
        total = jnp.sum(weights, axis=1, keepdims=True)
        numerator = jnp.dot(
            weights.astype(jnp.bfloat16), v_ref[g], preferred_element_type=jnp.float32
        )
        block_out = (numerator / jnp.maximum(total, 1.0)).astype(jnp.bfloat16).astype(jnp.float32)
        new_best = jnp.maximum(best, peak)
        rescale = jnp.exp(best - new_best)
        factor = jnp.exp(peak - new_best) * total
        return (new_best, weighted * rescale + factor * block_out, factor_sum * rescale + factor)

    start = (
        jnp.full((q_rows, 1), -1e30, jnp.float32),
        jnp.zeros((q_rows, head_dim), jnp.float32),
        jnp.zeros((q_rows, 1), jnp.float32),
    )
    best, weighted, factor_sum = lax.fori_loop(0, key_blocks, one_block, start)
    o_ref[...] = (weighted / factor_sum).astype(o_ref.dtype)


def bias_tables(head_table, length, q_rows, cache_rows, new_rows, query_blocks, key_blocks):
    edges = bucket_edges(head_table.shape[1], MAXDIST)
    blocks = jnp.arange(query_blocks, dtype=jnp.int32)[:, None, None]
    key_ids = jnp.arange(key_blocks, dtype=jnp.int32)[None, :, None]
    cache_lanes = jnp.arange(cache_rows + q_rows, dtype=jnp.int32)[None, None, :]
    new_lanes = jnp.arange(new_rows + q_rows, dtype=jnp.int32)[None, None, :]
    cache_distance = length + blocks * q_rows - key_ids * cache_rows + q_rows - cache_lanes
    new_distance = (blocks * q_rows - key_ids * new_rows) + q_rows - new_lanes
    cache_bucket = bucket_index(jnp.maximum(cache_distance, 0), edges)
    new_bucket = bucket_index(jnp.maximum(new_distance, 0), edges)
    choices = jnp.arange(head_table.shape[1], dtype=jnp.int32)
    cache_hot = (cache_bucket[..., None] == choices).astype(jnp.float32)
    new_hot = (new_bucket[..., None] == choices).astype(jnp.float32)
    cache_table = jnp.einsum("agmk,hk->agm", cache_hot, head_table, precision=lax.Precision.HIGHEST)
    new_table = jnp.einsum("agmk,hk->agm", new_hot, head_table, precision=lax.Precision.HIGHEST)
    return cache_table, new_table


def block_partials(query_rows, key_rows, value_rows, head_table, length, cache_rows, q_rows):
    key_blocks, key_span, head_dim = key_rows.shape
    new_rows = key_span - cache_rows
    query_total = query_rows.shape[0]
    query_blocks = query_total // q_rows
    cache_table, new_table = bias_tables(
        head_table, length, q_rows, cache_rows, new_rows, query_blocks, key_blocks
    )
    scalars = jnp.stack([length]).astype(jnp.int32)
    grid_spec = pltpu.PrefetchScalarGridSpec(
        num_scalar_prefetch=1,
        grid=(query_blocks,),
        in_specs=[
            pl.BlockSpec((q_rows, head_dim), lambda b, s: (b, 0)),
            pl.BlockSpec((key_blocks, key_span, head_dim), lambda b, s: (0, 0, 0)),
            pl.BlockSpec((key_blocks, key_span, head_dim), lambda b, s: (0, 0, 0)),
            pl.BlockSpec((1, key_blocks, cache_table.shape[2]), lambda b, s: (b, 0, 0)),
            pl.BlockSpec((1, key_blocks, new_table.shape[2]), lambda b, s: (b, 0, 0)),
        ],
        out_specs=pl.BlockSpec((q_rows, head_dim), lambda b, s: (b, 0)),
    )
    pairs = query_total * key_span * key_blocks
    return pl.pallas_call(
        attention_kernel,
        grid_spec=grid_spec,
        out_shape=jax.ShapeDtypeStruct((query_total, head_dim), jnp.bfloat16),
        cost_estimate=pl.CostEstimate(
            flops=4 * pairs * head_dim,
            transcendentals=pairs,
            bytes_accessed=4 * query_total * head_dim * key_blocks + 4 * key_span * key_blocks * head_dim,
        ),
    )(scalars, query_rows, key_rows, value_rows, cache_table, new_table)


def per_device(
    queries,
    new_keys,
    new_values,
    cache_keys,
    cache_values,
    cache_lengths,
    relative_bias,
    residual,
    out_weight,
    norm_gain,
    router_weight,
    routes,
    gate_weight,
    up_weight,
    down_weight,
):
    cut_count = lax.axis_size("cuts")
    cut_index = lax.axis_index("cuts")
    q_rows = queries.shape[1]
    cache_rows = cache_keys.shape[1]
    model_width = queries.shape[2]
    head_count = relative_bias.shape[0]
    head_dim = model_width // head_count
    bucket_count = relative_bias.shape[1]
    length = cache_lengths[0]
    query_total = q_rows * cut_count
    local_keys = jnp.concatenate([cache_keys[0], new_keys[0]], axis=0)
    local_values = jnp.concatenate([cache_values[0], new_values[0]], axis=0)
    head_queries = lax.all_to_all(
        queries[0].reshape(q_rows, head_count, head_dim), "cuts", split_axis=1, concat_axis=0, tiled=True
    ).reshape(query_total, head_dim)
    key_span = local_keys.shape[0]
    head_keys = lax.all_to_all(
        local_keys.reshape(key_span, head_count, head_dim), "cuts", split_axis=1, concat_axis=0, tiled=True
    ).reshape(cut_count, key_span, head_dim)
    head_values = lax.all_to_all(
        local_values.reshape(key_span, head_count, head_dim), "cuts", split_axis=1, concat_axis=0, tiled=True
    ).reshape(cut_count, key_span, head_dim)
    head_table = lax.dynamic_slice_in_dim(relative_bias, cut_index, 1, 0)
    head_out = block_partials(
        head_queries, head_keys, head_values, head_table, length, cache_rows, q_rows
    )
    attended = lax.all_to_all(
        head_out.reshape(cut_count, q_rows, head_dim), "cuts", split_axis=0, concat_axis=0, tiled=True
    ).transpose(1, 0, 2).reshape(q_rows, model_width)
    hidden = residual[0].astype(jnp.float32) + jnp.dot(
        attended, out_weight, preferred_element_type=jnp.float32
    )
    inv_rms = lax.rsqrt(jnp.mean(hidden * hidden, axis=1, keepdims=True) + 1e-06)
    normed = (hidden * inv_rms * norm_gain.astype(jnp.float32)).astype(jnp.bfloat16)
    experts = router_weight.shape[1]
    capacity = (10 * q_rows + 4 * experts - 1) // (4 * experts)
    logits = jnp.dot(normed, router_weight, preferred_element_type=jnp.float32)
    chosen = routes[0]
    onehot = (chosen[:, :, None] == jnp.arange(experts, dtype=jnp.int32)[None, None, :]).astype(
        jnp.float32
    )
    gate_values = jax.nn.sigmoid(jnp.sum(onehot * logits[:, None, :], axis=2))
    named_count = jnp.sum(onehot, axis=1)
    earlier_mask = (jnp.arange(q_rows)[:, None] > jnp.arange(q_rows)[None, :]).astype(jnp.bfloat16)
    earlier = jnp.dot(
        earlier_mask, named_count.astype(jnp.bfloat16), preferred_element_type=jnp.float32
    )
    slot_number = jnp.sum(onehot * earlier[:, None, :], axis=2)
    slot_hot = (
        slot_number[:, :, None] == jnp.arange(capacity, dtype=jnp.float32)[None, None, :]
    ).astype(jnp.float32)
    dispatch = jnp.einsum("tke,tkc->ect", onehot, slot_hot)
    buffers = jnp.einsum(
        "ect,td->ecd", dispatch.astype(jnp.bfloat16), normed, preferred_element_type=jnp.float32
    ).astype(jnp.bfloat16)
    arrived = lax.all_to_all(buffers, "req", split_axis=0, concat_axis=0, tiled=True)
    full_gate = lax.all_gather(gate_weight[0], "cuts", axis=1, tiled=True)
    full_up = lax.all_gather(up_weight[0], "cuts", axis=1, tiled=True)
    full_down = lax.all_gather(down_weight[0], "cuts", axis=1, tiled=True)
    flat_rows = arrived.reshape(-1, model_width)
    gate_act = jnp.dot(flat_rows, full_gate, preferred_element_type=jnp.float32)
    up_act = jnp.dot(flat_rows, full_up, preferred_element_type=jnp.float32)
    act_rows = (jax.nn.gelu(gate_act) * up_act).astype(jnp.bfloat16)
    expert_out = lax.dot_general(
        act_rows, full_down, (((1,), (1,)), ((), ())), preferred_element_type=jnp.float32
    ).astype(jnp.bfloat16).reshape(arrived.shape)
    returned = lax.all_to_all(expert_out, "req", split_axis=0, concat_axis=0, tiled=True)
    combine = jnp.einsum(
        "tke,tkc,tk->ect", onehot, slot_hot, gate_values, precision=lax.Precision.HIGHEST
    )
    gathered_back = jnp.einsum(
        "ect,ecd->td", combine, returned.astype(jnp.float32), precision=lax.Precision.HIGHEST
    )
    layer_out = hidden + gathered_back
    return layer_out.astype(jnp.bfloat16)[None]


def solution(mesh):
    return jax.shard_map(
        per_device,
        mesh=mesh,
        in_specs=(
            P("req", "cuts", None),
            P("req", "cuts", None),
            P("req", "cuts", None),
            P("req", "cuts", None),
            P("req", "cuts", None),
            P("req"),
            P(),
            P("req", "cuts", None),
            P(),
            P(),
            P(),
            P("req", "cuts", None),
            P("req", None, "cuts"),
            P("req", None, "cuts"),
            P("req", None, "cuts"),
        ),
        out_specs=P("req", "cuts", None),
        check_vma=False,
    )
```

time: 351 us -> 298 us (0.85)
  waiting for transfers between devices: 155 us -> 62 us
  Pallas kernels: 77.9 us -> 112 us
  starting transfers between devices: 19.3 us -> 29.2 us
  matrix products: 28.5 us -> 34.3 us
  other arithmetic: 11.7 us -> 6.06 us
  local copies, waits for them, and re-layouts: 23.6 us -> 18.6 us
    all_to_all x3 -> x4, waiting for transfers between devices: 119 us -> 50.6 us  [the longest x1 25.4 us: per_device(): lax.all_to_all(local_keys.reshape(key_span, head_count, head_dim), 'cuts'...]
    pallas_call x1, Pallas kernels: 77.9 us -> 112 us  [block_partials(): pl.pallas_call(attention_kernel, grid_spec=grid_spec, out_shape=jax.Shape...]
    all_gather x1 -> x0, waiting for transfers between devices: 24.9 us -> none  [per_device(): every_query = lax.all_gather(queries[0], 'cuts', axis=0, tiled=True)]
    all_to_all x3 -> x4, starting transfers between devices: 13.9 us -> 23.9 us  [the longest x1 8.57 us: per_device(): lax.all_to_all(queries[0].reshape(q_rows, head_count, head_dim), 'cuts',...]
    concatenate x4 -> x0, local copies, waits for them, and re-layouts: 5.95 us -> none  [the longest x2 3.41 us: per_device(): local_values = jnp.concatenate([cache_values[0], new_values[0]], axis=0)]
    dot_general x2, matrix products: 2.11 us -> 7.86 us  [the longest x1 4.55 us: bias_tables(): jnp.einsum('agmk,hk->agm', cache_hot, head_table, precision=lax.Precision...]
    all_to_all x0 -> x3, local copies, waits for them, and re-layouts: none -> 5.02 us  [the longest x1 2.44 us: per_device(): lax.all_to_all(local_values.reshape(key_span, head_count, head_dim), 'cut...]
    reshape x1, local copies, waits for them, and re-layouts: 6.44 us -> 1.94 us  [per_device(): head_out.reshape(cut_count, q_rows, head_dim)]
  transfers between devices with their start and end apart: 8 -> 8, of which waited for: 5 -> 5; matrix products, arithmetic and copies ran while one was open for 14% -> 14% of each run, Pallas kernels for 22% -> 38%
where the time goes in v3:
time: 298 us; the launch traced here: 297 us
  Pallas kernels  112 us (38%)
  waiting for transfers between devices  62 us (21%)
  matrix products  34.3 us (12%)
  starting transfers between devices  29.2 us (10%)
  blocking collectives  21 us (7%)
  local copies, waits for them, and re-layouts  18.6 us (6%)
  between operations  13.9 us (5%)
  other arithmetic  6.06 us (2%)
    pallas_call x1, Pallas kernels, block_partials(): pl.pallas_call(attention_kernel, grid_spec=grid_spec, out_shape=jax.Shape...  112 us
    all_to_all x1, waiting for transfers between devices, per_device(): lax.all_to_all(local_keys.reshape(key_span, head_count, head_dim), 'cuts'...  25.4 us
    all_to_all x1, blocking collectives, per_device(): lax.all_to_all(buffers, 'req', split_axis=0, concat_axis=0, tiled=True)  21 us
    all_to_all x1, waiting for transfers between devices, per_device(): lax.all_to_all(head_out.reshape(cut_count, q_rows, head_dim), 'cuts', spl...  10.6 us
    dot_general x1, matrix products, per_device(): lax.dot_general(act_rows, full_down, (((1,), (1,)), ((), ())), preferred_...  10.1 us
    all_to_all x1, waiting for transfers between devices, per_device(): lax.all_to_all(expert_out, 'req', split_axis=0, concat_axis=0, tiled=True)  9.29 us
    all_to_all x1, starting transfers between devices, per_device(): lax.all_to_all(queries[0].reshape(q_rows, head_count, head_dim), 'cuts',...  8.57 us
    all_to_all x1, waiting for transfers between devices, per_device(): lax.all_to_all(queries[0].reshape(q_rows, head_count, head_dim), 'cuts',...  8.34 us
  transfers between devices with their start and end apart: 8, of which 5 were waited for; matrix products, arithmetic and copies ran while one was open for 14% of the time, Pallas kernels for 38%

profile of v3, /device:TPU:8, one launch (start us, length us, event | category | flops | bytes accessed | tf_op | source)
XLA Modules:
  0.0 296.7 jit_solution(18326845158092786297)
XLA Ops:
  6.5 0.7 all-gather.7.cloned.1.call-update
  7.3 0.7 all-gather.11.cloned.1.call-update
  8.1 0.7 all-gather.9.cloned.1.call-update
  8.7 1.8 copy.89
  10.5 8.6 %all-to-all-start = ((bf16[128,16,64]{0,2,1:T(8,128)(2,1)}), bf16[128,16,64]{0,2,1:T(8,128)(2,1)S(1)}, u32[]{:S(2)}, u32[]{:S(2)}) async-start(bf16[128,16,64]{0,2,1:T(8,128)(2,1)} %bitcast.1), calls=%async_computation | async-start | bytes 524288 | tf_op jit(solution)/shard_map/all_to_all | solution.py:175
  19.1 1.1 copy.92
  20.2 1.2 copy.91
  21.5 1.0 pad_maximum_fusion
  22.5 8.3 %all-to-all-done = bf16[128,16,64]{0,2,1:T(8,128)(2,1)S(1)} async-done(((bf16[128,16,64]{0,2,1:T(8,128)(2,1)}), bf16[128,16,64]{0,2,1:T(8,128)(2,1)S(1)}, u32[]{:S(2)}, u32[]{:S(2)}) %all-to-all-start) | async-done | bytes 262176 | tf_op jit(solution)/shard_map/all_to_all | solution.py:175
  30.8 0.7 copy-done.1
  31.5 4.3 %all-to-all-start.1 = ((bf16[384,16,64]{0,2,1:T(8,128)(2,1)}), bf16[384,16,64]{0,2,1:T(8,128)(2,1)S(1)}, u32[]{:S(2)}, u32[]{:S(2)}) async-start(bf16[384,16,64]{0,2,1:T(8,128)(2,1)} %pad_maximum_fusion), calls=%async_computation.1 | async-start | bytes 1572864 | tf_op jit(solution)/shard_map/all_to_all | solution.py:179
  36.5 0.8 copy.95
  37.3 1.2 copy.94
  38.6 1.9 pad_maximum_fusion.1
  40.5 25.4 %all-to-all-done.1 = bf16[384,16,64]{0,2,1:T(8,128)(2,1)S(1)} async-done(((bf16[384,16,64]{0,2,1:T(8,128)(2,1)}), bf16[384,16,64]{0,2,1:T(8,128)(2,1)S(1)}, u32[]{:S(2)}, u32[]{:S(2)}) %all-to-all-start.1) | async-done | bytes 786464 | tf_op jit(solution)/shard_map/all_to_all | solution.py:179
  65.9 4.5 %all-to-all-start.2 = ((bf16[384,16,64]{0,2,1:T(8,128)(2,1)}), bf16[384,16,64]{0,2,1:T(8,128)(2,1)}, u32[]{:S(2)}, u32[]{:S(2)}) async-start(bf16[384,16,64]{0,2,1:T(8,128)(2,1)} %pad_maximum_fusion.1), calls=%async_computation.2 | async-start | bytes 1572864 | tf_op jit(solution)/shard_map/all_to_all | solution.py:182
  70.5 1.3 convert_add_fusion
  71.8 4.6 %fusion = f32[1,16,16,384]{3,0,2,1:T(1,128)S(1)} fusion(s32[16,16,384]{2,1,0:T(8,128)S(1)} %convert_add_fusion, f32[16,32]{1,0:T(8,128)} %param.21, s32[]{:T(128)S(6)} %select_n.3), kind=kOutput, calls=%fused_computation.1 | convolution fusion | flops 40894464 | bytes 786948 | tf_op jit(solution)/shard_map/agmk,hk->agm/dot_general | solution.py:107
  76.3 0.8 copy.118
  77.1 0.1 subtract_add_fusion
  77.2 0.9 convert_add_fusion.1
  78.1 3.3 %fusion.1 = f32[1,16,16,256]{3,0,2,1:T(1,128)S(1)} fusion(s32[16,16,256]{2,1,0:T(8,128)S(1)} %convert_add_fusion.1, f32[16,32]{1,0:T(8,128)} %param.21, s32[]{:T(128)S(6)} %select_n.3), kind=kOutput, calls=%fused_computation.3 | convolution fusion | flops 27262976 | bytes 524804 | tf_op jit(solution)/shard_map/agmk,hk->agm/dot_general | solution.py:108
  81.4 0.7 copy.119
  82.1 1.0 copy.90
  83.2 1.6 copy.93
  84.7 6.4 %all-to-all-done.2 = bf16[384,16,64]{0,2,1:T(8,128)(2,1)} async-done(((bf16[384,16,64]{0,2,1:T(8,128)(2,1)}), bf16[384,16,64]{0,2,1:T(8,128)(2,1)}, u32[]{:S(2)}, u32[]{:S(2)}) %all-to-all-start.2) | async-done | bytes 786464 | tf_op jit(solution)/shard_map/all_to_all | solution.py:182
  91.1 2.4 copy.96
  93.5 111.7 %shard_map.145 = bf16[2048,64]{1,0:T(8,128)(2,1)} custom-call(s32[1]{0:T(128)} %copy.120.scalars, bf16[2048,64]{1,0:T(8,128)(2,1)} %bitcast.96, bf16[16,384,64]{2,1,0:T(8,128)(2,1)} %bitcast.90, bf16[16,384,64]{2,1,0:T(8,128)(2,1)} %bitcast.91, f32[16,16,384]{2,1,0:T(8,128)} %bitcast.98, f32[16,16,256]{2,1,0:T(8,128)} %bitcast.99), custom_call_target="tpu_custom_call" | custom-call | flops 3221225472 | bytes 9961472 | tf_op jit(solution)/shard_map/pallas_call | solution.py:134
  205.2 1.9 copy.97
  207.1 6.5 %all-to-all-start.3 = ((bf16[16,128,64]{1,2,0:T(8,128)(2,1)}), bf16[16,128,64]{1,2,0:T(8,128)(2,1)S(1)}, u32[]{:S(2)}, u32[]{:S(2)}) async-start(bf16[16,128,64]{1,2,0:T(8,128)(2,1)} %copy.97), calls=%async_computation.3 | async-start | bytes 524288 | tf_op jit(solution)/shard_map/all_to_all | solution.py:189
  213.7 0.1 copy.98
  213.8 0.3 convert_reduce_fusion
  214.1 0.1 fusion.106
  214.2 10.6 %all-to-all-done.3 = bf16[16,128,64]{1,2,0:T(8,128)(2,1)S(1)} async-done(((bf16[16,128,64]{1,2,0:T(8,128)(2,1)}), bf16[16,128,64]{1,2,0:T(8,128)(2,1)S(1)}, u32[]{:S(2)}, u32[]{:S(2)}) %all-to-all-start.3) | async-done | bytes 262176 | tf_op jit(solution)/shard_map/all_to_all | solution.py:189
  224.8 0.5 multiply_reduce_fusion
  225.4 0.3 fusion.109
  225.7 0.5 select_reduce_fusion
  226.2 0.8 fusion.28
  227.0 0.5 convolution_convert_fusion
  227.5 21.0 %all_to_all.60 = bf16[16,20,1024]{2,1,0:T(8,128)(2,1)S(1)} all-to-all(bf16[16,20,1024]{2,1,0:T(8,128)(2,1)S(1)} %convolution_convert_fusion), channel_id=1, replica_groups=mesh['req'=16,'cuts'=16] {'req'}, dimensions={0} | all-to-all | bytes 1310720 | tf_op jit(solution)/shard_map/all_to_all | solution.py:218
  248.5 1.0 reshape.333
  249.4 7.5 %fusion.22 = f32[320,2816]{1,0:T(8,128)} fusion(bf16[320,1024]{1,0:T(8,128)(2,1)} %reshape.333, bf16[1,1024,2816]{1,2,0:T(8,128)(2,1)} %all-gather.7.cloned.1.call-done), kind=kOutput, calls=%fused_computation.21 | convolution fusion | flops 1852702720 | bytes 10027008 | tf_op jit(solution)/shard_map/dot_general | solution.py:223
  257.0 10.1 %fusion.25 = bf16[320,1024]{1,0:T(8,128)(2,1)} fusion(bf16[1,1024,2816]{1,2,0:T(8,128)(2,1)} %all-gather.11.cloned.1.call-done, f32[320,2816]{1,0:T(8,128)} %fusion.22, bf16[320,1024]{1,0:T(8,128)(2,1)S(1)} %copy-done.3, bf16[1,1024,2816]{1,2,0:T(8,128)(2,1)} %all-gather.9.cloned.1.call-done), kind=kOutput, calls=%fused_computation.24 | convolution fusion | flops 3693117440 | bytes 16449536 | tf_op jit(solution)/shard_map/dot_general | solution.py:226
  267.1 2.0 reshape.334
  269.1 5.2 %all-to-all-start.5 = ((bf16[16,20,1024]{2,1,0:T(8,128)(2,1)}), bf16[16,20,1024]{2,1,0:T(8,128)(2,1)S(1)}, u32[]{:S(2)}, u32[]{:S(2)}) async-start(bf16[16,20,1024]{2,1,0:T(8,128)(2,1)} %reshape.334), calls=%async_computation.5 | async-start | bytes 1572864 | tf_op jit(solution)/shard_map/all_to_all | solution.py:229
  274.4 3.3 %convolution_bitcast_fusion = f32[16,20,128]{1,0,2:T(8,128)} fusion(f32[128,2]{1,0:T(8,128)S(1)} %add_divide_fusion, f32[128,2]{1,0:T(8,128)} %copy-done.6, s32[128,2]{1,0:T(8,128)S(1)} %copy.98), kind=kOutput, calls=%fused_computation.23 | convolution fusion | flops 997376 | bytes 166912 | tf_op jit(solution)/shard_map/tke,tkc,tk->ect/dot_general | solution.py:230
  277.7 9.3 %all-to-all-done.5 = bf16[16,20,1024]{2,1,0:T(8,128)(2,1)S(1)} async-done(((bf16[16,20,1024]{2,1,0:T(8,128)(2,1)}), bf16[16,20,1024]{2,1,0:T(8,128)(2,1)S(1)}, u32[]{:S(2)}, u32[]{:S(2)}) %all-to-all-start.5) | async-done | bytes 655392 | tf_op jit(solution)/shard_map/all_to_all | solution.py:229
  287.0 3.2 %fusion.31 = bf16[1,128,1024]{2,1,0:T(8,128)(2,1)} fusion(f32[128,1024]{1,0:T(8,128)S(1)} %get-tuple-element.8, bf16[16,20,1024]{2,1,0:T(8,128)(2,1)S(1)} %all-to-all-done.5, f32[16,20,128]{1,0,2:T(8,128)} %convolution_bitcast_fusion), kind=kOutput, calls=%fused_computation.31 | convolution fusion | flops 503578624 | bytes 1605632 | tf_op jit(solution)/shard_map/ect,ecd->td/dot_general | solution.py:233
  (31 shorter events, 0.2 us)
Async XLA Ops:
  6.5 218.3 %copy-start = (bf16[1024,1024]{1,0:T(8,128)(2,1)S(1)}, bf16[1024,1024]{1,0:T(8,128)(2,1)}, u32[]{:S(2)}) copy-start(bf16[1024,1024]{1,0:T(8,128)(2,1)} %param.23) | copy-start | bytes 6291460
  6.5 29.9 %copy-start.4 = (bf16[1,128,1024]{2,1,0:T(8,128)(2,1)S(1)}, bf16[1,128,1024]{2,1,0:T(8,128)(2,1)}, u32[]{:S(2)}) copy-start(bf16[1,128,1024]{2,1,0:T(8,128)(2,1)} %param.17) | copy-start | bytes 786436
  6.5 242.9 %all-gather.7.cloned.1.call-start = ((), (), s32[]{:S(2)}) async-start(), calls=%async_computation.6 | async-start | bytes 6127616 | tf_op jit(solution)/shard_map/all_gather | solution.py:219
  7.3 249.7 %all-gather.11.cloned.1.call-start = ((), (), s32[]{:S(2)}) async-start(), calls=%async_computation.8 | async-start | bytes 6127616 | tf_op jit(solution)/shard_map/all_gather | solution.py:221
  8.0 249.0 %all-gather.9.cloned.1.call-start = ((), (), s32[]{:S(2)}) async-start(), calls=%async_computation.7 | async-start | bytes 6127616 | tf_op jit(solution)/shard_map/all_gather | solution.py:220
  10.5 20.3 %all-to-all-start = ((bf16[128,16,64]{0,2,1:T(8,128)(2,1)}), bf16[128,16,64]{0,2,1:T(8,128)(2,1)S(1)}, u32[]{:S(2)}, u32[]{:S(2)}) async-start(bf16[128,16,64]{0,2,1:T(8,128)(2,1)} %bitcast.1), calls=%async_computation | async-start | bytes 524288 | tf_op jit(solution)/shard_map/all_to_all | solution.py:175
  30.8 0.7 copy-start.1
  31.5 34.3 %all-to-all-start.1 = ((bf16[384,16,64]{0,2,1:T(8,128)(2,1)}), bf16[384,16,64]{0,2,1:T(8,128)(2,1)S(1)}, u32[]{:S(2)}, u32[]{:S(2)}) async-start(bf16[384,16,64]{0,2,1:T(8,128)(2,1)} %pad_maximum_fusion), calls=%async_computation.1 | async-start | bytes 1572864 | tf_op jit(solution)/shard_map/all_to_all | solution.py:179
  65.9 25.2 %all-to-all-start.2 = ((bf16[384,16,64]{0,2,1:T(8,128)(2,1)}), bf16[384,16,64]{0,2,1:T(8,128)(2,1)}, u32[]{:S(2)}, u32[]{:S(2)}) async-start(bf16[384,16,64]{0,2,1:T(8,128)(2,1)} %pad_maximum_fusion.1), calls=%async_computation.2 | async-start | bytes 1572864 | tf_op jit(solution)/shard_map/all_to_all | solution.py:182
  70.4 11.7 %copy-start.2 = (bf16[128,16,64]{0,2,1:T(8,128)(2,1)S(1)}, bf16[128,16,64]{0,2,1:T(8,128)(2,1)}, u32[]{:S(2)}) copy-start(bf16[128,16,64]{0,2,1:T(8,128)(2,1)} %copy-done.1) | copy-start | bytes 786436
  93.5 120.2 %copy-start.8 = (bf16[1024]{0:T(1024)(128)(2,1)S(1)}, bf16[1024]{0:T(1024)(128)(2,1)}, u32[]{:S(2)}) copy-start(bf16[1024]{0:T(1024)(128)(2,1)} %param.24) | copy-start | bytes 6148
  93.5 120.2 %copy-start.9 = (s32[1,128,2]{1,2,0:T(2,128)S(1)}, s32[1,128,2]{1,2,0:T(2,128)}, u32[]{:S(2)}) copy-start(s32[1,128,2]{1,2,0:T(2,128)} %param.26) | copy-start | bytes 3076
  93.5 131.3 %copy-start.5 = (bf16[1,128,1024]{2,1,0:T(8,128)(2,1)S(1)}, bf16[1,128,1024]{2,1,0:T(8,128)(2,1)}, u32[]{:S(2)}) copy-start(bf16[1,128,1024]{2,1,0:T(8,128)(2,1)} %param.22) | copy-start | bytes 786436
  205.2 20.2 %copy-start.7 = (bf16[1024,16]{0,1:T(8,128)(2,1)S(1)}, bf16[1024,16]{0,1:T(8,128)(2,1)}, u32[]{:S(2)}) copy-start(bf16[1024,16]{0,1:T(8,128)(2,1)} %param.25) | copy-start | bytes 98308
  207.1 17.7 %all-to-all-start.3 = ((bf16[16,128,64]{1,2,0:T(8,128)(2,1)}), bf16[16,128,64]{1,2,0:T(8,128)(2,1)S(1)}, u32[]{:S(2)}, u32[]{:S(2)}) async-start(bf16[16,128,64]{1,2,0:T(8,128)(2,1)} %copy.97), calls=%async_computation.3 | async-start | bytes 524288 | tf_op jit(solution)/shard_map/all_to_all | solution.py:189
  226.2 0.8 copy-start.6
  249.4 7.5 %copy-start.3 = (bf16[320,1024]{1,0:T(8,128)(2,1)S(1)}, bf16[320,1024]{1,0:T(8,128)(2,1)}, u32[]{:S(2)}) copy-start(bf16[320,1024]{1,0:T(8,128)(2,1)} %reshape.333) | copy-start | bytes 1966084
  269.1 17.8 %all-to-all-start.5 = ((bf16[16,20,1024]{2,1,0:T(8,128)(2,1)}), bf16[16,20,1024]{2,1,0:T(8,128)(2,1)S(1)}, u32[]{:S(2)}, u32[]{:S(2)}) async-start(bf16[16,20,1024]{2,1,0:T(8,128)(2,1)} %reshape.334), calls=%async_computation.5 | async-start | bytes 1572864 | tf_op jit(solution)/shard_map/all_to_all | solution.py:229
Sparse Core Ops, SparseCore 0:
  9.2 65.8 all-gather.6
  76.9 43.8 all-gather.10
  122.6 43.2 all-gather.8

commit v4 on v3

--- a/solution.py
+++ b/solution.py
@@ -42,36 +42,30 @@
     return bucket_level
 
 
-def attention_kernel(scalars, q_ref, k_ref, v_ref, tc_ref, tn_ref, o_ref):
-    length = scalars[0]
-    block = pl.program_id(0)
+def attention_kernel(scalars, q_ref, k_ref, v_ref, tc_ref, tn_ref, live_ref, o_ref):
     q_rows = q_ref.shape[0]
     key_blocks, key_span, head_dim = k_ref.shape
     cache_rows = tc_ref.shape[2] - q_rows
     new_rows = key_span - cache_rows
-    row = lax.broadcasted_iota(jnp.int32, (q_rows, key_span), 0)
-    col = lax.broadcasted_iota(jnp.int32, (q_rows, key_span), 1)
-    is_cache = col < cache_rows
     cache_width = tc_ref.shape[2]
     new_width = tn_ref.shape[2]
     query = q_ref[...]
 
     def one_block(g, carry):
         best, weighted, factor_sum = carry
-        cache_live = g * cache_rows + col < length
-        new_live = g * new_rows + (col - cache_rows) <= block * q_rows + row
-        visible = (is_cache & cache_live) | (jnp.logical_not(is_cache) & new_live)
         scores = lax.dot_general(
             query, k_ref[g], (((1,), (1,)), ((), ())), preferred_element_type=jnp.float32
-        ) / 8.0
+        )
         cache_table = jnp.broadcast_to(tc_ref[0, pl.ds(g, 1), :], (q_rows, cache_width))
         cache_bias = pltpu.roll(cache_table, cache_width - q_rows, 1, stride=1, stride_axis=0)
         new_table = jnp.broadcast_to(tn_ref[0, pl.ds(g, 1), :], (q_rows, new_width))
         new_bias = pltpu.roll(new_table, new_width - q_rows, 1, stride=1, stride_axis=0)
-        bias = jnp.concatenate([cache_bias[:, :cache_rows], new_bias[:, :new_rows]], axis=1)
-        masked = jnp.where(visible, scores + bias, -1e30)
+        bias = jnp.concatenate(
+            [cache_bias[:, :cache_rows] + live_ref[pl.ds(g, 1), :], new_bias[:, :new_rows]], axis=1
+        )
+        masked = scores + bias
         peak = jnp.max(masked, axis=1, keepdims=True)
-        weights = jnp.where(visible, jnp.exp(masked - peak), 0.0)
+        weights = jnp.exp(masked - peak)
         total = jnp.sum(weights, axis=1, keepdims=True)
         numerator = jnp.dot(
             weights.astype(jnp.bfloat16), v_ref[g], preferred_element_type=jnp.float32
@@ -106,7 +100,10 @@
     new_hot = (new_bucket[..., None] == choices).astype(jnp.float32)
     cache_table = jnp.einsum("agmk,hk->agm", cache_hot, head_table, precision=lax.Precision.HIGHEST)
     new_table = jnp.einsum("agmk,hk->agm", new_hot, head_table, precision=lax.Precision.HIGHEST)
-    return cache_table, new_table
+    new_table = jnp.where(new_distance >= 0, new_table, -1e30)
+    cache_slots = key_ids[0] * cache_rows + jnp.arange(cache_rows, dtype=jnp.int32)[None, :]
+    live = jnp.where(cache_slots < length, 0.0, -1e30).astype(jnp.float32)
+    return cache_table, new_table, live
 
 
 def block_partials(query_rows, key_rows, value_rows, head_table, length, cache_rows, q_rows):
@@ -114,7 +111,7 @@
     new_rows = key_span - cache_rows
     query_total = query_rows.shape[0]
     query_blocks = query_total // q_rows
-    cache_table, new_table = bias_tables(
+    cache_table, new_table, live = bias_tables(
         head_table, length, q_rows, cache_rows, new_rows, query_blocks, key_blocks
     )
     scalars = jnp.stack([length]).astype(jnp.int32)
@@ -127,6 +124,7 @@
             pl.BlockSpec((key_blocks, key_span, head_dim), lambda b, s: (0, 0, 0)),
             pl.BlockSpec((1, key_blocks, cache_table.shape[2]), lambda b, s: (b, 0, 0)),
             pl.BlockSpec((1, key_blocks, new_table.shape[2]), lambda b, s: (b, 0, 0)),
+            pl.BlockSpec(live.shape, lambda b, s: (0, 0)),
         ],
         out_specs=pl.BlockSpec((q_rows, head_dim), lambda b, s: (b, 0)),
     )
@@ -140,7 +138,7 @@
             transcendentals=pairs,
             bytes_accessed=4 * query_total * head_dim * key_blocks + 4 * key_span * key_blocks * head_dim,
         ),
-    )(scalars, query_rows, key_rows, value_rows, cache_table, new_table)
+    )(scalars, query_rows, key_rows, value_rows, cache_table, new_table, live)
 
 
 def per_device(
@@ -172,16 +170,16 @@
     query_total = q_rows * cut_count
     local_keys = jnp.concatenate([cache_keys[0], new_keys[0]], axis=0)
     local_values = jnp.concatenate([cache_values[0], new_values[0]], axis=0)
-    head_queries = lax.all_to_all(
-        queries[0].reshape(q_rows, head_count, head_dim), "cuts", split_axis=1, concat_axis=0, tiled=True
-    ).reshape(query_total, head_dim)
     key_span = local_keys.shape[0]
-    head_keys = lax.all_to_all(
-        local_keys.reshape(key_span, head_count, head_dim), "cuts", split_axis=1, concat_axis=0, tiled=True
-    ).reshape(cut_count, key_span, head_dim)
-    head_values = lax.all_to_all(
-        local_values.reshape(key_span, head_count, head_dim), "cuts", split_axis=1, concat_axis=0, tiled=True
-    ).reshape(cut_count, key_span, head_dim)
+    packed = jnp.concatenate(
+        [queries[0] * jnp.asarray(0.125, queries.dtype), local_keys, local_values], axis=0
+    )
+    packed = lax.all_to_all(
+        packed.reshape(packed.shape[0], head_count, head_dim), "cuts", split_axis=1, concat_axis=0, tiled=True
+    ).reshape(cut_count, packed.shape[0], head_dim)
+    head_queries = packed[:, :q_rows].reshape(query_total, head_dim)
+    head_keys = packed[:, q_rows:q_rows + key_span]
+    head_values = packed[:, q_rows + key_span:]
     head_table = lax.dynamic_slice_in_dim(relative_bias, cut_index, 1, 0)
     head_out = block_partials(
         head_queries, head_keys, head_values, head_table, length, cache_rows, q_rows

time: 298 us -> 304 us (1.020)
  local copies, waits for them, and re-layouts: 18.6 us -> 28.5 us
  starting transfers between devices: 29.2 us -> 20.3 us
  waiting for transfers between devices: 62 us -> 69 us
    all_to_all x3 -> x1, starting transfers between devices: 17.4 us -> 8.61 us  [per_device(): lax.all_to_all(packed.reshape(packed.shape[0], head_count, head_dim), 'cu...]
    all_to_all x3 -> x1, waiting for transfers between devices: 40.1 us -> 47 us  [per_device(): lax.all_to_all(packed.reshape(packed.shape[0], head_count, head_dim), 'cu...]
    slice x0 -> x2, local copies, waits for them, and re-layouts: none -> 5.8 us  [the longest x1 3.91 us: per_device(): head_values = packed[:, q_rows + key_span:]]
    unnamed x25 -> x23, local copies, waits for them, and re-layouts: 6.98 us -> 11.4 us
  transfers between devices with their start and end apart: 8 -> 6, of which waited for: 5 -> 3; matrix products, arithmetic and copies ran while one was open for 14% -> 17% of each run, Pallas kernels for 38% -> 37%
where the time goes in v4:
time: 304 us; the launch traced here: 303 us
  Pallas kernels  111 us (37%)
  waiting for transfers between devices  69 us (23%)
  matrix products  34.2 us (11%)
  local copies, waits for them, and re-layouts  28.5 us (9%)
  blocking collectives  20.7 us (7%)
  starting transfers between devices  20.3 us (7%)
  between operations  13.9 us (5%)
  other arithmetic  5.6 us (2%)
    pallas_call x1, Pallas kernels, block_partials(): pl.pallas_call(attention_kernel, grid_spec=grid_spec, out_shape=jax.Shape...  111 us
    all_to_all x1, waiting for transfers between devices, per_device(): lax.all_to_all(packed.reshape(packed.shape[0], head_count, head_dim), 'cu...  47 us
    all_to_all x1, blocking collectives, per_device(): lax.all_to_all(buffers, 'req', split_axis=0, concat_axis=0, tiled=True)  20.7 us
    unnamed x23, local copies, waits for them, and re-layouts  11.4 us
    all_to_all x1, waiting for transfers between devices, per_device(): lax.all_to_all(head_out.reshape(cut_count, q_rows, head_dim), 'cuts', spl...  10.6 us
    dot_general x1, matrix products, per_device(): lax.dot_general(act_rows, full_down, (((1,), (1,)), ((), ())), preferred_...  10.1 us
    all_to_all x1, waiting for transfers between devices, per_device(): lax.all_to_all(expert_out, 'req', split_axis=0, concat_axis=0, tiled=True)  9.29 us
    all_to_all x1, starting transfers between devices, per_device(): lax.all_to_all(packed.reshape(packed.shape[0], head_count, head_dim), 'cu...  8.61 us
  transfers between devices with their start and end apart: 6, of which 3 were waited for; matrix products, arithmetic and copies ran while one was open for 17% of the time, Pallas kernels for 37%

profile of v4, /device:TPU:8, one launch (start us, length us, event | category | flops | bytes accessed | tf_op | source)
XLA Modules:
  0.0 303.0 jit_solution(5874671754404525670)
XLA Ops:
  6.5 0.7 all-gather.7.cloned.1.call-update
  7.3 0.7 all-gather.11.cloned.1.call-update
  8.1 0.7 all-gather.9.cloned.1.call-update
  8.7 1.8 copy.80
  10.5 1.2 copy.81
  11.8 1.8 copy.82
  13.6 1.2 copy.83
  14.8 1.1 copy.84
  16.0 1.0 broadcast_multiply_fusion
  16.9 0.7 constant_dynamic-update-slice_fusion.4
  17.7 0.9 constant_dynamic-update-slice_fusion.3
  18.6 1.7 constant_dynamic-update-slice_fusion.2
  20.3 0.9 constant_dynamic-update-slice_fusion.1
  21.1 0.7 constant_dynamic-update-slice_fusion
  21.9 8.6 %all-to-all-start = ((bf16[896,16,64]{0,2,1:T(8,128)(2,1)}), bf16[896,16,64]{0,2,1:T(8,128)(2,1)}, u32[]{:S(2)}, u32[]{:S(2)}) async-start(bf16[896,16,64]{0,2,1:T(8,128)(2,1)} %constant_dynamic-update-slice_fusion), calls=%async_computation | async-start | bytes 3670016 | tf_op jit(solution)/shard_map/all_to_all | solution.py:177
  31.2 1.3 convert_add_fusion
  32.5 4.6 %fusion = f32[1,16,16,384]{3,0,2,1:T(1,128)S(1)} fusion(s32[16,16,384]{2,1,0:T(8,128)S(1)} %convert_add_fusion, f32[16,32]{1,0:T(8,128)} %param.21, s32[]{:T(128)S(6)} %select_n.11), kind=kOutput, calls=%fused_computation.1 | convolution fusion | flops 40894464 | bytes 786948 | tf_op jit(solution)/shard_map/agmk,hk->agm/dot_general | solution.py:101
  37.1 0.8 copy.107
  37.9 0.1 subtract_add_fusion
  38.0 0.7 fusion.110.live_ref
  38.7 0.9 convert_add_fusion.1
  39.5 3.3 %fusion.1 = f32[1,16,16,256]{3,0,2,1:T(1,128)S(1)} fusion(s32[16,16,256]{2,1,0:T(8,128)S(1)} %convert_add_fusion.1, f32[16,32]{1,0:T(8,128)} %param.21, s32[]{:T(128)S(6)} %select_n.11), kind=kOutput, calls=%fused_computation.3 | convolution fusion | flops 27262976 | bytes 524804 | tf_op jit(solution)/shard_map/agmk,hk->agm/dot_general | solution.py:102
  42.9 0.8 bitcast_select_fusion.tn_ref
  43.7 47.0 %all-to-all-done = bf16[896,16,64]{0,2,1:T(8,128)(2,1)} async-done(((bf16[896,16,64]{0,2,1:T(8,128)(2,1)}), bf16[896,16,64]{0,2,1:T(8,128)(2,1)}, u32[]{:S(2)}, u32[]{:S(2)}) %all-to-all-start) | async-done | bytes 1835040 | tf_op jit(solution)/shard_map/all_to_all | solution.py:177
  90.7 4.6 %copy.85 = bf16[896,16,64]{2,0,1:T(8,128)(2,1)} copy(bf16[896,16,64]{0,2,1:T(8,128)(2,1)} %all-to-all-done) | data formatting | bytes 3670016 | tf_op jit(solution)/shard_map/all_to_all | solution.py:177
  95.2 1.9 slice.12
  97.1 3.9 %fusion.113 = (bf16[16,384,64]{2,1,0:T(8,128)(2,1)}, bf16[16,384,64]{2,1,0:T(8,128)(2,1)}) fusion(bf16[16,896,64]{2,1,0:T(8,128)(2,1)} %bitcast.81), kind=kLoop, calls=%fused_computation.140 | loop fusion | bytes 3145728 | tf_op jit(solution)/shard_map/slice | solution.py:182
  101.0 110.8 %shard_map.145 = bf16[2048,64]{1,0:T(8,128)(2,1)} custom-call(s32[1]{0:T(128)} %copy.112.scalars, bf16[2048,64]{1,0:T(8,128)(2,1)} %bitcast.89, bf16[16,384,64]{2,1,0:T(8,128)(2,1)} %get-tuple-element.8.k_ref, bf16[16,384,64]{2,1,0:T(8,128)(2,1)} %get-tuple-element.7.v_ref, f32[16,16,384]{2,1,0:T(8,128)} %bitcast.90, ...), custom_call_target="tpu_custom_call" | custom-call | flops 3221225472 | bytes 9961472 | tf_op jit(solution)/shard_map/pallas_call | solution.py:132
  211.8 1.9 copy.86
  213.8 6.4 %all-to-all-start.1 = ((bf16[16,128,64]{1,2,0:T(8,128)(2,1)}), bf16[16,128,64]{1,2,0:T(8,128)(2,1)S(1)}, u32[]{:S(2)}, u32[]{:S(2)}) async-start(bf16[16,128,64]{1,2,0:T(8,128)(2,1)} %copy.86), calls=%async_computation.1 | async-start | bytes 524288 | tf_op jit(solution)/shard_map/all_to_all | solution.py:187
  220.2 0.1 copy.87
  220.3 0.3 convert_reduce_fusion
  220.6 0.1 fusion.108
  220.8 10.6 %all-to-all-done.1 = bf16[16,128,64]{1,2,0:T(8,128)(2,1)S(1)} async-done(((bf16[16,128,64]{1,2,0:T(8,128)(2,1)}), bf16[16,128,64]{1,2,0:T(8,128)(2,1)S(1)}, u32[]{:S(2)}, u32[]{:S(2)}) %all-to-all-start.1) | async-done | bytes 262176 | tf_op jit(solution)/shard_map/all_to_all | solution.py:187
  231.3 0.5 multiply_reduce_fusion
  231.9 0.3 fusion.112
  232.2 0.5 select_reduce_fusion
  232.7 0.8 fusion.28
  233.5 0.5 convolution_convert_fusion
  234.0 20.7 %all_to_all.30 = bf16[16,20,1024]{2,1,0:T(8,128)(2,1)S(1)} all-to-all(bf16[16,20,1024]{2,1,0:T(8,128)(2,1)S(1)} %convolution_convert_fusion), channel_id=1, replica_groups=mesh['req'=16,'cuts'=16] {'req'}, dimensions={0} | all-to-all | bytes 1310720 | tf_op jit(solution)/shard_map/all_to_all | solution.py:216
  254.7 1.0 reshape.335
  255.6 7.5 %fusion.22 = f32[320,2816]{1,0:T(8,128)} fusion(bf16[320,1024]{1,0:T(8,128)(2,1)} %reshape.335, bf16[1,1024,2816]{1,2,0:T(8,128)(2,1)} %all-gather.7.cloned.1.call-done), kind=kOutput, calls=%fused_computation.21 | convolution fusion | flops 1852702720 | bytes 10027008 | tf_op jit(solution)/shard_map/dot_general | solution.py:221
  263.1 10.1 %fusion.25 = bf16[320,1024]{1,0:T(8,128)(2,1)} fusion(bf16[1,1024,2816]{1,2,0:T(8,128)(2,1)} %all-gather.11.cloned.1.call-done, f32[320,2816]{1,0:T(8,128)} %fusion.22, bf16[320,1024]{1,0:T(8,128)(2,1)S(1)} %copy-done.1, bf16[1,1024,2816]{1,2,0:T(8,128)(2,1)} %all-gather.9.cloned.1.call-done), kind=kOutput, calls=%fused_computation.24 | convolution fusion | flops 3693117440 | bytes 16449536 | tf_op jit(solution)/shard_map/dot_general | solution.py:224
  273.3 2.1 reshape.336
  275.4 5.2 %all-to-all-start.3 = ((bf16[16,20,1024]{2,1,0:T(8,128)(2,1)}), bf16[16,20,1024]{2,1,0:T(8,128)(2,1)S(1)}, u32[]{:S(2)}, u32[]{:S(2)}) async-start(bf16[16,20,1024]{2,1,0:T(8,128)(2,1)} %reshape.336), calls=%async_computation.3 | async-start | bytes 1572864 | tf_op jit(solution)/shard_map/all_to_all | solution.py:227
  280.6 3.3 %convolution_bitcast_fusion = f32[16,20,128]{1,0,2:T(8,128)} fusion(f32[128,2]{1,0:T(8,128)S(1)} %add_divide_fusion, f32[128,2]{1,0:T(8,128)} %copy-done.3, s32[128,2]{1,0:T(8,128)S(1)} %copy.87), kind=kOutput, calls=%fused_computation.23 | convolution fusion | flops 997376 | bytes 166912 | tf_op jit(solution)/shard_map/tke,tkc,tk->ect/dot_general | solution.py:228
  283.9 9.3 %all-to-all-done.3 = bf16[16,20,1024]{2,1,0:T(8,128)(2,1)S(1)} async-done(((bf16[16,20,1024]{2,1,0:T(8,128)(2,1)}), bf16[16,20,1024]{2,1,0:T(8,128)(2,1)S(1)}, u32[]{:S(2)}, u32[]{:S(2)}) %all-to-all-start.3) | async-done | bytes 655392 | tf_op jit(solution)/shard_map/all_to_all | solution.py:227
  293.2 3.2 %fusion.31 = bf16[1,128,1024]{2,1,0:T(8,128)(2,1)} fusion(f32[128,1024]{1,0:T(8,128)S(1)} %get-tuple-element.10, bf16[16,20,1024]{2,1,0:T(8,128)(2,1)S(1)} %all-to-all-done.3, f32[16,20,128]{1,0,2:T(8,128)} %convolution_bitcast_fusion), kind=kOutput, calls=%fused_computation.31 | convolution fusion | flops 503578624 | bytes 1605632 | tf_op jit(solution)/shard_map/ect,ecd->td/dot_general | solution.py:231
  (26 shorter events, 0.2 us)
Async XLA Ops:
  6.5 224.8 %copy-start = (bf16[1024,1024]{1,0:T(8,128)(2,1)S(1)}, bf16[1024,1024]{1,0:T(8,128)(2,1)}, u32[]{:S(2)}) copy-start(bf16[1024,1024]{1,0:T(8,128)(2,1)} %param.23) | copy-start | bytes 6291460
  6.5 249.1 %all-gather.7.cloned.1.call-start = ((), (), s32[]{:S(2)}) async-start(), calls=%async_computation.4 | async-start | bytes 6127616 | tf_op jit(solution)/shard_map/all_gather | solution.py:217
  7.3 255.9 %all-gather.11.cloned.1.call-start = ((), (), s32[]{:S(2)}) async-start(), calls=%async_computation.6 | async-start | bytes 6127616 | tf_op jit(solution)/shard_map/all_gather | solution.py:219
  8.0 255.1 %all-gather.9.cloned.1.call-start = ((), (), s32[]{:S(2)}) async-start(), calls=%async_computation.5 | async-start | bytes 6127616 | tf_op jit(solution)/shard_map/all_gather | solution.py:218
  21.9 68.8 %all-to-all-start = ((bf16[896,16,64]{0,2,1:T(8,128)(2,1)}), bf16[896,16,64]{0,2,1:T(8,128)(2,1)}, u32[]{:S(2)}, u32[]{:S(2)}) async-start(bf16[896,16,64]{0,2,1:T(8,128)(2,1)} %constant_dynamic-update-slice_fusion), calls=%async_computation | async-start | bytes 3670016 | tf_op jit(solution)/shard_map/all_to_all | solution.py:177
  101.0 119.2 %copy-start.5 = (bf16[1024]{0:T(1024)(128)(2,1)S(1)}, bf16[1024]{0:T(1024)(128)(2,1)}, u32[]{:S(2)}) copy-start(bf16[1024]{0:T(1024)(128)(2,1)} %param.24) | copy-start | bytes 6148
  101.0 119.2 %copy-start.6 = (s32[1,128,2]{1,2,0:T(2,128)S(1)}, s32[1,128,2]{1,2,0:T(2,128)}, u32[]{:S(2)}) copy-start(s32[1,128,2]{1,2,0:T(2,128)} %param.26) | copy-start | bytes 3076
  101.0 130.3 %copy-start.2 = (bf16[1,128,1024]{2,1,0:T(8,128)(2,1)S(1)}, bf16[1,128,1024]{2,1,0:T(8,128)(2,1)}, u32[]{:S(2)}) copy-start(bf16[1,128,1024]{2,1,0:T(8,128)(2,1)} %param.22) | copy-start | bytes 786436
  211.8 20.1 %copy-start.4 = (bf16[1024,16]{0,1:T(8,128)(2,1)S(1)}, bf16[1024,16]{0,1:T(8,128)(2,1)}, u32[]{:S(2)}) copy-start(bf16[1024,16]{0,1:T(8,128)(2,1)} %param.25) | copy-start | bytes 98308
  213.8 17.6 %all-to-all-start.1 = ((bf16[16,128,64]{1,2,0:T(8,128)(2,1)}), bf16[16,128,64]{1,2,0:T(8,128)(2,1)S(1)}, u32[]{:S(2)}, u32[]{:S(2)}) async-start(bf16[16,128,64]{1,2,0:T(8,128)(2,1)} %copy.86), calls=%async_computation.1 | async-start | bytes 524288 | tf_op jit(solution)/shard_map/all_to_all | solution.py:187
  232.7 0.8 copy-start.3
  255.6 7.5 %copy-start.1 = (bf16[320,1024]{1,0:T(8,128)(2,1)S(1)}, bf16[320,1024]{1,0:T(8,128)(2,1)}, u32[]{:S(2)}) copy-start(bf16[320,1024]{1,0:T(8,128)(2,1)} %reshape.335) | copy-start | bytes 1966084
  275.4 17.8 %all-to-all-start.3 = ((bf16[16,20,1024]{2,1,0:T(8,128)(2,1)}), bf16[16,20,1024]{2,1,0:T(8,128)(2,1)S(1)}, u32[]{:S(2)}, u32[]{:S(2)}) async-start(bf16[16,20,1024]{2,1,0:T(8,128)(2,1)} %reshape.336), calls=%async_computation.3 | async-start | bytes 1572864 | tf_op jit(solution)/shard_map/all_to_all | solution.py:227
Sparse Core Ops, SparseCore 0:
  9.2 85.6 all-gather.6
  96.7 43.1 all-gather.10
  141.7 42.9 all-gather.8

commit v5 on v4

--- a/solution.py
+++ b/solution.py
@@ -81,7 +81,7 @@
         jnp.zeros((q_rows, head_dim), jnp.float32),
         jnp.zeros((q_rows, 1), jnp.float32),
     )
-    best, weighted, factor_sum = lax.fori_loop(0, key_blocks, one_block, start)
+    best, weighted, factor_sum = lax.fori_loop(0, key_blocks, one_block, start, unroll=2)
     o_ref[...] = (weighted / factor_sum).astype(o_ref.dtype)
 
 
@@ -107,6 +107,7 @@
 
 
 def block_partials(query_rows, key_rows, value_rows, head_table, length, cache_rows, q_rows):
+    q_rows = 2 * q_rows
     key_blocks, key_span, head_dim = key_rows.shape
     new_rows = key_span - cache_rows
     query_total = query_rows.shape[0]

time: 304 us -> 268 us (0.88)
  Pallas kernels: 111 us -> 74.5 us
    pallas_call x1, Pallas kernels: 111 us -> 74.5 us  [block_partials(): pl.pallas_call(attention_kernel, grid_spec=grid_spec, out_shape=jax.Shape...]
  transfers between devices with their start and end apart: 6 -> 6, of which waited for: 3 -> 3; matrix products, arithmetic and copies ran while one was open for 17% -> 19% of each run, Pallas kernels for 37% -> 28%
where the time goes in v5:
time: 268 us; the launch traced here: 267 us
  Pallas kernels  74.5 us (28%)
  waiting for transfers between devices  71.5 us (27%)
  matrix products  32.3 us (12%)
  local copies, waits for them, and re-layouts  28.3 us (11%)
  blocking collectives  20.6 us (8%)
  starting transfers between devices  20.4 us (8%)
  between operations  13.9 us (5%)
  other arithmetic  4.95 us (2%)
    pallas_call x1, Pallas kernels, block_partials(): pl.pallas_call(attention_kernel, grid_spec=grid_spec, out_shape=jax.Shape...  74.5 us
    all_to_all x1, waiting for transfers between devices, per_device(): lax.all_to_all(packed.reshape(packed.shape[0], head_count, head_dim), 'cu...  49.6 us
    all_to_all x1, blocking collectives, per_device(): lax.all_to_all(buffers, 'req', split_axis=0, concat_axis=0, tiled=True)  20.6 us
    unnamed x23, local copies, waits for them, and re-layouts  11.4 us
    all_to_all x1, waiting for transfers between devices, per_device(): lax.all_to_all(head_out.reshape(cut_count, q_rows, head_dim), 'cuts', spl...  10.6 us
    dot_general x1, matrix products, per_device(): lax.dot_general(act_rows, full_down, (((1,), (1,)), ((), ())), preferred_...  10.1 us
    all_to_all x1, waiting for transfers between devices, per_device(): lax.all_to_all(expert_out, 'req', split_axis=0, concat_axis=0, tiled=True)  9.28 us
    all_to_all x1, starting transfers between devices, per_device(): lax.all_to_all(packed.reshape(packed.shape[0], head_count, head_dim), 'cu...  8.61 us
  transfers between devices with their start and end apart: 6, of which 3 were waited for; matrix products, arithmetic and copies ran while one was open for 19% of the time, Pallas kernels for 28%

profile of v5, /device:TPU:8, one launch (start us, length us, event | category | flops | bytes accessed | tf_op | source)
XLA Modules:
  0.0 266.6 jit_solution(17269067747478360901)
XLA Ops:
  6.5 0.7 all-gather.7.cloned.1.call-update
  7.3 0.7 all-gather.11.cloned.1.call-update
  8.1 0.7 all-gather.9.cloned.1.call-update
  8.7 1.8 copy.80
  10.5 1.2 copy.81
  11.8 1.8 copy.82
  13.6 1.2 copy.83
  14.8 1.1 copy.84
  15.9 1.0 broadcast_multiply_fusion
  16.9 0.7 constant_dynamic-update-slice_fusion.4
  17.7 0.9 constant_dynamic-update-slice_fusion.3
  18.5 1.7 constant_dynamic-update-slice_fusion.2
  20.2 0.8 constant_dynamic-update-slice_fusion.1
  21.1 0.8 constant_dynamic-update-slice_fusion
  21.9 8.6 %all-to-all-start = ((bf16[896,16,64]{0,2,1:T(8,128)(2,1)}), bf16[896,16,64]{0,2,1:T(8,128)(2,1)}, u32[]{:S(2)}, u32[]{:S(2)}) async-start(bf16[896,16,64]{0,2,1:T(8,128)(2,1)} %constant_dynamic-update-slice_fusion), calls=%async_computation | async-start | bytes 3670016 | tf_op jit(solution)/shard_map/all_to_all | solution.py:178
  31.2 0.9 convert_add_fusion
  32.1 3.3 %fusion = f32[1,8,16,512]{3,0,2,1:T(1,128)S(1)} fusion(s32[8,16,512]{2,1,0:T(8,128)S(1)} %convert_add_fusion, f32[16,32]{1,0:T(8,128)} %param.21, s32[]{:T(128)S(6)} %select_n.11), kind=kOutput, calls=%fused_computation.1 | convolution fusion | flops 27262976 | bytes 524804 | tf_op jit(solution)/shard_map/agmk,hk->agm/dot_general | solution.py:101
  35.4 0.7 copy.107
  36.1 0.1 subtract_add_fusion
  36.2 0.7 fusion.110.live_ref
  36.9 0.7 convert_add_fusion.1
  37.6 2.7 %fusion.1 = f32[1,8,16,384]{3,0,2,1:T(1,128)S(1)} fusion(s32[8,16,384]{2,1,0:T(8,128)S(1)} %convert_add_fusion.1, f32[16,32]{1,0:T(8,128)} %param.21, s32[]{:T(128)S(6)} %select_n.11), kind=kOutput, calls=%fused_computation.3 | convolution fusion | flops 20447232 | bytes 393732 | tf_op jit(solution)/shard_map/agmk,hk->agm/dot_general | solution.py:102
  40.3 0.8 bitcast_select_fusion.tn_ref
  41.0 49.6 %all-to-all-done = bf16[896,16,64]{0,2,1:T(8,128)(2,1)} async-done(((bf16[896,16,64]{0,2,1:T(8,128)(2,1)}), bf16[896,16,64]{0,2,1:T(8,128)(2,1)}, u32[]{:S(2)}, u32[]{:S(2)}) %all-to-all-start) | async-done | bytes 1835040 | tf_op jit(solution)/shard_map/all_to_all | solution.py:178
  90.6 4.6 %copy.85 = bf16[896,16,64]{2,0,1:T(8,128)(2,1)} copy(bf16[896,16,64]{0,2,1:T(8,128)(2,1)} %all-to-all-done) | data formatting | bytes 3670016 | tf_op jit(solution)/shard_map/all_to_all | solution.py:178
  95.2 1.9 slice.12
  97.0 3.9 %fusion.113 = (bf16[16,384,64]{2,1,0:T(8,128)(2,1)}, bf16[16,384,64]{2,1,0:T(8,128)(2,1)}) fusion(bf16[16,896,64]{2,1,0:T(8,128)(2,1)} %bitcast.81), kind=kLoop, calls=%fused_computation.141 | loop fusion | bytes 3145728 | tf_op jit(solution)/shard_map/slice | solution.py:183
  101.0 74.5 %shard_map.145 = bf16[2048,64]{1,0:T(8,128)(2,1)} custom-call(s32[1]{0:T(128)} %copy.112.scalars, bf16[2048,64]{1,0:T(8,128)(2,1)} %bitcast.89, bf16[16,384,64]{2,1,0:T(8,128)(2,1)} %get-tuple-element.8.k_ref, bf16[16,384,64]{2,1,0:T(8,128)(2,1)} %get-tuple-element.7.v_ref, f32[8,16,512]{2,1,0:T(8,128)} %bitcast.90, ...), custom_call_target="tpu_custom_call" | custom-call | flops 3221225472 | bytes 9961472 | tf_op jit(solution)/shard_map/pallas_call | solution.py:133
  175.5 1.9 copy.86
  177.4 6.5 %all-to-all-start.1 = ((bf16[16,128,64]{1,2,0:T(8,128)(2,1)}), bf16[16,128,64]{1,2,0:T(8,128)(2,1)S(1)}, u32[]{:S(2)}, u32[]{:S(2)}) async-start(bf16[16,128,64]{1,2,0:T(8,128)(2,1)} %copy.86), calls=%async_computation.1 | async-start | bytes 524288 | tf_op jit(solution)/shard_map/all_to_all | solution.py:188
  184.0 0.1 copy.87
  184.1 0.3 convert_reduce_fusion
  184.4 0.1 fusion.108
  184.5 10.6 %all-to-all-done.1 = bf16[16,128,64]{1,2,0:T(8,128)(2,1)S(1)} async-done(((bf16[16,128,64]{1,2,0:T(8,128)(2,1)}), bf16[16,128,64]{1,2,0:T(8,128)(2,1)S(1)}, u32[]{:S(2)}, u32[]{:S(2)}) %all-to-all-start.1) | async-done | bytes 262176 | tf_op jit(solution)/shard_map/all_to_all | solution.py:188
  195.1 0.5 multiply_reduce_fusion
  195.6 0.3 fusion.112
  195.9 0.5 select_reduce_fusion
  196.4 0.8 fusion.28
  197.3 0.5 convolution_convert_fusion
  197.7 20.6 %all_to_all.30 = bf16[16,20,1024]{2,1,0:T(8,128)(2,1)S(1)} all-to-all(bf16[16,20,1024]{2,1,0:T(8,128)(2,1)S(1)} %convolution_convert_fusion), channel_id=1, replica_groups=mesh['req'=16,'cuts'=16] {'req'}, dimensions={0} | all-to-all | bytes 1310720 | tf_op jit(solution)/shard_map/all_to_all | solution.py:217
  218.4 1.0 reshape.335
  219.3 7.5 %fusion.21 = f32[320,2816]{1,0:T(8,128)} fusion(bf16[320,1024]{1,0:T(8,128)(2,1)} %reshape.335, bf16[1,1024,2816]{1,2,0:T(8,128)(2,1)} %all-gather.7.cloned.1.call-done), kind=kOutput, calls=%fused_computation.20 | convolution fusion | flops 1852702720 | bytes 10027008 | tf_op jit(solution)/shard_map/dot_general | solution.py:222
  226.8 10.1 %fusion.25 = bf16[320,1024]{1,0:T(8,128)(2,1)} fusion(bf16[1,1024,2816]{1,2,0:T(8,128)(2,1)} %all-gather.11.cloned.1.call-done, f32[320,2816]{1,0:T(8,128)} %fusion.21, bf16[320,1024]{1,0:T(8,128)(2,1)S(1)} %copy-done.1, bf16[1,1024,2816]{1,2,0:T(8,128)(2,1)} %all-gather.9.cloned.1.call-done), kind=kOutput, calls=%fused_computation.24 | convolution fusion | flops 3693117440 | bytes 16449536 | tf_op jit(solution)/shard_map/dot_general | solution.py:225
  237.0 2.1 reshape.336
  239.1 5.2 %all-to-all-start.3 = ((bf16[16,20,1024]{2,1,0:T(8,128)(2,1)}), bf16[16,20,1024]{2,1,0:T(8,128)(2,1)S(1)}, u32[]{:S(2)}, u32[]{:S(2)}) async-start(bf16[16,20,1024]{2,1,0:T(8,128)(2,1)} %reshape.336), calls=%async_computation.3 | async-start | bytes 1572864 | tf_op jit(solution)/shard_map/all_to_all | solution.py:228
  244.3 3.3 %convolution_bitcast_fusion = f32[16,20,128]{1,0,2:T(8,128)} fusion(f32[128,2]{1,0:T(8,128)S(1)} %add_divide_fusion, f32[128,2]{1,0:T(8,128)} %copy-done.3, s32[128,2]{1,0:T(8,128)S(1)} %copy.87), kind=kOutput, calls=%fused_computation.23 | convolution fusion | flops 997376 | bytes 166912 | tf_op jit(solution)/shard_map/tke,tkc,tk->ect/dot_general | solution.py:229
  247.6 9.3 %all-to-all-done.3 = bf16[16,20,1024]{2,1,0:T(8,128)(2,1)S(1)} async-done(((bf16[16,20,1024]{2,1,0:T(8,128)(2,1)}), bf16[16,20,1024]{2,1,0:T(8,128)(2,1)S(1)}, u32[]{:S(2)}, u32[]{:S(2)}) %all-to-all-start.3) | async-done | bytes 655392 | tf_op jit(solution)/shard_map/all_to_all | solution.py:228
  256.9 3.2 %fusion.31 = bf16[1,128,1024]{2,1,0:T(8,128)(2,1)} fusion(f32[128,1024]{1,0:T(8,128)S(1)} %get-tuple-element.10, bf16[16,20,1024]{2,1,0:T(8,128)(2,1)S(1)} %all-to-all-done.3, f32[16,20,128]{1,0,2:T(8,128)} %convolution_bitcast_fusion), kind=kOutput, calls=%fused_computation.31 | convolution fusion | flops 503578624 | bytes 1605632 | tf_op jit(solution)/shard_map/ect,ecd->td/dot_general | solution.py:232
  (28 shorter events, 0.2 us)
Async XLA Ops:
  6.5 188.5 %copy-start = (bf16[1024,1024]{1,0:T(8,128)(2,1)S(1)}, bf16[1024,1024]{1,0:T(8,128)(2,1)}, u32[]{:S(2)}) copy-start(bf16[1024,1024]{1,0:T(8,128)(2,1)} %param.23) | copy-start | bytes 6291460
  6.5 212.8 %all-gather.7.cloned.1.call-start = ((), (), s32[]{:S(2)}) async-start(), calls=%async_computation.4 | async-start | bytes 6127616 | tf_op jit(solution)/shard_map/all_gather | solution.py:218
  7.3 219.6 %all-gather.11.cloned.1.call-start = ((), (), s32[]{:S(2)}) async-start(), calls=%async_computation.6 | async-start | bytes 6127616 | tf_op jit(solution)/shard_map/all_gather | solution.py:220
  8.0 218.8 %all-gather.9.cloned.1.call-start = ((), (), s32[]{:S(2)}) async-start(), calls=%async_computation.5 | async-start | bytes 6127616 | tf_op jit(solution)/shard_map/all_gather | solution.py:219
  21.9 68.7 %all-to-all-start = ((bf16[896,16,64]{0,2,1:T(8,128)(2,1)}), bf16[896,16,64]{0,2,1:T(8,128)(2,1)}, u32[]{:S(2)}, u32[]{:S(2)}) async-start(bf16[896,16,64]{0,2,1:T(8,128)(2,1)} %constant_dynamic-update-slice_fusion), calls=%async_computation | async-start | bytes 3670016 | tf_op jit(solution)/shard_map/all_to_all | solution.py:178
  100.9 83.0 %copy-start.5 = (bf16[1024]{0:T(1024)(128)(2,1)S(1)}, bf16[1024]{0:T(1024)(128)(2,1)}, u32[]{:S(2)}) copy-start(bf16[1024]{0:T(1024)(128)(2,1)} %param.24) | copy-start | bytes 6148
  100.9 83.0 %copy-start.6 = (s32[1,128,2]{1,2,0:T(2,128)S(1)}, s32[1,128,2]{1,2,0:T(2,128)}, u32[]{:S(2)}) copy-start(s32[1,128,2]{1,2,0:T(2,128)} %param.26) | copy-start | bytes 3076
  101.0 94.1 %copy-start.2 = (bf16[1,128,1024]{2,1,0:T(8,128)(2,1)S(1)}, bf16[1,128,1024]{2,1,0:T(8,128)(2,1)}, u32[]{:S(2)}) copy-start(bf16[1,128,1024]{2,1,0:T(8,128)(2,1)} %param.22) | copy-start | bytes 786436
  175.5 20.2 %copy-start.4 = (bf16[1024,16]{0,1:T(8,128)(2,1)S(1)}, bf16[1024,16]{0,1:T(8,128)(2,1)}, u32[]{:S(2)}) copy-start(bf16[1024,16]{0,1:T(8,128)(2,1)} %param.25) | copy-start | bytes 98308
  177.4 17.7 %all-to-all-start.1 = ((bf16[16,128,64]{1,2,0:T(8,128)(2,1)}), bf16[16,128,64]{1,2,0:T(8,128)(2,1)S(1)}, u32[]{:S(2)}, u32[]{:S(2)}) async-start(bf16[16,128,64]{1,2,0:T(8,128)(2,1)} %copy.86), calls=%async_computation.1 | async-start | bytes 524288 | tf_op jit(solution)/shard_map/all_to_all | solution.py:188
  196.4 0.8 copy-start.3
  219.3 7.5 %copy-start.1 = (bf16[320,1024]{1,0:T(8,128)(2,1)S(1)}, bf16[320,1024]{1,0:T(8,128)(2,1)}, u32[]{:S(2)}) copy-start(bf16[320,1024]{1,0:T(8,128)(2,1)} %reshape.335) | copy-start | bytes 1966084
  239.1 17.8 %all-to-all-start.3 = ((bf16[16,20,1024]{2,1,0:T(8,128)(2,1)}), bf16[16,20,1024]{2,1,0:T(8,128)(2,1)S(1)}, u32[]{:S(2)}, u32[]{:S(2)}) async-start(bf16[16,20,1024]{2,1,0:T(8,128)(2,1)} %reshape.336), calls=%async_computation.3 | async-start | bytes 1572864 | tf_op jit(solution)/shard_map/all_to_all | solution.py:228
Sparse Core Ops, SparseCore 0:
  9.2 85.6 all-gather.6
  96.7 43.3 all-gather.10
  142.0 42.8 all-gather.8

commit v6 on v5

--- a/solution.py
+++ b/solution.py
@@ -43,13 +43,13 @@
 
 
 def attention_kernel(scalars, q_ref, k_ref, v_ref, tc_ref, tn_ref, live_ref, o_ref):
-    q_rows = q_ref.shape[0]
     key_blocks, key_span, head_dim = k_ref.shape
+    q_rows = q_ref.shape[0] * q_ref.shape[1]
     cache_rows = tc_ref.shape[2] - q_rows
     new_rows = key_span - cache_rows
     cache_width = tc_ref.shape[2]
     new_width = tn_ref.shape[2]
-    query = q_ref[...]
+    query = q_ref[...].reshape(q_rows, head_dim)
 
     def one_block(g, carry):
         best, weighted, factor_sum = carry
@@ -106,12 +106,16 @@
     return cache_table, new_table, live
 
 
-def block_partials(query_rows, key_rows, value_rows, head_table, length, cache_rows, q_rows):
+def block_partials(packed, head_table, length, cache_rows, q_rows):
+    source_rows = q_rows
     q_rows = 2 * q_rows
-    key_blocks, key_span, head_dim = key_rows.shape
+    key_blocks, packed_rows, head_dim = packed.shape
+    key_span = (packed_rows - source_rows) // 2
     new_rows = key_span - cache_rows
-    query_total = query_rows.shape[0]
+    query_total = key_blocks * source_rows
     query_blocks = query_total // q_rows
+    sources = q_rows // source_rows
+    query_offset = 2 * key_span // source_rows
     cache_table, new_table, live = bias_tables(
         head_table, length, q_rows, cache_rows, new_rows, query_blocks, key_blocks
     )
@@ -120,9 +124,9 @@
         num_scalar_prefetch=1,
         grid=(query_blocks,),
         in_specs=[
-            pl.BlockSpec((q_rows, head_dim), lambda b, s: (b, 0)),
+            pl.BlockSpec((sources, source_rows, head_dim), lambda b, s: (b, query_offset, 0)),
             pl.BlockSpec((key_blocks, key_span, head_dim), lambda b, s: (0, 0, 0)),
-            pl.BlockSpec((key_blocks, key_span, head_dim), lambda b, s: (0, 0, 0)),
+            pl.BlockSpec((key_blocks, key_span, head_dim), lambda b, s: (0, 1, 0)),
             pl.BlockSpec((1, key_blocks, cache_table.shape[2]), lambda b, s: (b, 0, 0)),
             pl.BlockSpec((1, key_blocks, new_table.shape[2]), lambda b, s: (b, 0, 0)),
             pl.BlockSpec(live.shape, lambda b, s: (0, 0)),
@@ -139,7 +143,7 @@
             transcendentals=pairs,
             bytes_accessed=4 * query_total * head_dim * key_blocks + 4 * key_span * key_blocks * head_dim,
         ),
-    )(scalars, query_rows, key_rows, value_rows, cache_table, new_table, live)
+    )(scalars, packed, packed, packed, cache_table, new_table, live)
 
 
 def per_device(
@@ -173,18 +177,13 @@
     local_values = jnp.concatenate([cache_values[0], new_values[0]], axis=0)
     key_span = local_keys.shape[0]
     packed = jnp.concatenate(
-        [queries[0] * jnp.asarray(0.125, queries.dtype), local_keys, local_values], axis=0
+        [local_keys, local_values, queries[0] * jnp.asarray(0.125, queries.dtype)], axis=0
     )
     packed = lax.all_to_all(
         packed.reshape(packed.shape[0], head_count, head_dim), "cuts", split_axis=1, concat_axis=0, tiled=True
     ).reshape(cut_count, packed.shape[0], head_dim)
-    head_queries = packed[:, :q_rows].reshape(query_total, head_dim)
-    head_keys = packed[:, q_rows:q_rows + key_span]
-    head_values = packed[:, q_rows + key_span:]
     head_table = lax.dynamic_slice_in_dim(relative_bias, cut_index, 1, 0)
-    head_out = block_partials(
-        head_queries, head_keys, head_values, head_table, length, cache_rows, q_rows
-    )
+    head_out = block_partials(packed, head_table, length, cache_rows, q_rows)
     attended = lax.all_to_all(
         head_out.reshape(cut_count, q_rows, head_dim), "cuts", split_axis=0, concat_axis=0, tiled=True
     ).transpose(1, 0, 2).reshape(q_rows, model_width)

time: 268 us -> 261 us (0.974)
  local copies, waits for them, and re-layouts: 28.3 us -> 22.6 us
    slice x2 -> x0, local copies, waits for them, and re-layouts: 5.78 us -> none  [the longest x1 3.9 us: per_device(): head_values = packed[:, q_rows + key_span:]]
    unnamed x23 -> x25, local copies, waits for them, and re-layouts: 11.4 us -> 11.4 us
  transfers between devices with their start and end apart: 6 -> 6, of which waited for: 3 -> 3; matrix products, arithmetic and copies ran while one was open for 19% -> 17% of each run, Pallas kernels for 28% -> 29%
where the time goes in v6:
time: 261 us; the launch traced here: 260 us
  Pallas kernels  74.6 us (29%)
  waiting for transfers between devices  72.2 us (28%)
  matrix products  32.4 us (12%)
  local copies, waits for them, and re-layouts  22.6 us (9%)
  starting transfers between devices  20.3 us (8%)
  blocking collectives  19.8 us (8%)
  between operations  13.9 us (5%)
  other arithmetic  4.01 us (2%)
    pallas_call x1, Pallas kernels, block_partials(): pl.pallas_call(attention_kernel, grid_spec=grid_spec, out_shape=jax.Shape...  74.6 us
    all_to_all x1, waiting for transfers between devices, per_device(): lax.all_to_all(packed.reshape(packed.shape[0], head_count, head_dim), 'cu...  49.9 us
    all_to_all x1, blocking collectives, per_device(): lax.all_to_all(buffers, 'req', split_axis=0, concat_axis=0, tiled=True)  19.8 us
    all_to_all x1, waiting for transfers between devices, per_device(): lax.all_to_all(head_out.reshape(cut_count, q_rows, head_dim), 'cuts', spl...  11.4 us
    unnamed x25, local copies, waits for them, and re-layouts  11.4 us
    dot_general x1, matrix products, per_device(): lax.dot_general(act_rows, full_down, (((1,), (1,)), ((), ())), preferred_...  10.1 us
    all_to_all x1, waiting for transfers between devices, per_device(): lax.all_to_all(expert_out, 'req', split_axis=0, concat_axis=0, tiled=True)  8.77 us
    all_to_all x1, starting transfers between devices, per_device(): lax.all_to_all(packed.reshape(packed.shape[0], head_count, head_dim), 'cu...  8.61 us
  transfers between devices with their start and end apart: 6, of which 3 were waited for; matrix products, arithmetic and copies ran while one was open for 17% of the time, Pallas kernels for 29%

profile of v6, /device:TPU:8, one launch (start us, length us, event | category | flops | bytes accessed | tf_op | source)
XLA Modules:
  0.0 259.8 jit_solution(4624490157446017836)
XLA Ops:
  6.5 0.7 all-gather.7.cloned.1.call-update
  7.3 0.0 all-gather.11.cloned.1.call-start
  7.3 0.7 all-gather.11.cloned.1.call-update
  8.0 0.0 all-gather.9.cloned.1.call-start
  8.1 0.7 all-gather.9.cloned.1.call-update
  8.7 1.2 copy.80
  10.0 1.8 copy.81
  11.8 1.2 copy.82
  13.0 0.8 copy.83
  13.9 1.1 copy.84
  15.0 0.9 constant_dynamic-update-slice_fusion.4
  15.9 1.7 constant_dynamic-update-slice_fusion.3
  17.6 0.9 constant_dynamic-update-slice_fusion.2
  18.4 1.7 constant_dynamic-update-slice_fusion.1
  20.1 0.8 constant_dynamic-update-slice_fusion
  20.9 8.6 %all-to-all-start = ((bf16[896,16,64]{0,2,1:T(8,128)(2,1)}), bf16[896,16,64]{0,2,1:T(8,128)(2,1)}, u32[]{:S(2)}, u32[]{:S(2)}) async-start(bf16[896,16,64]{0,2,1:T(8,128)(2,1)} %constant_dynamic-update-slice_fusion), calls=%async_computation | async-start | bytes 3670016 | tf_op jit(solution)/shard_map/all_to_all | solution.py:182
  30.2 0.1 subtract_add_fusion.1
  30.3 0.9 convert_add_fusion
  31.2 3.3 %fusion = f32[1,8,16,512]{3,0,2,1:T(1,128)S(1)} fusion(s32[8,16,512]{2,1,0:T(8,128)S(1)} %convert_add_fusion, f32[16,32]{1,0:T(8,128)} %param.21, s32[]{:T(128)S(6)} %select_n.11), kind=kOutput, calls=%fused_computation.1 | convolution fusion | flops 27262976 | bytes 524804 | tf_op jit(solution)/shard_map/agmk,hk->agm/dot_general | solution.py:101
  34.5 0.7 copy.107
  35.2 0.1 subtract_add_fusion
  35.3 0.7 fusion.110.live_ref
  36.0 0.7 convert_add_fusion.1
  36.6 2.7 %fusion.1 = f32[1,8,16,384]{3,0,2,1:T(1,128)S(1)} fusion(s32[8,16,384]{2,1,0:T(8,128)S(1)} %convert_add_fusion.1, f32[16,32]{1,0:T(8,128)} %param.21, s32[]{:T(128)S(6)} %select_n.11), kind=kOutput, calls=%fused_computation.3 | convolution fusion | flops 20447232 | bytes 393732 | tf_op jit(solution)/shard_map/agmk,hk->agm/dot_general | solution.py:102
  39.3 0.8 bitcast_select_fusion.tn_ref
  40.1 49.9 %all-to-all-done = bf16[896,16,64]{0,2,1:T(8,128)(2,1)} async-done(((bf16[896,16,64]{0,2,1:T(8,128)(2,1)}), bf16[896,16,64]{0,2,1:T(8,128)(2,1)}, u32[]{:S(2)}, u32[]{:S(2)}) %all-to-all-start) | async-done | bytes 1835040 | tf_op jit(solution)/shard_map/all_to_all | solution.py:182
  90.0 4.6 %copy.85 = bf16[896,16,64]{2,0,1:T(8,128)(2,1)} copy(bf16[896,16,64]{0,2,1:T(8,128)(2,1)} %all-to-all-done) | data formatting | bytes 3670016 | tf_op jit(solution)/shard_map/all_to_all | solution.py:182
  94.6 74.6 %shard_map.145 = bf16[2048,64]{1,0:T(8,128)(2,1)} custom-call(s32[1]{0:T(128)} %copy.112.scalars, bf16[16,896,64]{2,1,0:T(8,128)(2,1)} %bitcast.79, bf16[16,896,64]{2,1,0:T(8,128)(2,1)} %bitcast.80, bf16[16,896,64]{2,1,0:T(8,128)(2,1)} %bitcast.81, f32[8,16,512]{2,1,0:T(8,128)} %bitcast.89, f32[8,16,384]{2,1,0:T(8,128)} %bitcast_select_fusion.tn_ref, ...), custom_call_target="tpu_custom_call" | custom-call | flops 3221225472 | bytes 9961472 | tf_op jit(solution)/shard_map/pallas_call | solution.py:137
  169.2 1.9 copy.86
  171.2 6.5 %all-to-all-start.1 = ((bf16[16,128,64]{1,2,0:T(8,128)(2,1)}), bf16[16,128,64]{1,2,0:T(8,128)(2,1)S(1)}, u32[]{:S(2)}, u32[]{:S(2)}) async-start(bf16[16,128,64]{1,2,0:T(8,128)(2,1)} %copy.86), calls=%async_computation.1 | async-start | bytes 524288 | tf_op jit(solution)/shard_map/all_to_all | solution.py:187
  177.7 0.1 copy.87
  177.8 0.3 convert_reduce_fusion
  178.1 0.1 fusion.108
  178.2 11.4 %all-to-all-done.1 = bf16[16,128,64]{1,2,0:T(8,128)(2,1)S(1)} async-done(((bf16[16,128,64]{1,2,0:T(8,128)(2,1)}), bf16[16,128,64]{1,2,0:T(8,128)(2,1)S(1)}, u32[]{:S(2)}, u32[]{:S(2)}) %all-to-all-start.1) | async-done | bytes 262176 | tf_op jit(solution)/shard_map/all_to_all | solution.py:187
  189.6 0.5 multiply_reduce_fusion
  190.2 0.3 fusion.112
  190.5 0.5 select_reduce_fusion
  191.0 0.8 fusion.28
  191.8 0.5 convolution_convert_fusion
  192.3 19.8 %all_to_all.30 = bf16[16,20,1024]{2,1,0:T(8,128)(2,1)S(1)} all-to-all(bf16[16,20,1024]{2,1,0:T(8,128)(2,1)S(1)} %convolution_convert_fusion), channel_id=1, replica_groups=mesh['req'=16,'cuts'=16] {'req'}, dimensions={0} | all-to-all | bytes 1310720 | tf_op jit(solution)/shard_map/all_to_all | solution.py:216
  212.1 1.0 reshape.331
  213.1 7.5 %fusion.21 = f32[320,2816]{1,0:T(8,128)} fusion(bf16[320,1024]{1,0:T(8,128)(2,1)} %reshape.331, bf16[1,1024,2816]{1,2,0:T(8,128)(2,1)} %all-gather.7.cloned.1.call-done), kind=kOutput, calls=%fused_computation.20 | convolution fusion | flops 1852702720 | bytes 10027008 | tf_op jit(solution)/shard_map/dot_general | solution.py:221
  220.6 10.1 %fusion.25 = bf16[320,1024]{1,0:T(8,128)(2,1)} fusion(bf16[1,1024,2816]{1,2,0:T(8,128)(2,1)} %all-gather.11.cloned.1.call-done, f32[320,2816]{1,0:T(8,128)} %fusion.21, bf16[320,1024]{1,0:T(8,128)(2,1)S(1)} %copy-done.1, bf16[1,1024,2816]{1,2,0:T(8,128)(2,1)} %all-gather.9.cloned.1.call-done), kind=kOutput, calls=%fused_computation.24 | convolution fusion | flops 3693117440 | bytes 16449536 | tf_op jit(solution)/shard_map/dot_general | solution.py:224
  230.7 2.1 reshape.332
  232.8 5.2 %all-to-all-start.3 = ((bf16[16,20,1024]{2,1,0:T(8,128)(2,1)}), bf16[16,20,1024]{2,1,0:T(8,128)(2,1)S(1)}, u32[]{:S(2)}, u32[]{:S(2)}) async-start(bf16[16,20,1024]{2,1,0:T(8,128)(2,1)} %reshape.332), calls=%async_computation.3 | async-start | bytes 1572864 | tf_op jit(solution)/shard_map/all_to_all | solution.py:227
  238.0 3.3 %convolution_bitcast_fusion = f32[16,20,128]{1,0,2:T(8,128)} fusion(f32[128,2]{1,0:T(8,128)S(1)} %add_divide_fusion, f32[128,2]{1,0:T(8,128)} %copy-done.4, s32[128,2]{1,0:T(8,128)S(1)} %copy.87), kind=kOutput, calls=%fused_computation.23 | convolution fusion | flops 997376 | bytes 166912 | tf_op jit(solution)/shard_map/tke,tkc,tk->ect/dot_general | solution.py:228
  241.3 8.8 %all-to-all-done.3 = bf16[16,20,1024]{2,1,0:T(8,128)(2,1)S(1)} async-done(((bf16[16,20,1024]{2,1,0:T(8,128)(2,1)}), bf16[16,20,1024]{2,1,0:T(8,128)(2,1)S(1)}, u32[]{:S(2)}, u32[]{:S(2)}) %all-to-all-start.3) | async-done | bytes 655392 | tf_op jit(solution)/shard_map/all_to_all | solution.py:227
  250.1 3.2 %fusion.31 = bf16[1,128,1024]{2,1,0:T(8,128)(2,1)} fusion(f32[128,1024]{1,0:T(8,128)S(1)} %get-tuple-element.8, bf16[16,20,1024]{2,1,0:T(8,128)(2,1)S(1)} %all-to-all-done.3, f32[16,20,128]{1,0,2:T(8,128)} %convolution_bitcast_fusion), kind=kOutput, calls=%fused_computation.31 | convolution fusion | flops 503578624 | bytes 1605632 | tf_op jit(solution)/shard_map/ect,ecd->td/dot_general | solution.py:231
  (28 shorter events, 0.1 us)
Async XLA Ops:
  6.5 183.1 %copy-start = (bf16[1024,1024]{1,0:T(8,128)(2,1)S(1)}, bf16[1024,1024]{1,0:T(8,128)(2,1)}, u32[]{:S(2)}) copy-start(bf16[1024,1024]{1,0:T(8,128)(2,1)} %param.23) | copy-start | bytes 6291460
  6.5 6.5 %copy-start.2 = (bf16[1,128,1024]{2,1,0:T(8,128)(2,1)S(1)}, bf16[1,128,1024]{2,1,0:T(8,128)(2,1)}, u32[]{:S(2)}) copy-start(bf16[1,128,1024]{2,1,0:T(8,128)(2,1)} %param.17) | copy-start | bytes 786436
  6.5 206.6 %all-gather.7.cloned.1.call-start = ((), (), s32[]{:S(2)}) async-start(), calls=%async_computation.4 | async-start | bytes 6127616 | tf_op jit(solution)/shard_map/all_gather | solution.py:217
  7.3 213.3 %all-gather.11.cloned.1.call-start = ((), (), s32[]{:S(2)}) async-start(), calls=%async_computation.6 | async-start | bytes 6127616 | tf_op jit(solution)/shard_map/all_gather | solution.py:219
  8.0 212.6 %all-gather.9.cloned.1.call-start = ((), (), s32[]{:S(2)}) async-start(), calls=%async_computation.5 | async-start | bytes 6127616 | tf_op jit(solution)/shard_map/all_gather | solution.py:218
  20.9 69.1 %all-to-all-start = ((bf16[896,16,64]{0,2,1:T(8,128)(2,1)}), bf16[896,16,64]{0,2,1:T(8,128)(2,1)}, u32[]{:S(2)}, u32[]{:S(2)}) async-start(bf16[896,16,64]{0,2,1:T(8,128)(2,1)} %constant_dynamic-update-slice_fusion), calls=%async_computation | async-start | bytes 3670016 | tf_op jit(solution)/shard_map/all_to_all | solution.py:182
  94.6 83.0 %copy-start.6 = (bf16[1024]{0:T(1024)(128)(2,1)S(1)}, bf16[1024]{0:T(1024)(128)(2,1)}, u32[]{:S(2)}) copy-start(bf16[1024]{0:T(1024)(128)(2,1)} %param.24) | copy-start | bytes 6148
  94.6 83.1 %copy-start.7 = (s32[1,128,2]{1,2,0:T(2,128)S(1)}, s32[1,128,2]{1,2,0:T(2,128)}, u32[]{:S(2)}) copy-start(s32[1,128,2]{1,2,0:T(2,128)} %param.26) | copy-start | bytes 3076
  94.6 95.0 %copy-start.3 = (bf16[1,128,1024]{2,1,0:T(8,128)(2,1)S(1)}, bf16[1,128,1024]{2,1,0:T(8,128)(2,1)}, u32[]{:S(2)}) copy-start(bf16[1,128,1024]{2,1,0:T(8,128)(2,1)} %param.22) | copy-start | bytes 786436
  169.2 21.0 %copy-start.5 = (bf16[1024,16]{0,1:T(8,128)(2,1)S(1)}, bf16[1024,16]{0,1:T(8,128)(2,1)}, u32[]{:S(2)}) copy-start(bf16[1024,16]{0,1:T(8,128)(2,1)} %param.25) | copy-start | bytes 98308
  171.2 18.5 %all-to-all-start.1 = ((bf16[16,128,64]{1,2,0:T(8,128)(2,1)}), bf16[16,128,64]{1,2,0:T(8,128)(2,1)S(1)}, u32[]{:S(2)}, u32[]{:S(2)}) async-start(bf16[16,128,64]{1,2,0:T(8,128)(2,1)} %copy.86), calls=%async_computation.1 | async-start | bytes 524288 | tf_op jit(solution)/shard_map/all_to_all | solution.py:187
  191.0 0.8 copy-start.4
  213.1 7.5 %copy-start.1 = (bf16[320,1024]{1,0:T(8,128)(2,1)S(1)}, bf16[320,1024]{1,0:T(8,128)(2,1)}, u32[]{:S(2)}) copy-start(bf16[320,1024]{1,0:T(8,128)(2,1)} %reshape.331) | copy-start | bytes 1966084
  232.8 17.2 %all-to-all-start.3 = ((bf16[16,20,1024]{2,1,0:T(8,128)(2,1)}), bf16[16,20,1024]{2,1,0:T(8,128)(2,1)S(1)}, u32[]{:S(2)}, u32[]{:S(2)}) async-start(bf16[16,20,1024]{2,1,0:T(8,128)(2,1)} %reshape.332), calls=%async_computation.3 | async-start | bytes 1572864 | tf_op jit(solution)/shard_map/all_to_all | solution.py:227
Sparse Core Ops, SparseCore 0:
  9.2 85.7 all-gather.6
  96.7 43.6 all-gather.10
  142.3 47.2 all-gather.8

commit v7 on v6

--- a/solution.py
+++ b/solution.py
@@ -108,7 +108,7 @@
 
 def block_partials(packed, head_table, length, cache_rows, q_rows):
     source_rows = q_rows
-    q_rows = 2 * q_rows
+    q_rows = 4 * q_rows
     key_blocks, packed_rows, head_dim = packed.shape
     key_span = (packed_rows - source_rows) // 2
     new_rows = key_span - cache_rows

time: 261 us -> 261 us (level)
  waiting for transfers between devices: 72.2 us -> 75.4 us
  transfers between devices with their start and end apart: 6 -> 6, of which waited for: 3 -> 3; matrix products, arithmetic and copies ran while one was open for 17% -> 16% of each run, Pallas kernels for 29% -> 28%
where the time goes in v7:
time: 261 us; the launch traced here: 260 us
  waiting for transfers between devices  75.4 us (29%)
  Pallas kernels  73.1 us (28%)
  matrix products  31.4 us (12%)
  local copies, waits for them, and re-layouts  22.6 us (9%)
  starting transfers between devices  20.3 us (8%)
  blocking collectives  19.8 us (8%)
  between operations  13.9 us (5%)
  other arithmetic  3.68 us (1%)
    pallas_call x1, Pallas kernels, block_partials(): pl.pallas_call(attention_kernel, grid_spec=grid_spec, out_shape=jax.Shape...  73.1 us
    all_to_all x1, waiting for transfers between devices, per_device(): lax.all_to_all(packed.reshape(packed.shape[0], head_count, head_dim), 'cu...  51.2 us
    all_to_all x1, blocking collectives, per_device(): lax.all_to_all(buffers, 'req', split_axis=0, concat_axis=0, tiled=True)  19.8 us
    all_to_all x1, waiting for transfers between devices, per_device(): lax.all_to_all(head_out.reshape(cut_count, q_rows, head_dim), 'cuts', spl...  13.3 us
    unnamed x25, local copies, waits for them, and re-layouts  11.4 us
    dot_general x1, matrix products, per_device(): lax.dot_general(act_rows, full_down, (((1,), (1,)), ((), ())), preferred_...  10.1 us
    all_to_all x1, waiting for transfers between devices, per_device(): lax.all_to_all(expert_out, 'req', split_axis=0, concat_axis=0, tiled=True)  8.86 us
    all_to_all x1, starting transfers between devices, per_device(): lax.all_to_all(packed.reshape(packed.shape[0], head_count, head_dim), 'cu...  8.61 us
  transfers between devices with their start and end apart: 6, of which 3 were waited for; matrix products, arithmetic and copies ran while one was open for 16% of the time, Pallas kernels for 28%

profile of v7, /device:TPU:8, one launch (start us, length us, event | category | flops | bytes accessed | tf_op | source)
XLA Modules:
  0.0 260.2 jit_solution(12153960502840984647)
XLA Ops:
  6.5 0.7 all-gather.7.cloned.1.call-update
  7.3 0.0 all-gather.11.cloned.1.call-start
  7.3 0.7 all-gather.11.cloned.1.call-update
  8.0 0.0 all-gather.9.cloned.1.call-start
  8.1 0.7 all-gather.9.cloned.1.call-update
  8.7 1.2 copy.80
  10.0 1.8 copy.81
  11.8 1.2 copy.82
  13.0 0.8 copy.83
  13.9 1.1 copy.84
  15.0 0.9 constant_dynamic-update-slice_fusion.4
  15.9 1.7 constant_dynamic-update-slice_fusion.3
  17.6 0.9 constant_dynamic-update-slice_fusion.2
  18.4 1.7 constant_dynamic-update-slice_fusion.1
  20.1 0.8 constant_dynamic-update-slice_fusion
  20.9 8.6 %all-to-all-start = ((bf16[896,16,64]{0,2,1:T(8,128)(2,1)}), bf16[896,16,64]{0,2,1:T(8,128)(2,1)}, u32[]{:S(2)}, u32[]{:S(2)}) async-start(bf16[896,16,64]{0,2,1:T(8,128)(2,1)} %constant_dynamic-update-slice_fusion), calls=%async_computation | async-start | bytes 3670016 | tf_op jit(solution)/shard_map/all_to_all | solution.py:182
  30.2 0.1 subtract_add_fusion.1
  30.3 0.7 convert_add_fusion
  31.0 2.7 %fusion = f32[1,4,16,768]{3,0,2,1:T(1,128)S(1)} fusion(s32[4,16,768]{2,1,0:T(8,128)S(1)} %convert_add_fusion, f32[16,32]{1,0:T(8,128)} %param.21, s32[]{:T(128)S(6)} %select_n.11), kind=kOutput, calls=%fused_computation.1 | convolution fusion | flops 20447232 | bytes 393732 | tf_op jit(solution)/shard_map/agmk,hk->agm/dot_general | solution.py:101
  33.7 0.7 copy.107
  34.4 0.1 subtract_add_fusion
  34.4 0.7 fusion.110.live_ref
  35.1 0.6 convert_add_fusion.1
  35.7 2.4 fusion.7
  38.1 0.8 bitcast_select_fusion.tn_ref
  38.8 51.2 %all-to-all-done = bf16[896,16,64]{0,2,1:T(8,128)(2,1)} async-done(((bf16[896,16,64]{0,2,1:T(8,128)(2,1)}), bf16[896,16,64]{0,2,1:T(8,128)(2,1)}, u32[]{:S(2)}, u32[]{:S(2)}) %all-to-all-start) | async-done | bytes 1835040 | tf_op jit(solution)/shard_map/all_to_all | solution.py:182
  90.0 4.6 %copy.85 = bf16[896,16,64]{2,0,1:T(8,128)(2,1)} copy(bf16[896,16,64]{0,2,1:T(8,128)(2,1)} %all-to-all-done) | data formatting | bytes 3670016 | tf_op jit(solution)/shard_map/all_to_all | solution.py:182
  94.6 73.1 %shard_map.145 = bf16[2048,64]{1,0:T(8,128)(2,1)} custom-call(s32[1]{0:T(128)} %copy.112.scalars, bf16[16,896,64]{2,1,0:T(8,128)(2,1)} %bitcast.79, bf16[16,896,64]{2,1,0:T(8,128)(2,1)} %bitcast.80, bf16[16,896,64]{2,1,0:T(8,128)(2,1)} %bitcast.81, f32[4,16,768]{2,1,0:T(8,128)} %bitcast.89, f32[4,16,640]{2,1,0:T(8,128)} %bitcast_select_fusion.tn_ref, ...), custom_call_target="tpu_custom_call" | custom-call | flops 3221225472 | bytes 9961472 | tf_op jit(solution)/shard_map/pallas_call | solution.py:137
  167.7 1.9 copy.86
  169.7 6.5 %all-to-all-start.1 = ((bf16[16,128,64]{1,2,0:T(8,128)(2,1)}), bf16[16,128,64]{1,2,0:T(8,128)(2,1)S(1)}, u32[]{:S(2)}, u32[]{:S(2)}) async-start(bf16[16,128,64]{1,2,0:T(8,128)(2,1)} %copy.86), calls=%async_computation.1 | async-start | bytes 524288 | tf_op jit(solution)/shard_map/all_to_all | solution.py:187
  176.2 0.1 copy.87
  176.3 0.3 convert_reduce_fusion
  176.6 0.1 fusion.108
  176.7 13.3 %all-to-all-done.1 = bf16[16,128,64]{1,2,0:T(8,128)(2,1)S(1)} async-done(((bf16[16,128,64]{1,2,0:T(8,128)(2,1)}), bf16[16,128,64]{1,2,0:T(8,128)(2,1)S(1)}, u32[]{:S(2)}, u32[]{:S(2)}) %all-to-all-start.1) | async-done | bytes 262176 | tf_op jit(solution)/shard_map/all_to_all | solution.py:187
  190.0 0.5 multiply_reduce_fusion
  190.6 0.3 fusion.112
  190.9 0.5 select_reduce_fusion
  191.4 0.8 fusion.28
  192.2 0.5 convolution_convert_fusion
  192.7 19.8 %all_to_all.30 = bf16[16,20,1024]{2,1,0:T(8,128)(2,1)S(1)} all-to-all(bf16[16,20,1024]{2,1,0:T(8,128)(2,1)S(1)} %convolution_convert_fusion), channel_id=1, replica_groups=mesh['req'=16,'cuts'=16] {'req'}, dimensions={0} | all-to-all | bytes 1310720 | tf_op jit(solution)/shard_map/all_to_all | solution.py:216
  212.5 1.0 reshape.331
  213.4 7.5 %fusion.20 = f32[320,2816]{1,0:T(8,128)} fusion(bf16[320,1024]{1,0:T(8,128)(2,1)} %reshape.331, bf16[1,1024,2816]{1,2,0:T(8,128)(2,1)} %all-gather.7.cloned.1.call-done), kind=kOutput, calls=%fused_computation.19 | convolution fusion | flops 1852702720 | bytes 10027008 | tf_op jit(solution)/shard_map/dot_general | solution.py:221
  221.0 10.1 %fusion.25 = bf16[320,1024]{1,0:T(8,128)(2,1)} fusion(bf16[1,1024,2816]{1,2,0:T(8,128)(2,1)} %all-gather.11.cloned.1.call-done, f32[320,2816]{1,0:T(8,128)} %fusion.20, bf16[320,1024]{1,0:T(8,128)(2,1)S(1)} %copy-done.1, bf16[1,1024,2816]{1,2,0:T(8,128)(2,1)} %all-gather.9.cloned.1.call-done), kind=kOutput, calls=%fused_computation.24 | convolution fusion | flops 3693117440 | bytes 16449536 | tf_op jit(solution)/shard_map/dot_general | solution.py:224
  231.1 2.1 reshape.332
  233.2 5.1 %all-to-all-start.3 = ((bf16[16,20,1024]{2,1,0:T(8,128)(2,1)}), bf16[16,20,1024]{2,1,0:T(8,128)(2,1)S(1)}, u32[]{:S(2)}, u32[]{:S(2)}) async-start(bf16[16,20,1024]{2,1,0:T(8,128)(2,1)} %reshape.332), calls=%async_computation.3 | async-start | bytes 1572864 | tf_op jit(solution)/shard_map/all_to_all | solution.py:227
  238.3 3.3 %convolution_bitcast_fusion = f32[16,20,128]{1,0,2:T(8,128)} fusion(f32[128,2]{1,0:T(8,128)S(1)} %add_divide_fusion, f32[128,2]{1,0:T(8,128)} %copy-done.4, s32[128,2]{1,0:T(8,128)S(1)} %copy.87), kind=kOutput, calls=%fused_computation.23 | convolution fusion | flops 997376 | bytes 166912 | tf_op jit(solution)/shard_map/tke,tkc,tk->ect/dot_general | solution.py:228
  241.6 8.9 %all-to-all-done.3 = bf16[16,20,1024]{2,1,0:T(8,128)(2,1)S(1)} async-done(((bf16[16,20,1024]{2,1,0:T(8,128)(2,1)}), bf16[16,20,1024]{2,1,0:T(8,128)(2,1)S(1)}, u32[]{:S(2)}, u32[]{:S(2)}) %all-to-all-start.3) | async-done | bytes 655392 | tf_op jit(solution)/shard_map/all_to_all | solution.py:227
  250.5 3.2 %fusion.31 = bf16[1,128,1024]{2,1,0:T(8,128)(2,1)} fusion(f32[128,1024]{1,0:T(8,128)S(1)} %get-tuple-element.8, bf16[16,20,1024]{2,1,0:T(8,128)(2,1)S(1)} %all-to-all-done.3, f32[16,20,128]{1,0,2:T(8,128)} %convolution_bitcast_fusion), kind=kOutput, calls=%fused_computation.31 | convolution fusion | flops 503578624 | bytes 1605632 | tf_op jit(solution)/shard_map/ect,ecd->td/dot_general | solution.py:231
  (28 shorter events, 0.1 us)
Async XLA Ops:
  6.5 183.5 %copy-start = (bf16[1024,1024]{1,0:T(8,128)(2,1)S(1)}, bf16[1024,1024]{1,0:T(8,128)(2,1)}, u32[]{:S(2)}) copy-start(bf16[1024,1024]{1,0:T(8,128)(2,1)} %param.23) | copy-start | bytes 6291460
  6.5 6.5 %copy-start.2 = (bf16[1,128,1024]{2,1,0:T(8,128)(2,1)S(1)}, bf16[1,128,1024]{2,1,0:T(8,128)(2,1)}, u32[]{:S(2)}) copy-start(bf16[1,128,1024]{2,1,0:T(8,128)(2,1)} %param.17) | copy-start | bytes 786436
  6.5 206.9 %all-gather.7.cloned.1.call-start = ((), (), s32[]{:S(2)}) async-start(), calls=%async_computation.4 | async-start | bytes 6127616 | tf_op jit(solution)/shard_map/all_gather | solution.py:217
  7.3 213.7 %all-gather.11.cloned.1.call-start = ((), (), s32[]{:S(2)}) async-start(), calls=%async_computation.6 | async-start | bytes 6127616 | tf_op jit(solution)/shard_map/all_gather | solution.py:219
  8.0 213.0 %all-gather.9.cloned.1.call-start = ((), (), s32[]{:S(2)}) async-start(), calls=%async_computation.5 | async-start | bytes 6127616 | tf_op jit(solution)/shard_map/all_gather | solution.py:218
  20.9 69.1 %all-to-all-start = ((bf16[896,16,64]{0,2,1:T(8,128)(2,1)}), bf16[896,16,64]{0,2,1:T(8,128)(2,1)}, u32[]{:S(2)}, u32[]{:S(2)}) async-start(bf16[896,16,64]{0,2,1:T(8,128)(2,1)} %constant_dynamic-update-slice_fusion), calls=%async_computation | async-start | bytes 3670016 | tf_op jit(solution)/shard_map/all_to_all | solution.py:182
  94.6 81.6 %copy-start.6 = (bf16[1024]{0:T(1024)(128)(2,1)S(1)}, bf16[1024]{0:T(1024)(128)(2,1)}, u32[]{:S(2)}) copy-start(bf16[1024]{0:T(1024)(128)(2,1)} %param.24) | copy-start | bytes 6148
  94.6 81.6 %copy-start.7 = (s32[1,128,2]{1,2,0:T(2,128)S(1)}, s32[1,128,2]{1,2,0:T(2,128)}, u32[]{:S(2)}) copy-start(s32[1,128,2]{1,2,0:T(2,128)} %param.26) | copy-start | bytes 3076
  94.6 95.4 %copy-start.3 = (bf16[1,128,1024]{2,1,0:T(8,128)(2,1)S(1)}, bf16[1,128,1024]{2,1,0:T(8,128)(2,1)}, u32[]{:S(2)}) copy-start(bf16[1,128,1024]{2,1,0:T(8,128)(2,1)} %param.22) | copy-start | bytes 786436
  167.7 22.8 %copy-start.5 = (bf16[1024,16]{0,1:T(8,128)(2,1)S(1)}, bf16[1024,16]{0,1:T(8,128)(2,1)}, u32[]{:S(2)}) copy-start(bf16[1024,16]{0,1:T(8,128)(2,1)} %param.25) | copy-start | bytes 98308
  169.7 20.3 %all-to-all-start.1 = ((bf16[16,128,64]{1,2,0:T(8,128)(2,1)}), bf16[16,128,64]{1,2,0:T(8,128)(2,1)S(1)}, u32[]{:S(2)}, u32[]{:S(2)}) async-start(bf16[16,128,64]{1,2,0:T(8,128)(2,1)} %copy.86), calls=%async_computation.1 | async-start | bytes 524288 | tf_op jit(solution)/shard_map/all_to_all | solution.py:187
  191.4 0.8 copy-start.4
  213.4 7.5 %copy-start.1 = (bf16[320,1024]{1,0:T(8,128)(2,1)S(1)}, bf16[320,1024]{1,0:T(8,128)(2,1)}, u32[]{:S(2)}) copy-start(bf16[320,1024]{1,0:T(8,128)(2,1)} %reshape.331) | copy-start | bytes 1966084
  233.2 17.3 %all-to-all-start.3 = ((bf16[16,20,1024]{2,1,0:T(8,128)(2,1)}), bf16[16,20,1024]{2,1,0:T(8,128)(2,1)S(1)}, u32[]{:S(2)}, u32[]{:S(2)}) async-start(bf16[16,20,1024]{2,1,0:T(8,128)(2,1)} %reshape.332), calls=%async_computation.3 | async-start | bytes 1572864 | tf_op jit(solution)/shard_map/all_to_all | solution.py:227
Sparse Core Ops, SparseCore 0:
  9.2 85.7 all-gather.6
  96.7 43.3 all-gather.10
  142.0 47.2 all-gather.8

commit v8 on v6

--- a/solution.py
+++ b/solution.py
@@ -81,7 +81,7 @@
         jnp.zeros((q_rows, head_dim), jnp.float32),
         jnp.zeros((q_rows, 1), jnp.float32),
     )
-    best, weighted, factor_sum = lax.fori_loop(0, key_blocks, one_block, start, unroll=2)
+    best, weighted, factor_sum = lax.fori_loop(0, key_blocks, one_block, start, unroll=4)
     o_ref[...] = (weighted / factor_sum).astype(o_ref.dtype)
 
 

time: 261 us -> 260 us (level)
  Pallas kernels: 74.6 us -> 71 us
  waiting for transfers between devices: 72.2 us -> 75.1 us
    pallas_call x1, Pallas kernels: 74.6 us -> 71 us  [block_partials(): pl.pallas_call(attention_kernel, grid_spec=grid_spec, out_shape=jax.Shape...]
    all_to_all x1, waiting for transfers between devices: 11.4 us -> 14.2 us  [per_device(): lax.all_to_all(head_out.reshape(cut_count, q_rows, head_dim), 'cuts', spl...]
  transfers between devices with their start and end apart: 6 -> 6, of which waited for: 3 -> 3; matrix products, arithmetic and copies ran while one was open for 17% -> 17% of each run, Pallas kernels for 29% -> 27%
where the time goes in v8:
time: 260 us; the launch traced here: 259 us
  waiting for transfers between devices  75.1 us (29%)
  Pallas kernels  71 us (27%)
  matrix products  32.4 us (12%)
  local copies, waits for them, and re-layouts  22.6 us (9%)
  starting transfers between devices  20.3 us (8%)
  blocking collectives  20.1 us (8%)
  between operations  13.9 us (5%)
  other arithmetic  4.01 us (2%)
    pallas_call x1, Pallas kernels, block_partials(): pl.pallas_call(attention_kernel, grid_spec=grid_spec, out_shape=jax.Shape...  71 us
    all_to_all x1, waiting for transfers between devices, per_device(): lax.all_to_all(packed.reshape(packed.shape[0], head_count, head_dim), 'cu...  49.9 us
    all_to_all x1, blocking collectives, per_device(): lax.all_to_all(buffers, 'req', split_axis=0, concat_axis=0, tiled=True)  20.1 us
    all_to_all x1, waiting for transfers between devices, per_device(): lax.all_to_all(head_out.reshape(cut_count, q_rows, head_dim), 'cuts', spl...  14.2 us
    unnamed x25, local copies, waits for them, and re-layouts  11.4 us
    dot_general x1, matrix products, per_device(): lax.dot_general(act_rows, full_down, (((1,), (1,)), ((), ())), preferred_...  10.1 us
    all_to_all x1, waiting for transfers between devices, per_device(): lax.all_to_all(expert_out, 'req', split_axis=0, concat_axis=0, tiled=True)  8.96 us
    all_to_all x1, starting transfers between devices, per_device(): lax.all_to_all(packed.reshape(packed.shape[0], head_count, head_dim), 'cu...  8.61 us
  transfers between devices with their start and end apart: 6, of which 3 were waited for; matrix products, arithmetic and copies ran while one was open for 17% of the time, Pallas kernels for 27%

profile of v8, /device:TPU:8, one launch (start us, length us, event | category | flops | bytes accessed | tf_op | source)
XLA Modules:
  0.0 259.4 jit_solution(7570244708293208534)
XLA Ops:
  6.5 0.7 all-gather.7.cloned.1.call-update
  7.3 0.0 all-gather.11.cloned.1.call-start
  7.3 0.7 all-gather.11.cloned.1.call-update
  8.0 0.0 all-gather.9.cloned.1.call-start
  8.1 0.7 all-gather.9.cloned.1.call-update
  8.7 1.2 copy.80
  10.0 1.8 copy.81
  11.8 1.2 copy.82
  13.0 0.8 copy.83
  13.9 1.1 copy.84
  15.0 0.9 constant_dynamic-update-slice_fusion.4
  15.9 1.7 constant_dynamic-update-slice_fusion.3
  17.6 0.9 constant_dynamic-update-slice_fusion.2
  18.4 1.7 constant_dynamic-update-slice_fusion.1
  20.1 0.8 constant_dynamic-update-slice_fusion
  20.9 8.6 %all-to-all-start = ((bf16[896,16,64]{0,2,1:T(8,128)(2,1)}), bf16[896,16,64]{0,2,1:T(8,128)(2,1)}, u32[]{:S(2)}, u32[]{:S(2)}) async-start(bf16[896,16,64]{0,2,1:T(8,128)(2,1)} %constant_dynamic-update-slice_fusion), calls=%async_computation | async-start | bytes 3670016 | tf_op jit(solution)/shard_map/all_to_all | solution.py:182
  30.2 0.1 subtract_add_fusion.1
  30.3 0.9 convert_add_fusion
  31.2 3.3 %fusion = f32[1,8,16,512]{3,0,2,1:T(1,128)S(1)} fusion(s32[8,16,512]{2,1,0:T(8,128)S(1)} %convert_add_fusion, f32[16,32]{1,0:T(8,128)} %param.21, s32[]{:T(128)S(6)} %select_n.11), kind=kOutput, calls=%fused_computation.1 | convolution fusion | flops 27262976 | bytes 524804 | tf_op jit(solution)/shard_map/agmk,hk->agm/dot_general | solution.py:101
  34.5 0.7 copy.107
  35.2 0.1 subtract_add_fusion
  35.3 0.7 fusion.110.live_ref
  36.0 0.7 convert_add_fusion.1
  36.6 2.7 %fusion.1 = f32[1,8,16,384]{3,0,2,1:T(1,128)S(1)} fusion(s32[8,16,384]{2,1,0:T(8,128)S(1)} %convert_add_fusion.1, f32[16,32]{1,0:T(8,128)} %param.21, s32[]{:T(128)S(6)} %select_n.11), kind=kOutput, calls=%fused_computation.3 | convolution fusion | flops 20447232 | bytes 393732 | tf_op jit(solution)/shard_map/agmk,hk->agm/dot_general | solution.py:102
  39.3 0.8 bitcast_select_fusion.tn_ref
  40.1 49.9 %all-to-all-done = bf16[896,16,64]{0,2,1:T(8,128)(2,1)} async-done(((bf16[896,16,64]{0,2,1:T(8,128)(2,1)}), bf16[896,16,64]{0,2,1:T(8,128)(2,1)}, u32[]{:S(2)}, u32[]{:S(2)}) %all-to-all-start) | async-done | bytes 1835040 | tf_op jit(solution)/shard_map/all_to_all | solution.py:182
  90.0 4.6 %copy.85 = bf16[896,16,64]{2,0,1:T(8,128)(2,1)} copy(bf16[896,16,64]{0,2,1:T(8,128)(2,1)} %all-to-all-done) | data formatting | bytes 3670016 | tf_op jit(solution)/shard_map/all_to_all | solution.py:182
  94.6 71.0 %shard_map.145 = bf16[2048,64]{1,0:T(8,128)(2,1)} custom-call(s32[1]{0:T(128)} %copy.112.scalars, bf16[16,896,64]{2,1,0:T(8,128)(2,1)} %bitcast.79, bf16[16,896,64]{2,1,0:T(8,128)(2,1)} %bitcast.80, bf16[16,896,64]{2,1,0:T(8,128)(2,1)} %bitcast.81, f32[8,16,512]{2,1,0:T(8,128)} %bitcast.89, f32[8,16,384]{2,1,0:T(8,128)} %bitcast_select_fusion.tn_ref, ...), custom_call_target="tpu_custom_call" | custom-call | flops 3221225472 | bytes 9961472 | tf_op jit(solution)/shard_map/pallas_call | solution.py:137
  165.6 2.0 copy.86
  167.6 6.5 %all-to-all-start.1 = ((bf16[16,128,64]{1,2,0:T(8,128)(2,1)}), bf16[16,128,64]{1,2,0:T(8,128)(2,1)S(1)}, u32[]{:S(2)}, u32[]{:S(2)}) async-start(bf16[16,128,64]{1,2,0:T(8,128)(2,1)} %copy.86), calls=%async_computation.1 | async-start | bytes 524288 | tf_op jit(solution)/shard_map/all_to_all | solution.py:187
  174.1 0.1 copy.87
  174.2 0.3 convert_reduce_fusion
  174.4 0.1 fusion.108
  174.6 14.2 %all-to-all-done.1 = bf16[16,128,64]{1,2,0:T(8,128)(2,1)S(1)} async-done(((bf16[16,128,64]{1,2,0:T(8,128)(2,1)}), bf16[16,128,64]{1,2,0:T(8,128)(2,1)S(1)}, u32[]{:S(2)}, u32[]{:S(2)}) %all-to-all-start.1) | async-done | bytes 262176 | tf_op jit(solution)/shard_map/all_to_all | solution.py:187
  188.7 0.6 multiply_reduce_fusion
  189.3 0.3 fusion.112
  189.6 0.5 select_reduce_fusion
  190.1 0.8 fusion.28
  190.9 0.5 convolution_convert_fusion
  191.4 20.1 %all_to_all.30 = bf16[16,20,1024]{2,1,0:T(8,128)(2,1)S(1)} all-to-all(bf16[16,20,1024]{2,1,0:T(8,128)(2,1)S(1)} %convolution_convert_fusion), channel_id=1, replica_groups=mesh['req'=16,'cuts'=16] {'req'}, dimensions={0} | all-to-all | bytes 1310720 | tf_op jit(solution)/shard_map/all_to_all | solution.py:216
  211.5 1.0 reshape.331
  212.5 7.5 %fusion.21 = f32[320,2816]{1,0:T(8,128)} fusion(bf16[320,1024]{1,0:T(8,128)(2,1)} %reshape.331, bf16[1,1024,2816]{1,2,0:T(8,128)(2,1)} %all-gather.7.cloned.1.call-done), kind=kOutput, calls=%fused_computation.20 | convolution fusion | flops 1852702720 | bytes 10027008 | tf_op jit(solution)/shard_map/dot_general | solution.py:221
  220.0 10.1 %fusion.25 = bf16[320,1024]{1,0:T(8,128)(2,1)} fusion(bf16[1,1024,2816]{1,2,0:T(8,128)(2,1)} %all-gather.11.cloned.1.call-done, f32[320,2816]{1,0:T(8,128)} %fusion.21, bf16[320,1024]{1,0:T(8,128)(2,1)S(1)} %copy-done.1, bf16[1,1024,2816]{1,2,0:T(8,128)(2,1)} %all-gather.9.cloned.1.call-done), kind=kOutput, calls=%fused_computation.24 | convolution fusion | flops 3693117440 | bytes 16449536 | tf_op jit(solution)/shard_map/dot_general | solution.py:224
  230.1 2.1 reshape.332
  232.2 5.1 %all-to-all-start.3 = ((bf16[16,20,1024]{2,1,0:T(8,128)(2,1)}), bf16[16,20,1024]{2,1,0:T(8,128)(2,1)S(1)}, u32[]{:S(2)}, u32[]{:S(2)}) async-start(bf16[16,20,1024]{2,1,0:T(8,128)(2,1)} %reshape.332), calls=%async_computation.3 | async-start | bytes 1572864 | tf_op jit(solution)/shard_map/all_to_all | solution.py:227
  237.4 3.3 %convolution_bitcast_fusion = f32[16,20,128]{1,0,2:T(8,128)} fusion(f32[128,2]{1,0:T(8,128)S(1)} %add_divide_fusion, f32[128,2]{1,0:T(8,128)} %copy-done.4, s32[128,2]{1,0:T(8,128)S(1)} %copy.87), kind=kOutput, calls=%fused_computation.23 | convolution fusion | flops 997376 | bytes 166912 | tf_op jit(solution)/shard_map/tke,tkc,tk->ect/dot_general | solution.py:228
  240.7 9.0 %all-to-all-done.3 = bf16[16,20,1024]{2,1,0:T(8,128)(2,1)S(1)} async-done(((bf16[16,20,1024]{2,1,0:T(8,128)(2,1)}), bf16[16,20,1024]{2,1,0:T(8,128)(2,1)S(1)}, u32[]{:S(2)}, u32[]{:S(2)}) %all-to-all-start.3) | async-done | bytes 655392 | tf_op jit(solution)/shard_map/all_to_all | solution.py:227
  249.6 3.2 %fusion.31 = bf16[1,128,1024]{2,1,0:T(8,128)(2,1)} fusion(f32[128,1024]{1,0:T(8,128)S(1)} %get-tuple-element.8, bf16[16,20,1024]{2,1,0:T(8,128)(2,1)S(1)} %all-to-all-done.3, f32[16,20,128]{1,0,2:T(8,128)} %convolution_bitcast_fusion), kind=kOutput, calls=%fused_computation.31 | convolution fusion | flops 503578624 | bytes 1605632 | tf_op jit(solution)/shard_map/ect,ecd->td/dot_general | solution.py:231
  (28 shorter events, 0.1 us)
Async XLA Ops:
  6.5 182.2 %copy-start = (bf16[1024,1024]{1,0:T(8,128)(2,1)S(1)}, bf16[1024,1024]{1,0:T(8,128)(2,1)}, u32[]{:S(2)}) copy-start(bf16[1024,1024]{1,0:T(8,128)(2,1)} %param.23) | copy-start | bytes 6291460
  6.5 6.5 %copy-start.2 = (bf16[1,128,1024]{2,1,0:T(8,128)(2,1)S(1)}, bf16[1,128,1024]{2,1,0:T(8,128)(2,1)}, u32[]{:S(2)}) copy-start(bf16[1,128,1024]{2,1,0:T(8,128)(2,1)} %param.17) | copy-start | bytes 786436
  6.5 205.9 %all-gather.7.cloned.1.call-start = ((), (), s32[]{:S(2)}) async-start(), calls=%async_computation.4 | async-start | bytes 6127616 | tf_op jit(solution)/shard_map/all_gather | solution.py:217
  7.3 212.7 %all-gather.11.cloned.1.call-start = ((), (), s32[]{:S(2)}) async-start(), calls=%async_computation.6 | async-start | bytes 6127616 | tf_op jit(solution)/shard_map/all_gather | solution.py:219
  8.0 212.0 %all-gather.9.cloned.1.call-start = ((), (), s32[]{:S(2)}) async-start(), calls=%async_computation.5 | async-start | bytes 6127616 | tf_op jit(solution)/shard_map/all_gather | solution.py:218
  20.9 69.1 %all-to-all-start = ((bf16[896,16,64]{0,2,1:T(8,128)(2,1)}), bf16[896,16,64]{0,2,1:T(8,128)(2,1)}, u32[]{:S(2)}, u32[]{:S(2)}) async-start(bf16[896,16,64]{0,2,1:T(8,128)(2,1)} %constant_dynamic-update-slice_fusion), calls=%async_computation | async-start | bytes 3670016 | tf_op jit(solution)/shard_map/all_to_all | solution.py:182
  94.6 79.4 %copy-start.6 = (bf16[1024]{0:T(1024)(128)(2,1)S(1)}, bf16[1024]{0:T(1024)(128)(2,1)}, u32[]{:S(2)}) copy-start(bf16[1024]{0:T(1024)(128)(2,1)} %param.24) | copy-start | bytes 6148
  94.6 79.4 %copy-start.7 = (s32[1,128,2]{1,2,0:T(2,128)S(1)}, s32[1,128,2]{1,2,0:T(2,128)}, u32[]{:S(2)}) copy-start(s32[1,128,2]{1,2,0:T(2,128)} %param.26) | copy-start | bytes 3076
  94.6 94.1 %copy-start.3 = (bf16[1,128,1024]{2,1,0:T(8,128)(2,1)S(1)}, bf16[1,128,1024]{2,1,0:T(8,128)(2,1)}, u32[]{:S(2)}) copy-start(bf16[1,128,1024]{2,1,0:T(8,128)(2,1)} %param.22) | copy-start | bytes 786436
  165.6 23.7 %copy-start.5 = (bf16[1024,16]{0,1:T(8,128)(2,1)S(1)}, bf16[1024,16]{0,1:T(8,128)(2,1)}, u32[]{:S(2)}) copy-start(bf16[1024,16]{0,1:T(8,128)(2,1)} %param.25) | copy-start | bytes 98308
  167.6 21.2 %all-to-all-start.1 = ((bf16[16,128,64]{1,2,0:T(8,128)(2,1)}), bf16[16,128,64]{1,2,0:T(8,128)(2,1)S(1)}, u32[]{:S(2)}, u32[]{:S(2)}) async-start(bf16[16,128,64]{1,2,0:T(8,128)(2,1)} %copy.86), calls=%async_computation.1 | async-start | bytes 524288 | tf_op jit(solution)/shard_map/all_to_all | solution.py:187
  190.1 0.8 copy-start.4
  212.5 7.5 %copy-start.1 = (bf16[320,1024]{1,0:T(8,128)(2,1)S(1)}, bf16[320,1024]{1,0:T(8,128)(2,1)}, u32[]{:S(2)}) copy-start(bf16[320,1024]{1,0:T(8,128)(2,1)} %reshape.331) | copy-start | bytes 1966084
  232.2 17.4 %all-to-all-start.3 = ((bf16[16,20,1024]{2,1,0:T(8,128)(2,1)}), bf16[16,20,1024]{2,1,0:T(8,128)(2,1)S(1)}, u32[]{:S(2)}, u32[]{:S(2)}) async-start(bf16[16,20,1024]{2,1,0:T(8,128)(2,1)} %reshape.332), calls=%async_computation.3 | async-start | bytes 1572864 | tf_op jit(solution)/shard_map/all_to_all | solution.py:227
Sparse Core Ops, SparseCore 0:
  9.2 85.7 all-gather.6
  96.7 43.6 all-gather.10
  142.3 48.4 all-gather.8
